TPU v7x, 32 devices: a whole 2x2x4 slice. The times are simulated.
32 devices in a mesh: tile: 8 (over y, x, core), slab: 4 (over z).
Axes of the slice: x: 2, y: 2, z: 4, core: 2. Of those that a mesh axis runs over, the one named last changes fastest.
Arguments:
- estimate: float32 [64, 128, 512], P('slab', 'tile'), may hold values from 0.5 to 2
- observed: float32 [64, 128, 512], P('slab', 'tile'), may hold values from 0.25 to 4
- kernel_rows: float32 [31], replicated, may hold values from 0.001 to 1
- kernel_columns: float32 [31], replicated, may hold values from 0.001 to 1
- kernel_planes: float32 [31], replicated, may hold values from 0.001 to 1
Outputs:
- new_estimate: float32 [64, 128, 512], P('slab', 'tile')
- pyramid_level: float32 [64, 64, 256], P('slab', 'tile')
All inputs are finite; a program needn't handle non-finite values.
Results may differ from a plain program's by a relative error of at most 0.00005.
Values sent between devices are 32-bit elements; how exact they have to be, the bound alone decides.
No kernel may reach another device: no remote copies, remote signals or barrier semaphores. Data moves between devices by JAX's collectives and lax.ppermute only.
A program may use at most 64 MiB of HBM per device.

v0:
```python
import jax
import jax.numpy as jnp
from jax import lax
from jax.sharding import PartitionSpec as P

PRECISE = lax.Precision.HIGHEST


def extended(shard, sides, width):
    for axis, dim in sides:
        devices, length = (lax.axis_size(axis), shard.shape[dim])
        up = [(i, (i + 1) % devices) for i in range(devices - 1)]
        down = [(j, i) for i, j in up]
        last = lax.slice_in_dim(shard, length - width, length, axis=dim)
        initial = lax.slice_in_dim(shard, 0, width, axis=dim)
        before = lax.ppermute(last, axis, up)
        after = lax.ppermute(initial, axis, down)
        shard = jnp.concatenate([before, shard, after], axis=dim)
    return shard


def banded(kernel, row_count, col_count, orient, anchor):
    tap_count = kernel.shape[0]
    offset_index = (
        orient
        * (
            lax.broadcasted_iota(jnp.int32, (row_count, col_count), 0)
            - lax.broadcasted_iota(jnp.int32, (row_count, col_count), 1)
        )
        + anchor
    )
    inside = (offset_index >= 0) & (offset_index < tap_count)
    values = jnp.take(kernel, jnp.clip(offset_index, 0, tap_count - 1))
    return jnp.where(inside, values, jnp.zeros_like(values))


def pyramid_matrix(row_count, col_count, anchor):
    offset_index = (
        lax.broadcasted_iota(jnp.int32, (row_count, col_count), 0)
        - 2 * lax.broadcasted_iota(jnp.int32, (row_count, col_count), 1)
        + anchor
    )
    outer = (offset_index == 0) | (offset_index == 3)
    middle = (offset_index == 1) | (offset_index == 2)
    return jnp.where(
        outer, jnp.float32(0.125), jnp.where(middle, jnp.float32(0.375), jnp.float32(0.0))
    )


def across_depth(volume, matrix):
    return jnp.einsum("pxy,pq->qxy", volume, matrix, precision=PRECISE)


def across_rows(volume, matrix):
    return jnp.einsum("zpy,pq->zqy", volume, matrix, precision=PRECISE)


def across_columns(volume, matrix):
    return jnp.dot(volume, matrix, precision=PRECISE)


def shards(estimate, observed, kernel_rows, kernel_columns, kernel_planes):
    plane_count, row_count, col_count = estimate.shape
    reach_cells = (kernel_rows.shape[0] - 1) // 2
    groups = lax.axis_size("slab")
    planes_all = plane_count * groups
    padded = extended(estimate, (("tile", 1),), reach_cells)
    partial_value = across_rows(
        padded, banded(kernel_rows, row_count + 2 * reach_cells, row_count, 1, 0)
    )
    partial_value = across_columns(
        partial_value, banded(kernel_columns, col_count, col_count, 1, reach_cells)
    )
    forward_depth = banded(kernel_planes, planes_all, planes_all, 1, reach_cells)
    backward_depth = banded(kernel_planes, planes_all, planes_all, -1, reach_cells)
    turned = across_depth(
        lax.all_to_all(partial_value, "slab", split_axis=2, concat_axis=0, tiled=True),
        forward_depth,
    )
    blurred = lax.all_to_all(turned, "slab", split_axis=0, concat_axis=2, tiled=True)
    quotient = observed / blurred
    turned_back = across_depth(
        lax.all_to_all(quotient, "slab", split_axis=2, concat_axis=0, tiled=True), backward_depth
    )
    back_field = lax.all_to_all(turned_back, "slab", split_axis=0, concat_axis=2, tiled=True)
    spread = across_columns(
        back_field, banded(kernel_columns, col_count, col_count, -1, reach_cells)
    )
    padded_spread = extended(spread, (("tile", 1),), reach_cells)
    correction = across_rows(
        padded_spread,
        banded(kernel_rows, row_count + 2 * reach_cells, row_count, -1, 2 * reach_cells),
    )
    new_estimate = estimate * correction
    halved = across_columns(new_estimate, pyramid_matrix(col_count, col_count // 2, 1))
    padded_halved = extended(halved, (("tile", 1),), 1)
    pyramid_level = across_rows(padded_halved, pyramid_matrix(row_count + 2, row_count // 2, 0))
    return (new_estimate, pyramid_level)


def solution(mesh):
    in_specs = (P("slab", "tile", None), P("slab", "tile", None), P(), P(), P())
    out_specs = (P("slab", "tile", None), P("slab", "tile", None))
    return jax.shard_map(shards, mesh=mesh, in_specs=in_specs, out_specs=out_specs, check_vma=False)
```

profile of v0, /device:TPU:11, one launch (start us, length us, event | category | flops | bytes accessed | tf_op | source)
XLA Modules:
  0.0 227.2 jit_solution(3255726964246776414)
XLA Ops:
  0.6 0.0 copy-start
  0.7 1.3 fusion.571
  2.0 3.7 %collective-permute-start = (f32[16,15,512]{2,1,0:T(8,128)S(1)}, f32[16,15,512]{2,1,0:T(8,128)S(1)}, u32[]{:S(2)}, u32[]{:S(2)}) collective-permute-start(f32[16,15,512]{2,1,0:T(8,128)S(1)} %get-tuple-element.7), channel_id=1, source_target_pairs={{0,4},{4,8},{8,12},{12,16},{16,20},{20,24},{24,28},{1,5},{5,9},{9,... | collective-permute-start | bytes 1474568 | tf_op jit(solution)/shard_map/ppermute | solution.py:16
  5.7 1.9 collective-permute-start.1
  7.6 0.1 reshape.155
  7.7 0.0 copy-start.5
  7.7 0.0 copy-start.2
  7.8 4.8 %gather_fusion.3 = f32[736]{0:T(1024)S(1)} fusion(f32[31]{0:T(128)S(1)} %copy-done.1, s32[1024]{0:T(1024)S(1)} %pad_clamp_fusion), kind=kCustom, calls=%fused_computation.2.clone | custom fusion | bytes 8832 | tf_op jit(solution)/shard_map/jit(_take)/gather | solution.py:33
  12.6 0.1 reshape.158
  12.6 0.7 fusion.574
  13.3 0.7 fusion.573
  14.1 0.5 collective-permute-done
  14.6 4.5 %collective-permute-done.1 = f32[16,15,512]{2,1,0:T(8,128)S(1)} collective-permute-done((f32[16,15,512]{2,1,0:T(8,128)S(1)}, f32[16,15,512]{2,1,0:T(8,128)S(1)}, u32[]{:S(2)}, u32[]{:S(2)}) %collective-permute-start.1) | collective-permute-done | bytes 491552 | tf_op jit(solution)/shard_map/ppermute | solution.py:17
  19.1 1.0 fusion.15
  20.1 23.0 %fusion.23 = f32[16,16,512]{2,1,0:T(8,128)S(1)} fusion(f32[16,16,512]{2,1,0:T(8,128)S(1)} %fusion.15, f32[]{:T(128)} %bitcast.35, f32[]{:T(128)} %bitcast.34, f32[]{:T(128)} %bitcast.33, f32[]{:T(128)} %bitcast.32, f32[]{:T(128)} %bitcast.31, f32[]{:T(128)} %bitcast.30, f32[]{:T(128)} %bitcast.29, f32[]{:T(128)} %bitcast.28, f32[]{:T(128)} %bitcast.27, ...), kind=kOutput, calls=%fused_computation.25 | convolution fusion | flops 824705024 | bytes 1048700 | tf_op jit(solution)/shard_map/dot_general | solution.py:59
  43.0 3.6 %copy.19 = f32[16,16,512]{1,0,2:T(8,128)} copy(f32[16,16,512]{2,1,0:T(8,128)S(1)} %fusion.23) | data formatting | bytes 1048576 | tf_op jit(solution)/shard_map/dot_general | solution.py:59
  46.7 4.6 %reshape.229 = f32[4,1,32768]{2,1,0:T(1,128)} reshape(f32[512,16,16]{2,1,0:T(8,128)} %bitcast.121) | data formatting | bytes 1048576
  51.3 4.8 %all-to-all-start = ((f32[4,1,32768]{2,1,0:T(1,128)}), f32[4,1,32768]{2,1,0:T(1,128)S(1)}, u32[]{:S(2)}, u32[]{:S(2)}) async-start(f32[4,1,32768]{2,1,0:T(1,128)} %reshape.229), calls=%async_computation | async-start | bytes 1048576 | tf_op jit(solution)/shard_map/all_to_all | solution.py:77
  56.1 0.1 reshape.151
  56.2 24.7 %gather_fusion.2 = f32[4096]{0:T(1024)S(1)} fusion(f32[31]{0:T(128)S(1)} %copy-done, s32[4096]{0:T(1024)S(1)} %broadcast_clamp_fusion), kind=kCustom, calls=%fused_computation.3.clone | custom fusion | bytes 49152 | tf_op jit(solution)/shard_map/jit(_take)/gather | solution.py:33
  80.9 0.1 reshape.154
  80.9 0.0 all-to-all-done
  80.9 0.5 broadcast.948
  81.5 2.1 reduce
  83.6 3.4 %reshape.230 = f32[512,16,16]{2,1,0:T(8,128)} reshape(f32[4,32768]{1,0:T(4,128)S(1)} %reduce) | data formatting | bytes 1048576
  87.0 3.3 %copy.20 = f32[16,16,4,128]{3,0,2,1:T(8,128)S(1)} copy(f32[16,16,4,128]{1,0,3,2:T(8,128)} %bitcast.122) | data formatting | bytes 1048576 | tf_op jit(solution)/shard_map/all_to_all | solution.py:77
  90.3 0.0 copy-start.3
  90.3 0.6 fusion.379
  91.0 1.1 copy.22
  92.1 4.5 %all-to-all-start.1 = ((f32[64,16,128]{2,1,0:T(8,128)}), f32[64,16,128]{2,1,0:T(8,128)S(1)}, u32[]{:S(2)}, u32[]{:S(2)}) async-start(f32[64,16,128]{2,1,0:T(8,128)} %copy.22), calls=%async_computation.1 | async-start | bytes 1048576 | tf_op jit(solution)/shard_map/all_to_all | solution.py:80
  96.6 3.7 %copy.24 = f32[16,16,512]{1,0,2:T(8,128)} copy(f32[16,16,512]{2,1,0:T(8,128)S(1)} %copy-done.3) | data formatting | bytes 1048576 | tf_op args[1]
  100.3 8.4 %all-to-all-done.1 = f32[64,16,128]{2,1,0:T(8,128)S(1)} async-done(((f32[64,16,128]{2,1,0:T(8,128)}), f32[64,16,128]{2,1,0:T(8,128)S(1)}, u32[]{:S(2)}, u32[]{:S(2)}) %all-to-all-start.1) | async-done | bytes 524320 | tf_op jit(solution)/shard_map/all_to_all | solution.py:80
  108.6 2.8 %copy.23 = f32[16,16,4,128]{1,0,3,2:T(8,128)} copy(f32[16,16,4,128]{3,1,0,2:T(8,128)S(1)} %bitcast.124) | data formatting | bytes 1048576 | tf_op jit(solution)/shard_map/all_to_all | solution.py:80
  111.5 6.0 %bitcast_divide_fusion = f32[16,16,512]{1,0,2:T(8,128)} fusion(f32[16,16,512]{1,0,2:T(8,128)} %copy.24, f32[16,16,4,128]{1,0,3,2:T(8,128)} %copy.23), kind=kLoop, calls=%fused_computation.4 | loop fusion | flops 131072 | bytes 1572864 | tf_op jit(solution)/shard_map/div | solution.py:81
  117.5 4.6 %reshape.231 = f32[4,1,32768]{2,1,0:T(1,128)} reshape(f32[512,16,16]{2,1,0:T(8,128)} %bitcast.120) | data formatting | bytes 1048576
  122.1 6.4 %all-to-all-start.2 = ((f32[4,1,32768]{2,1,0:T(1,128)}), f32[4,1,32768]{2,1,0:T(1,128)S(1)}, u32[]{:S(2)}, u32[]{:S(2)}) async-start(f32[4,1,32768]{2,1,0:T(1,128)} %reshape.231), calls=%async_computation.2 | async-start | bytes 1048576 | tf_op jit(solution)/shard_map/all_to_all | solution.py:83
  128.5 0.1 reshape.147
  128.6 24.7 %gather_fusion.1 = f32[4096]{0:T(1024)S(1)} fusion(f32[31]{0:T(128)S(1)} %copy-done, s32[4096]{0:T(1024)S(1)} %broadcast_clamp_fusion.1), kind=kCustom, calls=%fused_computation.1.clone | custom fusion | bytes 49152 | tf_op jit(solution)/shard_map/jit(_take)/gather | solution.py:33
  153.3 0.1 reshape.150
  153.4 0.0 all-to-all-done.2
  153.4 2.1 reduce.1
  155.5 3.4 %reshape.232 = f32[512,16,16]{2,1,0:T(8,128)} reshape(f32[4,32768]{1,0:T(4,128)S(1)} %reduce.1) | data formatting | bytes 1048576
  158.9 3.3 %copy.25 = f32[16,16,4,128]{3,0,2,1:T(8,128)S(1)} copy(f32[16,16,4,128]{1,0,3,2:T(8,128)} %bitcast.123) | data formatting | bytes 1048576 | tf_op jit(solution)/shard_map/all_to_all | solution.py:83
  162.3 0.6 fusion.381
  162.9 0.3 copy.27
  163.2 16.3 %all_to_all.72 = f32[64,16,128]{2,1,0:T(8,128)S(1)} all-to-all(f32[64,16,128]{2,1,0:T(8,128)S(1)} %copy.27), channel_id=1, replica_groups=mesh['tile'=8,'slab'=4] {'slab'}, dimensions={0} | all-to-all | bytes 1048576 | tf_op jit(solution)/shard_map/all_to_all | solution.py:85
  179.5 0.3 copy.39
  179.9 0.2 all_to_all.67
  180.1 22.9 %fusion.21 = f32[16,16,512]{2,1,0:T(8,128)S(1)} fusion(f32[16,16,512]{2,1,0:T(8,128)S(1)} %all_to_all.67, f32[]{:T(128)} %bitcast.35, f32[]{:T(128)} %bitcast.34, f32[]{:T(128)} %bitcast.33, f32[]{:T(128)} %bitcast.32, f32[]{:T(128)} %bitcast.31, f32[]{:T(128)} %bitcast.30, f32[]{:T(128)} %bitcast.29, f32[]{:T(128)} %bitcast.28, f32[]{:T(128)} %bitcast.27, ...), kind=kOutput, calls=%fused_computation.23 | convolution fusion | flops 824967168 | bytes 1048700 | tf_op jit(solution)/shard_map/dot_general | solution.py:59
  203.0 0.1 fusion.570
  203.1 1.9 collective-permute-start.2
  205.1 4.1 %collective-permute-start.3 = (f32[16,15,512]{2,1,0:T(8,128)S(1)}, f32[16,15,512]{2,1,0:T(8,128)S(1)}, u32[]{:S(2)}, u32[]{:S(2)}) collective-permute-start(f32[16,15,512]{2,1,0:T(8,128)S(1)} %get-tuple-element.6), channel_id=1, source_target_pairs={{4,0},{8,4},{12,8},{16,12},{20,16},{24,20},{28,24},{5,1},{9,5},{13... | collective-permute-start | bytes 1474568 | tf_op jit(solution)/shard_map/ppermute | solution.py:17
  209.2 0.1 reshape.143
  209.3 4.8 %gather_fusion = f32[736]{0:T(1024)S(1)} fusion(f32[31]{0:T(128)S(1)} %copy-done.1, s32[1024]{0:T(1024)S(1)} %pad_clamp_fusion.1), kind=kCustom, calls=%fused_computation.clone | custom fusion | bytes 8832 | tf_op jit(solution)/shard_map/jit(_take)/gather | solution.py:33
  214.1 0.1 reshape.146
  214.1 2.3 %collective-permute-done.3 = f32[16,15,512]{2,1,0:T(8,128)S(1)} collective-permute-done((f32[16,15,512]{2,1,0:T(8,128)S(1)}, f32[16,15,512]{2,1,0:T(8,128)S(1)}, u32[]{:S(2)}, u32[]{:S(2)}) %collective-permute-start.3) | collective-permute-done | bytes 491552 | tf_op jit(solution)/shard_map/ppermute | solution.py:17
  216.5 1.0 fusion.18
  217.5 0.0 copy-start.4
  217.5 0.7 fusion.223
  218.2 1.9 collective-permute-start.4
  220.2 2.8 %collective-permute-start.5 = (f32[16,1,256]{2,1,0:T(1,128)S(1)}, f32[16,1,256]{2,1,0:T(1,128)S(1)}, u32[]{:S(2)}, u32[]{:S(2)}) collective-permute-start(f32[16,1,256]{2,1,0:T(1,128)S(1)} %get-tuple-element.10), channel_id=1, source_target_pairs={{4,0},{8,4},{12,8},{16,12},{20,16},{24,20},{28,24},{5,1},{9,5},{13... | collective-permute-start | bytes 49160 | tf_op jit(solution)/shard_map/ppermute | solution.py:17
  223.0 0.0 collective-permute-done.4
  223.0 3.1 %collective-permute-done.5 = f32[16,1,256]{2,1,0:T(1,128)S(1)} collective-permute-done((f32[16,1,256]{2,1,0:T(1,128)S(1)}, f32[16,1,256]{2,1,0:T(1,128)S(1)}, u32[]{:S(2)}, u32[]{:S(2)}) %collective-permute-start.5) | collective-permute-done | bytes 16416 | tf_op jit(solution)/shard_map/ppermute | solution.py:17
  226.1 1.0 convolution_bitcast_fusion
  (19 shorter events, 0.1 us)
Async XLA Ops:
  0.6 55.5 %copy-start = (f32[31]{0:T(128)S(1)}, f32[31]{0:T(128)}, u32[]{:S(2)}) copy-start(f32[31]{0:T(128)} %param.15) | copy-start | bytes 376
  0.6 7.1 %copy-start.1 = (f32[31]{0:T(128)S(1)}, f32[31]{0:T(128)}, u32[]{:S(2)}) copy-start(f32[31]{0:T(128)} %param.13) | copy-start | bytes 376
  2.0 12.6 %collective-permute-start = (f32[16,15,512]{2,1,0:T(8,128)S(1)}, f32[16,15,512]{2,1,0:T(8,128)S(1)}, u32[]{:S(2)}, u32[]{:S(2)}) collective-permute-start(f32[16,15,512]{2,1,0:T(8,128)S(1)} %get-tuple-element.7), channel_id=1, source_target_pairs={{0,4},{4,8},{8,12},{12,16},{16,20},{20,24},{24,28},{1,5},{5,9},{9,... | collective-permute-start | bytes 1474568 | tf_op jit(solution)/shard_map/ppermute | solution.py:16
  5.7 13.4 %collective-permute-start.1 = (f32[16,15,512]{2,1,0:T(8,128)S(1)}, f32[16,15,512]{2,1,0:T(8,128)S(1)}, u32[]{:S(2)}, u32[]{:S(2)}) collective-permute-start(f32[16,15,512]{2,1,0:T(8,128)S(1)} %get-tuple-element.8), channel_id=1, source_target_pairs={{4,0},{8,4},{12,8},{16,12},{20,16},{24,20},{28,24},{5,1},{9,5},{13... | collective-permute-start | bytes 1474568 | tf_op jit(solution)/shard_map/ppermute | solution.py:17
  7.7 4.9 %copy-start.5 = (f32[31]{0:T(128)S(1)}, f32[31]{0:T(128)}, u32[]{:S(2)}) copy-start(f32[31]{0:T(128)} %param.14) | copy-start | bytes 376
  7.7 11.3 %copy-start.2 = (f32[16,16,512]{2,1,0:T(8,128)S(1)}, f32[16,16,512]{2,1,0:T(8,128)}, u32[]{:S(2)}) copy-start(f32[16,16,512]{2,1,0:T(8,128)} %param.11) | copy-start | bytes 1572868
  51.3 29.6 %all-to-all-start = ((f32[4,1,32768]{2,1,0:T(1,128)}), f32[4,1,32768]{2,1,0:T(1,128)S(1)}, u32[]{:S(2)}, u32[]{:S(2)}) async-start(f32[4,1,32768]{2,1,0:T(1,128)} %reshape.229), calls=%async_computation | async-start | bytes 1048576 | tf_op jit(solution)/shard_map/all_to_all | solution.py:77
  90.3 6.3 %copy-start.3 = (f32[16,16,512]{2,1,0:T(8,128)S(1)}, f32[16,16,512]{2,1,0:T(8,128)}, u32[]{:S(2)}) copy-start(f32[16,16,512]{2,1,0:T(8,128)} %param.12) | copy-start | bytes 1572868
  92.1 16.5 %all-to-all-start.1 = ((f32[64,16,128]{2,1,0:T(8,128)}), f32[64,16,128]{2,1,0:T(8,128)S(1)}, u32[]{:S(2)}, u32[]{:S(2)}) async-start(f32[64,16,128]{2,1,0:T(8,128)} %copy.22), calls=%async_computation.1 | async-start | bytes 1048576 | tf_op jit(solution)/shard_map/all_to_all | solution.py:80
  122.1 31.3 %all-to-all-start.2 = ((f32[4,1,32768]{2,1,0:T(1,128)}), f32[4,1,32768]{2,1,0:T(1,128)S(1)}, u32[]{:S(2)}, u32[]{:S(2)}) async-start(f32[4,1,32768]{2,1,0:T(1,128)} %reshape.231), calls=%async_computation.2 | async-start | bytes 1048576 | tf_op jit(solution)/shard_map/all_to_all | solution.py:83
  203.1 11.0 %collective-permute-start.2 = (f32[16,15,512]{2,1,0:T(8,128)S(1)}, f32[16,15,512]{2,1,0:T(8,128)S(1)}, u32[]{:S(2)}, u32[]{:S(2)}) collective-permute-start(f32[16,15,512]{2,1,0:T(8,128)S(1)} %get-tuple-element.4), channel_id=1, source_target_pairs={{0,4},{4,8},{8,12},{12,16},{16,20},{20,24},{24,28},{1,5},{5,9},{9,... | collective-permute-start | bytes 1474568 | tf_op jit(solution)/shard_map/ppermute | solution.py:16
  205.1 11.4 %collective-permute-start.3 = (f32[16,15,512]{2,1,0:T(8,128)S(1)}, f32[16,15,512]{2,1,0:T(8,128)S(1)}, u32[]{:S(2)}, u32[]{:S(2)}) collective-permute-start(f32[16,15,512]{2,1,0:T(8,128)S(1)} %get-tuple-element.6), channel_id=1, source_target_pairs={{4,0},{8,4},{12,8},{16,12},{20,16},{24,20},{28,24},{5,1},{9,5},{13... | collective-permute-start | bytes 1474568 | tf_op jit(solution)/shard_map/ppermute | solution.py:17
  217.5 9.7 %copy-start.4 = (f32[16,16,512]{2,1,0:T(8,128)}, f32[16,16,512]{2,1,0:T(8,128)S(1)}, u32[]{:S(2)}) copy-start(f32[16,16,512]{2,1,0:T(8,128)S(1)} %fusion.18) | copy-start | bytes 1572868
  218.2 4.7 %collective-permute-start.4 = (f32[16,1,256]{2,1,0:T(1,128)S(1)}, f32[16,1,256]{2,1,0:T(1,128)S(1)}, u32[]{:S(2)}, u32[]{:S(2)}) collective-permute-start(f32[16,1,256]{2,1,0:T(1,128)S(1)} %get-tuple-element.9), channel_id=1, source_target_pairs={{0,4},{4,8},{8,12},{12,16},{16,20},{20,24},{24,28},{1,5},{5,9},{9,... | collective-permute-start | bytes 49160 | tf_op jit(solution)/shard_map/ppermute | solution.py:16
  220.2 6.0 %collective-permute-start.5 = (f32[16,1,256]{2,1,0:T(1,128)S(1)}, f32[16,1,256]{2,1,0:T(1,128)S(1)}, u32[]{:S(2)}, u32[]{:S(2)}) collective-permute-start(f32[16,1,256]{2,1,0:T(1,128)S(1)} %get-tuple-element.10), channel_id=1, source_target_pairs={{4,0},{8,4},{12,8},{16,12},{20,16},{24,20},{28,24},{5,1},{9,5},{13... | collective-permute-start | bytes 49160 | tf_op jit(solution)/shard_map/ppermute | solution.py:17
where the time goes:
time: 232 us; the launch traced here: 227 us
  local copies, waits for them, and re-layouts  97.8 us (42%)
  matrix products  50.9 us (22%)
  starting transfers between devices  32 us (14%)
  waiting for transfers between devices  18.8 us (8%)
  blocking collectives  16.3 us (7%)
  other arithmetic  10.3 us (4%)
    gather x10, local copies, waits for them, and re-layouts, banded(): values = jnp.take(kernel, jnp.clip(offset_index, 0, tap_count - 1))  60.7 us
    dot_general x3, matrix products, across_columns(): return jnp.dot(volume, matrix, precision=PRECISE)  46.6 us
    unnamed x17, local copies, waits for them, and re-layouts  19.8 us
    all_to_all x1, blocking collectives, shards(): lax.all_to_all(turned_back, 'slab', split_axis=0, concat_axis=2, tiled=True)  16.3 us
    ppermute x3, waiting for transfers between devices, extended(): after = lax.ppermute(initial, axis, down)  9.92 us
    ppermute x3, starting transfers between devices, extended(): after = lax.ppermute(initial, axis, down)  8.79 us
    all_to_all x1, waiting for transfers between devices, shards(): lax.all_to_all(turned, 'slab', split_axis=0, concat_axis=2, tiled=True)  8.35 us
    ppermute x3, starting transfers between devices, extended(): before = lax.ppermute(last, axis, up)  7.52 us
  transfers between devices with their start and end apart: 9, of which 5 were waited for; matrix products, arithmetic and copies ran while one was open for 28% of the time, Pallas kernels for 0%

commit v1 on v0

v1 whole, which is shorter than its diff:
```python
import jax
import jax.numpy as jnp
from jax import lax
from jax.sharding import PartitionSpec as P

PRECISE = lax.Precision.HIGHEST


def halo(shard, axis, dim, before_width, after_width):
    devices, length = lax.axis_size(axis), shard.shape[dim]
    pieces_before, pieces_after = [], []
    hop = 1
    while (hop - 1) * length < max(before_width, after_width):
        up = [(i, i + hop) for i in range(devices - hop)]
        down = [(i + hop, i) for i in range(devices - hop)]
        if (hop - 1) * length < before_width:
            start = max(0, hop * length - before_width)
            piece = lax.slice_in_dim(shard, start, length, axis=dim)
            pieces_before.insert(0, lax.ppermute(piece, axis, up))
        if (hop - 1) * length < after_width:
            stop = min(length, after_width - (hop - 1) * length)
            piece = lax.slice_in_dim(shard, 0, stop, axis=dim)
            pieces_after.append(lax.ppermute(piece, axis, down))
        hop += 1
    return jnp.concatenate(pieces_before + [shard] + pieces_after, axis=dim)


def band(kernel, n_in, n_out, sign, shift):
    offset = sign * (
        lax.broadcasted_iota(jnp.int32, (n_in, n_out), 0)
        - lax.broadcasted_iota(jnp.int32, (n_in, n_out), 1)
    ) + shift
    matrix = jnp.zeros((n_in, n_out), jnp.float32)
    for tap in range(kernel.shape[0]):
        matrix = jnp.where(offset == tap, kernel[tap], matrix)
    return matrix


def band_square(kernel, n, shift):
    block = 128
    taps = kernel.shape[0]
    if n % block or n == block or max(shift, taps - 1 - shift) >= block:
        return band(kernel, n, n, 1, shift)
    count = n // block
    parts = {
        d: band(kernel, block, block, 1, shift + d * block) for d in (-1, 0, 1)
    }
    zero = jnp.zeros((block, block), jnp.float32)
    rows = [
        jnp.concatenate([parts.get(i - j, zero) for j in range(count)], axis=1)
        for i in range(count)
    ]
    return jnp.concatenate(rows, axis=0)


def pyramid_matrix(row_count, col_count, anchor):
    offset_index = (
        lax.broadcasted_iota(jnp.int32, (row_count, col_count), 0)
        - 2 * lax.broadcasted_iota(jnp.int32, (row_count, col_count), 1)
        + anchor
    )
    outer = (offset_index == 0) | (offset_index == 3)
    middle = (offset_index == 1) | (offset_index == 2)
    return jnp.where(
        outer, jnp.float32(0.125), jnp.where(middle, jnp.float32(0.375), jnp.float32(0.0))
    )


def along_columns(volume, matrix, transpose=False):
    contract = 1 if transpose else 0
    return lax.dot_general(
        volume, matrix, (((2,), (contract,)), ((), ())), precision=PRECISE
    )


def along_rows(volume, matrix):
    planes = volume.shape[0]
    left = jnp.broadcast_to(matrix.T[None], (planes,) + matrix.T.shape)
    return lax.dot_general(
        left, volume, (((2,), (1,)), ((0,), (0,))), precision=PRECISE
    )


def along_planes(volume, matrix):
    return lax.dot_general(
        matrix.T, volume, (((1,), (0,)), ((), ())), precision=PRECISE
    )


def shards(estimate, observed, kernel_rows, kernel_columns, kernel_planes):
    plane_count, row_count, col_count = estimate.shape
    taps = kernel_rows.shape[0]
    reach = (taps - 1) // 2

    estimate_ext = halo(estimate, "tile", 1, reach, reach)
    col_band = band_square(kernel_columns, col_count, reach)
    blurred = along_columns(estimate_ext, col_band)
    rows_ext = row_count + 2 * reach
    blurred = along_rows(blurred, band(kernel_rows, rows_ext, row_count, 1, 0))
    blurred = halo(blurred, "slab", 0, reach, reach)
    planes_ext = plane_count + 2 * reach
    blurred = along_planes(blurred, band(kernel_planes, planes_ext, plane_count, 1, 0))

    quotient = observed / blurred

    spread = halo(quotient, "slab", 0, reach, reach)
    spread = along_planes(
        spread, band(kernel_planes, planes_ext, plane_count, -1, 2 * reach)
    )
    spread = along_columns(spread, col_band, transpose=True)
    spread = halo(spread, "tile", 1, reach, reach)
    correction = along_rows(spread, band(kernel_rows, rows_ext, row_count, -1, 2 * reach))
    new_estimate = estimate * correction

    halved = along_columns(new_estimate, pyramid_matrix(col_count, col_count // 2, 1))
    halved = halo(halved, "tile", 1, 1, 1)
    pyramid_level = along_rows(halved, pyramid_matrix(row_count + 2, row_count // 2, 0))
    return (new_estimate, pyramid_level)


def solution(mesh):
    in_specs = (P("slab", "tile", None), P("slab", "tile", None), P(), P(), P())
    out_specs = (P("slab", "tile", None), P("slab", "tile", None))
    return jax.shard_map(shards, mesh=mesh, in_specs=in_specs, out_specs=out_specs, check_vma=False)
```

time: 232 us -> 211 us (0.909)
  local copies, waits for them, and re-layouts: 97.8 us -> 6.12 us
  other arithmetic: 10.3 us -> 96.9 us
  blocking collectives: 16.3 us -> 0 us
  waiting for transfers between devices: 18.8 us -> 25.2 us
    select_n x4 -> x6, other arithmetic: 0.06 us -> 96.7 us  [the longest x5 96.6 us: band(): matrix = jnp.where(offset == tap, kernel[tap], matrix)]
    gather x10 -> x0, local copies, waits for them, and re-layouts: 60.7 us -> none  [banded(): values = jnp.take(kernel, jnp.clip(offset_index, 0, tap_count - 1))]
    unnamed x17 -> x12, local copies, waits for them, and re-layouts: 19.8 us -> 0.03 us
    all_to_all x1 -> x0, blocking collectives: 16.3 us -> none  [shards(): lax.all_to_all(turned_back, 'slab', split_axis=0, concat_axis=2, tiled=True)]
    all_to_all x3 -> x0, starting transfers between devices: 15.7 us -> none  [the longest x1 6.43 us: shards(): lax.all_to_all(quotient, 'slab', split_axis=2, concat_axis=0, tiled=True)]
    ppermute x6 -> x10, waiting for transfers between devices: 10.5 us -> 25.2 us  [the longest x5 15.4 us: halo(): pieces_before.insert(0, lax.ppermute(piece, axis, up))]
    ppermute x6 -> x10, starting transfers between devices: 16.3 us -> 29.9 us  [the longest x5 19.7 us: halo(): pieces_before.insert(0, lax.ppermute(piece, axis, up))]
    all_to_all x6 -> x0, local copies, waits for them, and re-layouts: 10.6 us -> none  [the longest x2 3.84 us: shards(): lax.all_to_all(partial_value, 'slab', split_axis=2, concat_axis=0, tiled=...]
  transfers between devices with their start and end apart: 9 -> 10, of which waited for: 5 -> 5; matrix products, arithmetic and copies ran while one was open for 28% -> 48% of each run, Pallas kernels for 0% -> 0%
where the time goes in v1:
time: 211 us; the launch traced here: 208 us
  other arithmetic  96.9 us (46%)
  matrix products  49.1 us (23%)
  starting transfers between devices  29.9 us (14%)
  waiting for transfers between devices  25.2 us (12%)
  local copies, waits for them, and re-layouts  6.12 us (3%)
    select_n x5, other arithmetic, band(): matrix = jnp.where(offset == tap, kernel[tap], matrix)  96.6 us
    dot_general x2, matrix products, along_planes(): lax.dot_general(matrix.T, volume, (((1,), (0,)), ((), ())), precision=PRE...  41.5 us
    ppermute x5, starting transfers between devices, halo(): pieces_before.insert(0, lax.ppermute(piece, axis, up))  19.7 us
    ppermute x5, waiting for transfers between devices, halo(): pieces_before.insert(0, lax.ppermute(piece, axis, up))  15.4 us
    ppermute x5, starting transfers between devices, halo(): pieces_after.append(lax.ppermute(piece, axis, down))  10.2 us
    ppermute x5, waiting for transfers between devices, halo(): pieces_after.append(lax.ppermute(piece, axis, down))  9.77 us
    dot_general x3, matrix products, along_columns(): lax.dot_general(volume, matrix, (((2,), (contract,)), ((), ())), precisio...  4.73 us
    slice x6, local copies, waits for them, and re-layouts, band(): matrix = jnp.where(offset == tap, kernel[tap], matrix)  4.27 us
  transfers between devices with their start and end apart: 10, of which 5 were waited for; matrix products, arithmetic and copies ran while one was open for 48% of the time, Pallas kernels for 0%

profile of v1, /device:TPU:11, one launch (start us, length us, event | category | flops | bytes accessed | tf_op | source)
XLA Modules:
  0.0 208.3 jit_solution(16345571272062152877)
XLA Ops:
  0.6 0.0 copy-start
  0.6 0.0 copy-start.3
  0.6 0.0 copy-start.4
  0.7 1.5 fusion.617
  2.1 3.7 %collective-permute-start = (f32[16,15,512]{2,1,0:T(8,128)S(1)}, f32[16,15,512]{2,1,0:T(8,128)S(1)}, u32[]{:S(2)}, u32[]{:S(2)}) collective-permute-start(f32[16,15,512]{2,1,0:T(8,128)S(1)} %get-tuple-element.8), channel_id=1, source_target_pairs={{0,4},{4,8},{8,12},{12,16},{16,20},{20,24},{24,28},{1,5},{5,9},{9,... | collective-permute-start | bytes 1474568 | tf_op jit(solution)/shard_map/ppermute | solution.py:19
  5.8 1.9 collective-permute-start.1
  7.7 0.0 copy-done.3
  7.8 0.7 fusion.621
  8.5 0.7 fusion.622
  9.2 0.0 copy-done.4
  9.2 0.7 fusion.624
  9.9 19.3 %select_select_fusion.3 = f32[16,46]{1,0:T(8,128)S(1)} fusion(f32[]{:T(128)} %bitcast.30, f32[]{:T(128)} %bitcast.29, f32[]{:T(128)} %bitcast.28, f32[]{:T(128)} %bitcast.27, f32[]{:T(128)} %bitcast.26, f32[]{:T(128)} %bitcast.25, f32[]{:T(128)} %bitcast.24, f32[]{:T(128)} %bitcast.23, f32[]{:T(128)} %bitcast.22, f32[]{:T(128)} %bitcast.21, f32[]{:T(128)} %bitcast.20, ...), kind=kLoop, calls=%fused_computation.157 | loop fusion | flops 46368 | bytes 3068 | tf_op jit(solution)/shard_map/jit(_where)/select_n | solution.py:35
  29.2 0.7 fusion.623
  29.9 19.3 %select_select_fusion.1 = f32[128,128]{1,0:T(8,128)S(1)} fusion(f32[]{:T(128)} %bitcast.94, f32[]{:T(128)} %bitcast.93, f32[]{:T(128)} %bitcast.92, f32[]{:T(128)} %bitcast.91, f32[]{:T(128)} %bitcast.90, f32[]{:T(128)} %bitcast.89, f32[]{:T(128)} %bitcast.88, f32[]{:T(128)} %bitcast.87, f32[]{:T(128)} %bitcast.86, f32[]{:T(128)} %bitcast.85, f32[]{:T(128)} %bitcast.84, ...), kind=kLoop, calls=%fused_computation.52 | loop fusion | flops 1048576 | bytes 65660 | tf_op jit(solution)/shard_map/jit(_where)/select_n | solution.py:35
  49.2 19.3 %select_select_fusion = f32[128,128]{1,0:T(8,128)S(1)} fusion(f32[]{:T(128)} %bitcast.94, f32[]{:T(128)} %bitcast.93, f32[]{:T(128)} %bitcast.92, f32[]{:T(128)} %bitcast.91, f32[]{:T(128)} %bitcast.90, f32[]{:T(128)} %bitcast.89, f32[]{:T(128)} %bitcast.88, f32[]{:T(128)} %bitcast.87, f32[]{:T(128)} %bitcast.86, f32[]{:T(128)} %bitcast.85, f32[]{:T(128)} %bitcast.84, ...), kind=kLoop, calls=%fused_computation.51 | loop fusion | flops 1048576 | bytes 65660 | tf_op jit(solution)/shard_map/jit(_where)/select_n | solution.py:35
  68.6 19.5 %select_select_fusion.2 = f32[128,128]{1,0:T(8,128)S(1)} fusion(f32[]{:T(128)} %bitcast.94, f32[]{:T(128)} %bitcast.93, f32[]{:T(128)} %bitcast.92, f32[]{:T(128)} %bitcast.91, f32[]{:T(128)} %bitcast.90, f32[]{:T(128)} %bitcast.89, f32[]{:T(128)} %bitcast.88, f32[]{:T(128)} %bitcast.87, f32[]{:T(128)} %bitcast.86, f32[]{:T(128)} %bitcast.85, f32[]{:T(128)} %bitcast.84, ...), kind=kLoop, calls=%fused_computation.53 | loop fusion | flops 1048576 | bytes 65660 | tf_op jit(solution)/shard_map/jit(_where)/select_n | solution.py:35
  88.0 0.0 collective-permute-done
  88.0 0.0 collective-permute-done.1
  88.1 0.0 copy-done
  88.1 2.7 %fusion = f32[16,46,512]{2,1,0:T(8,128)S(1)} fusion(f32[16,15,512]{2,1,0:T(8,128)S(1)} %collective-permute-done.1, f32[16,16,512]{2,1,0:T(8,128)S(1)} %copy-done, f32[16,15,512]{2,1,0:T(8,128)S(1)} %collective-permute-done, f32[128,128]{1,0:T(8,128)S(1)} %select_select_fusion.2, f32[128,128]{1,0:T(8,128)S(1)} %select_select_fusion, ...), kind=kOutput, calls=%fused_computation | convolution fusion | flops 2319417344 | bytes 3407872 | tf_op jit(solution)/shard_map/dot_general | solution.py:71
  90.8 0.0 copy-start.5
  90.8 0.9 fusion.150
  91.7 0.1 fusion.616
  91.8 3.2 %collective-permute-start.2 = (f32[15,16,512]{2,1,0:T(8,128)S(1)}, f32[15,16,512]{2,1,0:T(8,128)S(1)}, u32[]{:S(2)}, u32[]{:S(2)}) collective-permute-start(f32[15,16,512]{2,1,0:T(8,128)S(1)} %get-tuple-element.6), channel_id=1, source_target_pairs={{0,1},{1,2},{2,3},{4,5},{5,6},{6,7},{8,9},{9,10},{10,11},{12,13},{... | collective-permute-start | bytes 1474568 | tf_op jit(solution)/shard_map/ppermute | solution.py:19
  95.0 2.1 %collective-permute-start.3 = (f32[15,16,512]{2,1,0:T(8,128)S(1)}, f32[15,16,512]{2,1,0:T(8,128)S(1)}, u32[]{:S(2)}, u32[]{:S(2)}) collective-permute-start(f32[15,16,512]{2,1,0:T(8,128)S(1)} %get-tuple-element.7), channel_id=1, source_target_pairs={{1,0},{2,1},{3,2},{5,4},{6,5},{7,6},{9,8},{10,9},{11,10},{13,12},{... | collective-permute-start | bytes 1474568 | tf_op jit(solution)/shard_map/ppermute | solution.py:23
  97.1 0.0 copy-done.5
  97.2 0.7 fusion.620
  97.9 0.0 copy-start.2
  97.9 0.7 fusion.619
  98.6 7.3 %collective-permute-done.2 = f32[15,16,512]{2,1,0:T(8,128)S(1)} collective-permute-done((f32[15,16,512]{2,1,0:T(8,128)S(1)}, f32[15,16,512]{2,1,0:T(8,128)S(1)}, u32[]{:S(2)}, u32[]{:S(2)}) %collective-permute-start.2) | collective-permute-done | bytes 491552 | tf_op jit(solution)/shard_map/ppermute | solution.py:19
  105.9 2.9 %collective-permute-done.3 = f32[15,16,512]{2,1,0:T(8,128)S(1)} collective-permute-done((f32[15,16,512]{2,1,0:T(8,128)S(1)}, f32[15,16,512]{2,1,0:T(8,128)S(1)}, u32[]{:S(2)}, u32[]{:S(2)}) %collective-permute-start.3) | collective-permute-done | bytes 491552 | tf_op jit(solution)/shard_map/ppermute | solution.py:23
  108.7 0.2 pad_maximum_fusion
  108.9 0.0 copy-done.2
  109.0 21.2 %fusion.20 = f32[16,16,512]{2,0,1:T(8,128)S(1)} fusion(f32[46,16,512]{2,1,0:T(8,128)S(1)} %pad_maximum_fusion, f32[16,16,512]{2,1,0:T(8,128)S(1)} %copy-done.2, f32[]{:T(128)} %bitcast.61, f32[]{:T(128)} %bitcast.60, f32[]{:T(128)} %bitcast.59, f32[]{:T(128)} %bitcast.58, f32[]{:T(128)} %bitcast.57, f32[]{:T(128)} %bitcast.56, f32[]{:T(128)} %bitcast.55, ...), kind=kOutput, calls=%fused_computation.21 | convolution fusion | flops 72529184 | bytes 2556028 | tf_op jit(solution)/shard_map/dot_general | solution.py:85
  130.2 0.1 fusion.615
  130.3 3.2 %collective-permute-start.4 = (f32[15,16,512]{2,0,1:T(8,128)S(1)}, f32[15,16,512]{2,0,1:T(8,128)S(1)}, u32[]{:S(2)}, u32[]{:S(2)}) collective-permute-start(f32[15,16,512]{2,0,1:T(8,128)S(1)} %get-tuple-element.4), channel_id=1, source_target_pairs={{0,1},{1,2},{2,3},{4,5},{5,6},{6,7},{8,9},{9,10},{10,11},{12,13},{... | collective-permute-start | bytes 1474568 | tf_op jit(solution)/shard_map/ppermute | solution.py:19
  133.5 2.1 %collective-permute-start.5 = (f32[15,16,512]{2,0,1:T(8,128)S(1)}, f32[15,16,512]{2,0,1:T(8,128)S(1)}, u32[]{:S(2)}, u32[]{:S(2)}) collective-permute-start(f32[15,16,512]{2,0,1:T(8,128)S(1)} %get-tuple-element.5), channel_id=1, source_target_pairs={{1,0},{2,1},{3,2},{5,4},{6,5},{7,6},{9,8},{10,9},{11,10},{13,12},{... | collective-permute-start | bytes 1474568 | tf_op jit(solution)/shard_map/ppermute | solution.py:23
  135.6 8.2 %collective-permute-done.4 = f32[15,16,512]{2,0,1:T(8,128)S(1)} collective-permute-done((f32[15,16,512]{2,0,1:T(8,128)S(1)}, f32[15,16,512]{2,0,1:T(8,128)S(1)}, u32[]{:S(2)}, u32[]{:S(2)}) %collective-permute-start.4) | collective-permute-done | bytes 491552 | tf_op jit(solution)/shard_map/ppermute | solution.py:19
  143.8 2.9 %collective-permute-done.5 = f32[15,16,512]{2,0,1:T(8,128)S(1)} collective-permute-done((f32[15,16,512]{2,0,1:T(8,128)S(1)}, f32[15,16,512]{2,0,1:T(8,128)S(1)}, u32[]{:S(2)}, u32[]{:S(2)}) %collective-permute-start.5) | collective-permute-done | bytes 491552 | tf_op jit(solution)/shard_map/ppermute | solution.py:23
  146.7 20.3 %fusion.6 = f32[16,16,512]{2,0,1:T(8,128)S(1)} fusion(f32[15,16,512]{2,0,1:T(8,128)S(1)} %collective-permute-done.5, f32[16,16,512]{2,0,1:T(8,128)S(1)} %fusion.20, f32[15,16,512]{2,0,1:T(8,128)S(1)} %collective-permute-done.4, f32[]{:T(128)} %bitcast.61, f32[]{:T(128)} %bitcast.60, f32[]{:T(128)} %bitcast.59, f32[]{:T(128)} %bitcast.58, f32[]{:T(128)} %bitcast.57, ...), kind=kOutput, calls=%fused_computation.6 | convolution fusion | flops 73153248 | bytes 2031740 | tf_op jit(solution)/shard_map/dot_general | solution.py:85
  167.0 1.3 fusion.26
  168.4 0.1 fusion.614
  168.5 5.1 %collective-permute-start.6 = (f32[16,15,512]{2,1,0:T(8,128)S(1)}, f32[16,15,512]{2,1,0:T(8,128)S(1)}, u32[]{:S(2)}, u32[]{:S(2)}) collective-permute-start(f32[16,15,512]{2,1,0:T(8,128)S(1)} %get-tuple-element.2), channel_id=1, source_target_pairs={{0,4},{4,8},{8,12},{12,16},{16,20},{20,24},{24,28},{1,5},{5,9},{9,... | collective-permute-start | bytes 1474568 | tf_op jit(solution)/shard_map/ppermute | solution.py:19
  173.6 2.1 %collective-permute-start.7 = (f32[16,15,512]{2,1,0:T(8,128)S(1)}, f32[16,15,512]{2,1,0:T(8,128)S(1)}, u32[]{:S(2)}, u32[]{:S(2)}) collective-permute-start(f32[16,15,512]{2,1,0:T(8,128)S(1)} %get-tuple-element.3), channel_id=1, source_target_pairs={{4,0},{8,4},{12,8},{16,12},{20,16},{24,20},{28,24},{5,1},{9,5},{13... | collective-permute-start | bytes 1474568 | tf_op jit(solution)/shard_map/ppermute | solution.py:23
  175.7 19.3 %select_select_fusion.4 = f32[16,46]{1,0:T(8,128)S(1)} fusion(f32[]{:T(128)} %bitcast.30, f32[]{:T(128)} %bitcast.29, f32[]{:T(128)} %bitcast.28, f32[]{:T(128)} %bitcast.27, f32[]{:T(128)} %bitcast.26, f32[]{:T(128)} %bitcast.25, f32[]{:T(128)} %bitcast.24, f32[]{:T(128)} %bitcast.23, f32[]{:T(128)} %bitcast.22, f32[]{:T(128)} %bitcast.21, f32[]{:T(128)} %bitcast.20, ...), kind=kLoop, calls=%fused_computation.284 | loop fusion | flops 47840 | bytes 3068 | tf_op jit(solution)/shard_map/jit(_where)/select_n | solution.py:35
  195.0 0.0 collective-permute-done.6
  195.0 0.0 collective-permute-done.7
  195.0 1.0 fusion.23
  196.0 0.0 copy-start.1
  196.0 0.7 fusion.27
  196.8 4.5 %collective-permute-start.8 = (f32[16,1,256]{2,1,0:T(1,128)S(1)}, f32[16,1,256]{2,1,0:T(1,128)S(1)}, u32[]{:S(2)}, u32[]{:S(2)}) collective-permute-start(f32[16,1,256]{2,1,0:T(1,128)S(1)} %get-tuple-element.10), channel_id=1, source_target_pairs={{0,4},{4,8},{8,12},{12,16},{16,20},{20,24},{24,28},{1,5},{5,9},{9,... | collective-permute-start | bytes 49160 | tf_op jit(solution)/shard_map/ppermute | solution.py:19
  201.3 1.9 collective-permute-start.9
  203.2 0.1 select_select_fusion.5
  203.3 0.0 collective-permute-done.8
  203.3 4.0 %collective-permute-done.9 = f32[16,1,256]{2,1,0:T(1,128)S(1)} collective-permute-done((f32[16,1,256]{2,1,0:T(1,128)S(1)}, f32[16,1,256]{2,1,0:T(1,128)S(1)}, u32[]{:S(2)}, u32[]{:S(2)}) %collective-permute-start.9) | collective-permute-done | bytes 16416 | tf_op jit(solution)/shard_map/ppermute | solution.py:23
  207.3 1.0 fusion.40
  208.3 0.0 copy-done.1
  (5 shorter events, 0.0 us)
Async XLA Ops:
  0.6 87.5 %copy-start = (f32[16,16,512]{2,1,0:T(8,128)S(1)}, f32[16,16,512]{2,1,0:T(8,128)}, u32[]{:S(2)}) copy-start(f32[16,16,512]{2,1,0:T(8,128)} %param.5) | copy-start | bytes 1572868
  0.6 7.1 %copy-start.3 = (f32[31]{0:T(128)S(1)}, f32[31]{0:T(128)}, u32[]{:S(2)}) copy-start(f32[31]{0:T(128)} %param.7) | copy-start | bytes 376
  0.6 8.5 %copy-start.4 = (f32[31]{0:T(128)S(1)}, f32[31]{0:T(128)}, u32[]{:S(2)}) copy-start(f32[31]{0:T(128)} %param.8) | copy-start | bytes 376
  2.1 85.9 %collective-permute-start = (f32[16,15,512]{2,1,0:T(8,128)S(1)}, f32[16,15,512]{2,1,0:T(8,128)S(1)}, u32[]{:S(2)}, u32[]{:S(2)}) collective-permute-start(f32[16,15,512]{2,1,0:T(8,128)S(1)} %get-tuple-element.8), channel_id=1, source_target_pairs={{0,4},{4,8},{8,12},{12,16},{16,20},{20,24},{24,28},{1,5},{5,9},{9,... | collective-permute-start | bytes 1474568 | tf_op jit(solution)/shard_map/ppermute | solution.py:19
  5.8 82.2 %collective-permute-start.1 = (f32[16,15,512]{2,1,0:T(8,128)S(1)}, f32[16,15,512]{2,1,0:T(8,128)S(1)}, u32[]{:S(2)}, u32[]{:S(2)}) collective-permute-start(f32[16,15,512]{2,1,0:T(8,128)S(1)} %get-tuple-element.9), channel_id=1, source_target_pairs={{4,0},{8,4},{12,8},{16,12},{20,16},{24,20},{28,24},{5,1},{9,5},{13... | collective-permute-start | bytes 1474568 | tf_op jit(solution)/shard_map/ppermute | solution.py:23
  90.8 6.3 %copy-start.5 = (f32[31]{0:T(128)S(1)}, f32[31]{0:T(128)}, u32[]{:S(2)}) copy-start(f32[31]{0:T(128)} %param.9) | copy-start | bytes 376
  91.8 14.0 %collective-permute-start.2 = (f32[15,16,512]{2,1,0:T(8,128)S(1)}, f32[15,16,512]{2,1,0:T(8,128)S(1)}, u32[]{:S(2)}, u32[]{:S(2)}) collective-permute-start(f32[15,16,512]{2,1,0:T(8,128)S(1)} %get-tuple-element.6), channel_id=1, source_target_pairs={{0,1},{1,2},{2,3},{4,5},{5,6},{6,7},{8,9},{9,10},{10,11},{12,13},{... | collective-permute-start | bytes 1474568 | tf_op jit(solution)/shard_map/ppermute | solution.py:19
  95.0 13.7 %collective-permute-start.3 = (f32[15,16,512]{2,1,0:T(8,128)S(1)}, f32[15,16,512]{2,1,0:T(8,128)S(1)}, u32[]{:S(2)}, u32[]{:S(2)}) collective-permute-start(f32[15,16,512]{2,1,0:T(8,128)S(1)} %get-tuple-element.7), channel_id=1, source_target_pairs={{1,0},{2,1},{3,2},{5,4},{6,5},{7,6},{9,8},{10,9},{11,10},{13,12},{... | collective-permute-start | bytes 1474568 | tf_op jit(solution)/shard_map/ppermute | solution.py:23
  97.9 11.1 %copy-start.2 = (f32[16,16,512]{2,1,0:T(8,128)S(1)}, f32[16,16,512]{2,1,0:T(8,128)}, u32[]{:S(2)}) copy-start(f32[16,16,512]{2,1,0:T(8,128)} %param.6) | copy-start | bytes 1572868
  130.3 13.5 %collective-permute-start.4 = (f32[15,16,512]{2,0,1:T(8,128)S(1)}, f32[15,16,512]{2,0,1:T(8,128)S(1)}, u32[]{:S(2)}, u32[]{:S(2)}) collective-permute-start(f32[15,16,512]{2,0,1:T(8,128)S(1)} %get-tuple-element.4), channel_id=1, source_target_pairs={{0,1},{1,2},{2,3},{4,5},{5,6},{6,7},{8,9},{9,10},{10,11},{12,13},{... | collective-permute-start | bytes 1474568 | tf_op jit(solution)/shard_map/ppermute | solution.py:19
  133.5 13.2 %collective-permute-start.5 = (f32[15,16,512]{2,0,1:T(8,128)S(1)}, f32[15,16,512]{2,0,1:T(8,128)S(1)}, u32[]{:S(2)}, u32[]{:S(2)}) collective-permute-start(f32[15,16,512]{2,0,1:T(8,128)S(1)} %get-tuple-element.5), channel_id=1, source_target_pairs={{1,0},{2,1},{3,2},{5,4},{6,5},{7,6},{9,8},{10,9},{11,10},{13,12},{... | collective-permute-start | bytes 1474568 | tf_op jit(solution)/shard_map/ppermute | solution.py:23
  168.5 26.5 %collective-permute-start.6 = (f32[16,15,512]{2,1,0:T(8,128)S(1)}, f32[16,15,512]{2,1,0:T(8,128)S(1)}, u32[]{:S(2)}, u32[]{:S(2)}) collective-permute-start(f32[16,15,512]{2,1,0:T(8,128)S(1)} %get-tuple-element.2), channel_id=1, source_target_pairs={{0,4},{4,8},{8,12},{12,16},{16,20},{20,24},{24,28},{1,5},{5,9},{9,... | collective-permute-start | bytes 1474568 | tf_op jit(solution)/shard_map/ppermute | solution.py:19
  173.6 21.4 %collective-permute-start.7 = (f32[16,15,512]{2,1,0:T(8,128)S(1)}, f32[16,15,512]{2,1,0:T(8,128)S(1)}, u32[]{:S(2)}, u32[]{:S(2)}) collective-permute-start(f32[16,15,512]{2,1,0:T(8,128)S(1)} %get-tuple-element.3), channel_id=1, source_target_pairs={{4,0},{8,4},{12,8},{16,12},{20,16},{24,20},{28,24},{5,1},{9,5},{13... | collective-permute-start | bytes 1474568 | tf_op jit(solution)/shard_map/ppermute | solution.py:23
  196.0 12.3 %copy-start.1 = (f32[16,16,512]{2,1,0:T(8,128)}, f32[16,16,512]{2,1,0:T(8,128)S(1)}, u32[]{:S(2)}) copy-start(f32[16,16,512]{2,1,0:T(8,128)S(1)} %fusion.23) | copy-start | bytes 1572868
  196.8 6.6 %collective-permute-start.8 = (f32[16,1,256]{2,1,0:T(1,128)S(1)}, f32[16,1,256]{2,1,0:T(1,128)S(1)}, u32[]{:S(2)}, u32[]{:S(2)}) collective-permute-start(f32[16,1,256]{2,1,0:T(1,128)S(1)} %get-tuple-element.10), channel_id=1, source_target_pairs={{0,4},{4,8},{8,12},{12,16},{16,20},{20,24},{24,28},{1,5},{5,9},{9,... | collective-permute-start | bytes 49160 | tf_op jit(solution)/shard_map/ppermute | solution.py:19
  201.3 6.0 %collective-permute-start.9 = (f32[16,1,256]{2,1,0:T(1,128)S(1)}, f32[16,1,256]{2,1,0:T(1,128)S(1)}, u32[]{:S(2)}, u32[]{:S(2)}) collective-permute-start(f32[16,1,256]{2,1,0:T(1,128)S(1)} %get-tuple-element.11), channel_id=1, source_target_pairs={{4,0},{8,4},{12,8},{16,12},{20,16},{24,20},{28,24},{5,1},{9,5},{13... | collective-permute-start | bytes 49160 | tf_op jit(solution)/shard_map/ppermute | solution.py:23

commit v2 on v1

--- a/solution.py
+++ b/solution.py
@@ -30,10 +30,9 @@
         lax.broadcasted_iota(jnp.int32, (n_in, n_out), 0)
         - lax.broadcasted_iota(jnp.int32, (n_in, n_out), 1)
     ) + shift
-    matrix = jnp.zeros((n_in, n_out), jnp.float32)
-    for tap in range(kernel.shape[0]):
-        matrix = jnp.where(offset == tap, kernel[tap], matrix)
-    return matrix
+    taps = lax.broadcasted_iota(jnp.int32, (1, 1, kernel.shape[0]), 2)
+    picked = jnp.where(offset[:, :, None] == taps, kernel[None, None, :], 0.0)
+    return jnp.sum(picked, axis=2)
 
 
 def band_square(kernel, n, shift):
@@ -92,29 +91,37 @@
     taps = kernel_rows.shape[0]
     reach = (taps - 1) // 2
 
+    rows_ext = row_count + 2 * reach
+    planes_ext = plane_count + 2 * reach
+    bands = lax.optimization_barrier((
+        band_square(kernel_columns, col_count, reach),
+        band(kernel_rows, rows_ext, row_count, 1, 0),
+        band(kernel_planes, planes_ext, plane_count, 1, 0),
+        band(kernel_planes, planes_ext, plane_count, -1, 2 * reach),
+        band(kernel_rows, rows_ext, row_count, -1, 2 * reach),
+        pyramid_matrix(col_count, col_count // 2, 1),
+        pyramid_matrix(row_count + 2, row_count // 2, 0),
+    ))
+    col_band, row_fwd, plane_fwd, plane_back, row_back, pyr_cols, pyr_rows = bands
+
     estimate_ext = halo(estimate, "tile", 1, reach, reach)
-    col_band = band_square(kernel_columns, col_count, reach)
     blurred = along_columns(estimate_ext, col_band)
-    rows_ext = row_count + 2 * reach
-    blurred = along_rows(blurred, band(kernel_rows, rows_ext, row_count, 1, 0))
+    blurred = along_rows(blurred, row_fwd)
     blurred = halo(blurred, "slab", 0, reach, reach)
-    planes_ext = plane_count + 2 * reach
-    blurred = along_planes(blurred, band(kernel_planes, planes_ext, plane_count, 1, 0))
+    blurred = along_planes(blurred, plane_fwd)
 
     quotient = observed / blurred
 
     spread = halo(quotient, "slab", 0, reach, reach)
-    spread = along_planes(
-        spread, band(kernel_planes, planes_ext, plane_count, -1, 2 * reach)
-    )
+    spread = along_planes(spread, plane_back)
     spread = along_columns(spread, col_band, transpose=True)
     spread = halo(spread, "tile", 1, reach, reach)
-    correction = along_rows(spread, band(kernel_rows, rows_ext, row_count, -1, 2 * reach))
+    correction = along_rows(spread, row_back)
     new_estimate = estimate * correction
 
-    halved = along_columns(new_estimate, pyramid_matrix(col_count, col_count // 2, 1))
+    halved = along_columns(new_estimate, pyr_cols)
     halved = halo(halved, "tile", 1, 1, 1)
-    pyramid_level = along_rows(halved, pyramid_matrix(row_count + 2, row_count // 2, 0))
+    pyramid_level = along_rows(halved, pyr_rows)
     return (new_estimate, pyramid_level)
 
 

time: 211 us -> 89.6 us (0.42)
  the two profiles are of different devices: /device:TPU:11 before, /device:TPU:1 now
where the time goes in v2:
time: 89.6 us; the launch traced here: 89.2 us
  waiting for transfers between devices  38.7 us (43%)
  starting transfers between devices  36 us (40%)
  matrix products  10.4 us (12%)
  local copies, waits for them, and re-layouts  1.74 us (2%)
  other arithmetic  1.36 us (2%)
  between operations  0.97 us (1%)
    ppermute x5, starting transfers between devices, halo(): pieces_before.insert(0, lax.ppermute(piece, axis, up))  27.2 us
    ppermute x5, waiting for transfers between devices, halo(): pieces_after.append(lax.ppermute(piece, axis, down))  22.4 us
    ppermute x5, waiting for transfers between devices, halo(): pieces_before.insert(0, lax.ppermute(piece, axis, up))  16.3 us
    ppermute x5, starting transfers between devices, halo(): pieces_after.append(lax.ppermute(piece, axis, down))  8.83 us
    dot_general x3, matrix products, along_columns(): lax.dot_general(volume, matrix, (((2,), (contract,)), ((), ())), precisio...  4.65 us
    dot_general x2, matrix products, along_planes(): lax.dot_general(matrix.T, volume, (((1,), (0,)), ((), ())), precision=PRE...  2.9 us
    dot_general x3, matrix products, along_rows(): lax.dot_general(left, volume, (((2,), (1,)), ((0,), (0,))), precision=PRE...  2.87 us
  transfers between devices with their start and end apart: 10, of which 9 were waited for; matrix products, arithmetic and copies ran while one was open for 1% of the time, Pallas kernels for 0%

profile of v2, /device:TPU:1, one launch (start us, length us, event | category | flops | bytes accessed | tf_op | source)
XLA Modules:
  0.0 89.2 jit_solution(18145043288117519322)
XLA Ops:
  0.6 0.0 copy-start.3
  0.6 0.0 copy-start.4
  0.7 0.0 copy-start.5
  0.7 1.4 %fusion.66 = (f32[16,15,512]{2,1,0:T(8,128)S(1)}, f32[16,15,512]{2,1,0:T(8,128)S(1)}) fusion(f32[16,16,512]{2,1,0:T(8,128)} %param.5), kind=kLoop, calls=%fused_computation.85 | loop fusion | bytes 1966080 | tf_op jit(solution)/shard_map/slice | solution.py:18
  2.0 0.0 copy-start
  2.1 4.6 %collective-permute-start = (f32[16,15,512]{2,1,0:T(8,128)S(1)}, f32[16,15,512]{2,1,0:T(8,128)S(1)}, u32[]{:S(2)}, u32[]{:S(2)}) collective-permute-start(f32[16,15,512]{2,1,0:T(8,128)S(1)} %get-tuple-element.31), channel_id=1, source_target_pairs={{0,4},{4,8},{8,12},{12,16},{16,20},{20,24},{24,28},{1,5},{5,9},{9,... | collective-permute-start | bytes 1474568 | tf_op jit(solution)/shard_map/ppermute | solution.py:19
  6.7 1.9 %collective-permute-start.1 = (f32[16,15,512]{2,1,0:T(8,128)S(1)}, f32[16,15,512]{2,1,0:T(8,128)S(1)}, u32[]{:S(2)}, u32[]{:S(2)}) collective-permute-start(f32[16,15,512]{2,1,0:T(8,128)S(1)} %get-tuple-element.32), channel_id=1, source_target_pairs={{4,0},{8,4},{12,8},{16,12},{20,16},{24,20},{28,24},{5,1},{9,5},{13... | collective-permute-start | bytes 1474568 | tf_op jit(solution)/shard_map/ppermute | solution.py:23
  8.7 0.0 copy-done.3
  8.7 0.0 copy-done.4
  8.7 0.2 select_reduce_fusion.5
  8.9 0.0 copy-done.5
  8.9 0.7 select_reduce_fusion.1
  9.6 0.1 maximum_maximum_fusion
  9.7 0.1 select_select_fusion.1
  9.8 0.1 select_select_fusion
  9.9 2.9 %collective-permute-done = f32[16,15,512]{2,1,0:T(8,128)S(1)} collective-permute-done((f32[16,15,512]{2,1,0:T(8,128)S(1)}, f32[16,15,512]{2,1,0:T(8,128)S(1)}, u32[]{:S(2)}, u32[]{:S(2)}) %collective-permute-start) | collective-permute-done | bytes 491552 | tf_op jit(solution)/shard_map/ppermute | solution.py:19
  12.8 7.3 %collective-permute-done.1 = f32[16,15,512]{2,1,0:T(8,128)S(1)} collective-permute-done((f32[16,15,512]{2,1,0:T(8,128)S(1)}, f32[16,15,512]{2,1,0:T(8,128)S(1)}, u32[]{:S(2)}, u32[]{:S(2)}) %collective-permute-start.1) | collective-permute-done | bytes 491552 | tf_op jit(solution)/shard_map/ppermute | solution.py:23
  20.1 0.0 copy-done
  20.1 2.7 %fusion = f32[16,46,512]{2,1,0:T(8,128)S(1)} fusion(f32[16,15,512]{2,1,0:T(8,128)S(1)} %collective-permute-done.1, f32[16,16,512]{2,1,0:T(8,128)S(1)} %copy-done, f32[16,15,512]{2,1,0:T(8,128)S(1)} %collective-permute-done, f32[512,512]{1,0:T(8,128)S(1)} %maximum_maximum_fusion), kind=kOutput, calls=%fused_computation.6 | convolution fusion | flops 2316009472 | bytes 4063232 | tf_op jit(solution)/shard_map/dot_general | solution.py:70
  22.8 0.9 fusion.44
  23.7 0.1 fusion.65
  23.8 0.0 copy-start.2
  23.8 3.7 %collective-permute-start.2 = (f32[15,16,512]{2,1,0:T(8,128)S(1)}, f32[15,16,512]{2,1,0:T(8,128)S(1)}, u32[]{:S(2)}, u32[]{:S(2)}) collective-permute-start(f32[15,16,512]{2,1,0:T(8,128)S(1)} %get-tuple-element.29), channel_id=1, source_target_pairs={{0,1},{1,2},{2,3},{4,5},{5,6},{6,7},{8,9},{9,10},{10,11},{12,13},{... | collective-permute-start | bytes 1474568 | tf_op jit(solution)/shard_map/ppermute | solution.py:19
  27.5 1.3 %collective-permute-start.3 = (f32[15,16,512]{2,1,0:T(8,128)S(1)}, f32[15,16,512]{2,1,0:T(8,128)S(1)}, u32[]{:S(2)}, u32[]{:S(2)}) collective-permute-start(f32[15,16,512]{2,1,0:T(8,128)S(1)} %get-tuple-element.30), channel_id=1, source_target_pairs={{1,0},{2,1},{3,2},{5,4},{6,5},{7,6},{9,8},{10,9},{11,10},{13,12},{... | collective-permute-start | bytes 1474568 | tf_op jit(solution)/shard_map/ppermute | solution.py:23
  28.8 4.4 %collective-permute-done.2 = f32[15,16,512]{2,1,0:T(8,128)S(1)} collective-permute-done((f32[15,16,512]{2,1,0:T(8,128)S(1)}, f32[15,16,512]{2,1,0:T(8,128)S(1)}, u32[]{:S(2)}, u32[]{:S(2)}) %collective-permute-start.2) | collective-permute-done | bytes 491552 | tf_op jit(solution)/shard_map/ppermute | solution.py:19
  33.2 3.8 %collective-permute-done.3 = f32[15,16,512]{2,1,0:T(8,128)S(1)} collective-permute-done((f32[15,16,512]{2,1,0:T(8,128)S(1)}, f32[15,16,512]{2,1,0:T(8,128)S(1)}, u32[]{:S(2)}, u32[]{:S(2)}) %collective-permute-start.3) | collective-permute-done | bytes 491552 | tf_op jit(solution)/shard_map/ppermute | solution.py:23
  37.1 0.2 pad_maximum_fusion
  37.2 0.0 copy-done.2
  37.3 1.9 %fusion.20 = f32[16,16,512]{2,0,1:T(8,128)S(1)} fusion(f32[46,16,512]{2,1,0:T(8,128)S(1)} %pad_maximum_fusion, f32[16,16,512]{2,1,0:T(8,128)S(1)} %copy-done.2, f32[46,16]{0,1:T(8,128)S(1)} %get-tuple-element.11), kind=kOutput, calls=%fused_computation.27 | convolution fusion | flops 72482816 | bytes 2558848 | tf_op jit(solution)/shard_map/dot_general | solution.py:84
  39.2 0.1 fusion.64
  39.3 3.5 %collective-permute-start.4 = (f32[15,16,512]{2,0,1:T(8,128)S(1)}, f32[15,16,512]{2,0,1:T(8,128)S(1)}, u32[]{:S(2)}, u32[]{:S(2)}) collective-permute-start(f32[15,16,512]{2,0,1:T(8,128)S(1)} %get-tuple-element.27), channel_id=1, source_target_pairs={{0,1},{1,2},{2,3},{4,5},{5,6},{6,7},{8,9},{9,10},{10,11},{12,13},{... | collective-permute-start | bytes 1474568 | tf_op jit(solution)/shard_map/ppermute | solution.py:19
  42.8 1.3 %collective-permute-start.5 = (f32[15,16,512]{2,0,1:T(8,128)S(1)}, f32[15,16,512]{2,0,1:T(8,128)S(1)}, u32[]{:S(2)}, u32[]{:S(2)}) collective-permute-start(f32[15,16,512]{2,0,1:T(8,128)S(1)} %get-tuple-element.28), channel_id=1, source_target_pairs={{1,0},{2,1},{3,2},{5,4},{6,5},{7,6},{9,8},{10,9},{11,10},{13,12},{... | collective-permute-start | bytes 1474568 | tf_op jit(solution)/shard_map/ppermute | solution.py:23
  44.1 4.8 %collective-permute-done.4 = f32[15,16,512]{2,0,1:T(8,128)S(1)} collective-permute-done((f32[15,16,512]{2,0,1:T(8,128)S(1)}, f32[15,16,512]{2,0,1:T(8,128)S(1)}, u32[]{:S(2)}, u32[]{:S(2)}) %collective-permute-start.4) | collective-permute-done | bytes 491552 | tf_op jit(solution)/shard_map/ppermute | solution.py:19
  48.9 3.8 %collective-permute-done.5 = f32[15,16,512]{2,0,1:T(8,128)S(1)} collective-permute-done((f32[15,16,512]{2,0,1:T(8,128)S(1)}, f32[15,16,512]{2,0,1:T(8,128)S(1)}, u32[]{:S(2)}, u32[]{:S(2)}) %collective-permute-start.5) | collective-permute-done | bytes 491552 | tf_op jit(solution)/shard_map/ppermute | solution.py:23
  52.7 1.0 %fusion.6 = f32[16,16,512]{2,0,1:T(8,128)S(1)} fusion(f32[15,16,512]{2,0,1:T(8,128)S(1)} %collective-permute-done.5, f32[16,16,512]{2,0,1:T(8,128)S(1)} %fusion.20, f32[15,16,512]{2,0,1:T(8,128)S(1)} %collective-permute-done.4, f32[46,16]{0,1:T(8,128)S(1)} %get-tuple-element.10), kind=kOutput, calls=%fused_computation.12 | convolution fusion | flops 73105408 | bytes 2034560 | tf_op jit(solution)/shard_map/dot_general | solution.py:84
  53.7 1.3 %fusion.26 = f32[16,16,512]{2,1,0:T(8,128)S(1)} fusion(f32[512,512]{1,0:T(8,128)S(1)} %maximum_maximum_fusion, f32[16,16,512]{2,0,1:T(8,128)S(1)} %fusion.6), kind=kOutput, calls=%fused_computation.30 | convolution fusion | flops 805306368 | bytes 2097152 | tf_op jit(solution)/shard_map/dot_general | solution.py:70
  55.0 0.1 fusion.63
  55.1 13.5 %collective-permute-start.6 = (f32[16,15,512]{2,1,0:T(8,128)S(1)}, f32[16,15,512]{2,1,0:T(8,128)S(1)}, u32[]{:S(2)}, u32[]{:S(2)}) collective-permute-start(f32[16,15,512]{2,1,0:T(8,128)S(1)} %get-tuple-element.25), channel_id=1, source_target_pairs={{0,4},{4,8},{8,12},{12,16},{16,20},{20,24},{24,28},{1,5},{5,9},{9,... | collective-permute-start | bytes 1474568 | tf_op jit(solution)/shard_map/ppermute | solution.py:19
  68.6 1.9 %collective-permute-start.7 = (f32[16,15,512]{2,1,0:T(8,128)S(1)}, f32[16,15,512]{2,1,0:T(8,128)S(1)}, u32[]{:S(2)}, u32[]{:S(2)}) collective-permute-start(f32[16,15,512]{2,1,0:T(8,128)S(1)} %get-tuple-element.26), channel_id=1, source_target_pairs={{4,0},{8,4},{12,8},{16,12},{20,16},{24,20},{28,24},{5,1},{9,5},{13... | collective-permute-start | bytes 1474568 | tf_op jit(solution)/shard_map/ppermute | solution.py:23
  70.5 4.2 %collective-permute-done.6 = f32[16,15,512]{2,1,0:T(8,128)S(1)} collective-permute-done((f32[16,15,512]{2,1,0:T(8,128)S(1)}, f32[16,15,512]{2,1,0:T(8,128)S(1)}, u32[]{:S(2)}, u32[]{:S(2)}) %collective-permute-start.6) | collective-permute-done | bytes 491552 | tf_op jit(solution)/shard_map/ppermute | solution.py:19
  74.7 4.8 %collective-permute-done.7 = f32[16,15,512]{2,1,0:T(8,128)S(1)} collective-permute-done((f32[16,15,512]{2,1,0:T(8,128)S(1)}, f32[16,15,512]{2,1,0:T(8,128)S(1)}, u32[]{:S(2)}, u32[]{:S(2)}) %collective-permute-start.7) | collective-permute-done | bytes 491552 | tf_op jit(solution)/shard_map/ppermute | solution.py:23
  79.5 1.0 %fusion.23 = f32[16,16,512]{2,1,0:T(8,128)S(1)} fusion(f32[16,16,512]{2,1,0:T(8,128)S(1)} %copy-done, f32[16,15,512]{2,1,0:T(8,128)S(1)} %collective-permute-done.7, f32[16,16,512]{2,1,0:T(8,128)S(1)} %fusion.26, f32[16,15,512]{2,1,0:T(8,128)S(1)} %collective-permute-done.6, f32[16,46]{1,0:T(8,128)S(1)} %bitcast.19), kind=kOutput, calls=%fused_computation.28 | convolution fusion | flops 73236480 | bytes 2558848 | tf_op jit(solution)/shard_map/dot_general | solution.py:78
  80.5 0.0 copy-start.1
  80.5 0.6 fusion.29
  81.2 1.9 %collective-permute-start.8 = (f32[16,1,256]{2,1,0:T(1,128)S(1)}, f32[16,1,256]{2,1,0:T(1,128)S(1)}, u32[]{:S(2)}, u32[]{:S(2)}) collective-permute-start(f32[16,1,256]{2,1,0:T(1,128)S(1)} %get-tuple-element.33), channel_id=1, source_target_pairs={{0,4},{4,8},{8,12},{12,16},{16,20},{20,24},{24,28},{1,5},{5,9},{9,... | collective-permute-start | bytes 49160 | tf_op jit(solution)/shard_map/ppermute | solution.py:19
  83.1 2.4 %collective-permute-start.9 = (f32[16,1,256]{2,1,0:T(1,128)S(1)}, f32[16,1,256]{2,1,0:T(1,128)S(1)}, u32[]{:S(2)}, u32[]{:S(2)}) collective-permute-start(f32[16,1,256]{2,1,0:T(1,128)S(1)} %get-tuple-element.34), channel_id=1, source_target_pairs={{4,0},{8,4},{12,8},{16,12},{20,16},{24,20},{28,24},{5,1},{9,5},{13... | collective-permute-start | bytes 49160 | tf_op jit(solution)/shard_map/ppermute | solution.py:23
  85.5 0.0 collective-permute-done.8
  85.5 2.6 %collective-permute-done.9 = f32[16,1,256]{2,1,0:T(1,128)S(1)} collective-permute-done((f32[16,1,256]{2,1,0:T(1,128)S(1)}, f32[16,1,256]{2,1,0:T(1,128)S(1)}, u32[]{:S(2)}, u32[]{:S(2)}) %collective-permute-start.9) | collective-permute-done | bytes 16416 | tf_op jit(solution)/shard_map/ppermute | solution.py:23
  88.2 1.0 %fusion.38 = f32[16,8,256]{2,1,0:T(8,128)} fusion(f32[16,1,256]{2,1,0:T(1,128)S(1)} %collective-permute-done.9, f32[16,16,256]{2,1,0:T(8,128)S(1)} %fusion.29, f32[16,1,256]{2,1,0:T(1,128)S(1)} %collective-permute-done.8, f32[8,18]{1,0:T(8,128)S(1)} %bitcast.21), kind=kOutput, calls=%fused_computation.44 | convolution fusion | flops 7225344 | bytes 426560 | tf_op jit(solution)/shard_map/dot_general | solution.py:78
  89.2 0.0 copy-done.1
  (8 shorter events, 0.1 us)
Async XLA Ops:
  0.6 8.1 %copy-start.3 = (f32[31]{0:T(128)S(1)}, f32[31]{0:T(128)}, u32[]{:S(2)}) copy-start(f32[31]{0:T(128)} %param.9) | copy-start | bytes 376
  0.6 8.1 %copy-start.4 = (f32[31]{0:T(128)S(1)}, f32[31]{0:T(128)}, u32[]{:S(2)}) copy-start(f32[31]{0:T(128)} %param.7) | copy-start | bytes 376
  0.7 8.3 %copy-start.5 = (f32[31]{0:T(128)S(1)}, f32[31]{0:T(128)}, u32[]{:S(2)}) copy-start(f32[31]{0:T(128)} %param.8) | copy-start | bytes 376
  2.0 18.0 %copy-start = (f32[16,16,512]{2,1,0:T(8,128)S(1)}, f32[16,16,512]{2,1,0:T(8,128)}, u32[]{:S(2)}) copy-start(f32[16,16,512]{2,1,0:T(8,128)} %param.5) | copy-start | bytes 1572868
  2.1 10.8 %collective-permute-start = (f32[16,15,512]{2,1,0:T(8,128)S(1)}, f32[16,15,512]{2,1,0:T(8,128)S(1)}, u32[]{:S(2)}, u32[]{:S(2)}) collective-permute-start(f32[16,15,512]{2,1,0:T(8,128)S(1)} %get-tuple-element.31), channel_id=1, source_target_pairs={{0,4},{4,8},{8,12},{12,16},{16,20},{20,24},{24,28},{1,5},{5,9},{9,... | collective-permute-start | bytes 1474568 | tf_op jit(solution)/shard_map/ppermute | solution.py:19
  6.7 13.4 %collective-permute-start.1 = (f32[16,15,512]{2,1,0:T(8,128)S(1)}, f32[16,15,512]{2,1,0:T(8,128)S(1)}, u32[]{:S(2)}, u32[]{:S(2)}) collective-permute-start(f32[16,15,512]{2,1,0:T(8,128)S(1)} %get-tuple-element.32), channel_id=1, source_target_pairs={{4,0},{8,4},{12,8},{16,12},{20,16},{24,20},{28,24},{5,1},{9,5},{13... | collective-permute-start | bytes 1474568 | tf_op jit(solution)/shard_map/ppermute | solution.py:23
  23.8 13.5 %copy-start.2 = (f32[16,16,512]{2,1,0:T(8,128)S(1)}, f32[16,16,512]{2,1,0:T(8,128)}, u32[]{:S(2)}) copy-start(f32[16,16,512]{2,1,0:T(8,128)} %param.6) | copy-start | bytes 1572868
  23.8 9.4 %collective-permute-start.2 = (f32[15,16,512]{2,1,0:T(8,128)S(1)}, f32[15,16,512]{2,1,0:T(8,128)S(1)}, u32[]{:S(2)}, u32[]{:S(2)}) collective-permute-start(f32[15,16,512]{2,1,0:T(8,128)S(1)} %get-tuple-element.29), channel_id=1, source_target_pairs={{0,1},{1,2},{2,3},{4,5},{5,6},{6,7},{8,9},{9,10},{10,11},{12,13},{... | collective-permute-start | bytes 1474568 | tf_op jit(solution)/shard_map/ppermute | solution.py:19
  27.5 9.6 %collective-permute-start.3 = (f32[15,16,512]{2,1,0:T(8,128)S(1)}, f32[15,16,512]{2,1,0:T(8,128)S(1)}, u32[]{:S(2)}, u32[]{:S(2)}) collective-permute-start(f32[15,16,512]{2,1,0:T(8,128)S(1)} %get-tuple-element.30), channel_id=1, source_target_pairs={{1,0},{2,1},{3,2},{5,4},{6,5},{7,6},{9,8},{10,9},{11,10},{13,12},{... | collective-permute-start | bytes 1474568 | tf_op jit(solution)/shard_map/ppermute | solution.py:23
  39.3 9.6 %collective-permute-start.4 = (f32[15,16,512]{2,0,1:T(8,128)S(1)}, f32[15,16,512]{2,0,1:T(8,128)S(1)}, u32[]{:S(2)}, u32[]{:S(2)}) collective-permute-start(f32[15,16,512]{2,0,1:T(8,128)S(1)} %get-tuple-element.27), channel_id=1, source_target_pairs={{0,1},{1,2},{2,3},{4,5},{5,6},{6,7},{8,9},{9,10},{10,11},{12,13},{... | collective-permute-start | bytes 1474568 | tf_op jit(solution)/shard_map/ppermute | solution.py:19
  42.8 9.9 %collective-permute-start.5 = (f32[15,16,512]{2,0,1:T(8,128)S(1)}, f32[15,16,512]{2,0,1:T(8,128)S(1)}, u32[]{:S(2)}, u32[]{:S(2)}) collective-permute-start(f32[15,16,512]{2,0,1:T(8,128)S(1)} %get-tuple-element.28), channel_id=1, source_target_pairs={{1,0},{2,1},{3,2},{5,4},{6,5},{7,6},{9,8},{10,9},{11,10},{13,12},{... | collective-permute-start | bytes 1474568 | tf_op jit(solution)/shard_map/ppermute | solution.py:23
  55.1 19.6 %collective-permute-start.6 = (f32[16,15,512]{2,1,0:T(8,128)S(1)}, f32[16,15,512]{2,1,0:T(8,128)S(1)}, u32[]{:S(2)}, u32[]{:S(2)}) collective-permute-start(f32[16,15,512]{2,1,0:T(8,128)S(1)} %get-tuple-element.25), channel_id=1, source_target_pairs={{0,4},{4,8},{8,12},{12,16},{16,20},{20,24},{24,28},{1,5},{5,9},{9,... | collective-permute-start | bytes 1474568 | tf_op jit(solution)/shard_map/ppermute | solution.py:19
  68.6 10.9 %collective-permute-start.7 = (f32[16,15,512]{2,1,0:T(8,128)S(1)}, f32[16,15,512]{2,1,0:T(8,128)S(1)}, u32[]{:S(2)}, u32[]{:S(2)}) collective-permute-start(f32[16,15,512]{2,1,0:T(8,128)S(1)} %get-tuple-element.26), channel_id=1, source_target_pairs={{4,0},{8,4},{12,8},{16,12},{20,16},{24,20},{28,24},{5,1},{9,5},{13... | collective-permute-start | bytes 1474568 | tf_op jit(solution)/shard_map/ppermute | solution.py:23
  80.5 8.6 %copy-start.1 = (f32[16,16,512]{2,1,0:T(8,128)}, f32[16,16,512]{2,1,0:T(8,128)S(1)}, u32[]{:S(2)}) copy-start(f32[16,16,512]{2,1,0:T(8,128)S(1)} %fusion.23) | copy-start | bytes 1572868
  81.2 4.3 %collective-permute-start.8 = (f32[16,1,256]{2,1,0:T(1,128)S(1)}, f32[16,1,256]{2,1,0:T(1,128)S(1)}, u32[]{:S(2)}, u32[]{:S(2)}) collective-permute-start(f32[16,1,256]{2,1,0:T(1,128)S(1)} %get-tuple-element.33), channel_id=1, source_target_pairs={{0,4},{4,8},{8,12},{12,16},{16,20},{20,24},{24,28},{1,5},{5,9},{9,... | collective-permute-start | bytes 49160 | tf_op jit(solution)/shard_map/ppermute | solution.py:19
  83.1 5.1 %collective-permute-start.9 = (f32[16,1,256]{2,1,0:T(1,128)S(1)}, f32[16,1,256]{2,1,0:T(1,128)S(1)}, u32[]{:S(2)}, u32[]{:S(2)}) collective-permute-start(f32[16,1,256]{2,1,0:T(1,128)S(1)} %get-tuple-element.34), channel_id=1, source_target_pairs={{4,0},{8,4},{12,8},{16,12},{20,16},{24,20},{28,24},{5,1},{9,5},{13... | collective-permute-start | bytes 49160 | tf_op jit(solution)/shard_map/ppermute | solution.py:23

commit v3 on v2

--- a/solution.py
+++ b/solution.py
@@ -98,7 +98,7 @@
         band(kernel_rows, rows_ext, row_count, 1, 0),
         band(kernel_planes, planes_ext, plane_count, 1, 0),
         band(kernel_planes, planes_ext, plane_count, -1, 2 * reach),
-        band(kernel_rows, rows_ext, row_count, -1, 2 * reach),
+        band(kernel_rows, rows_ext + 2, row_count + 2, -1, 2 * reach),
         pyramid_matrix(col_count, col_count // 2, 1),
         pyramid_matrix(row_count + 2, row_count // 2, 0),
     ))
@@ -115,12 +115,13 @@
     spread = halo(quotient, "slab", 0, reach, reach)
     spread = along_planes(spread, plane_back)
     spread = along_columns(spread, col_band, transpose=True)
-    spread = halo(spread, "tile", 1, reach, reach)
+    spread = halo(spread, "tile", 1, reach + 1, reach + 1)
     correction = along_rows(spread, row_back)
-    new_estimate = estimate * correction
+    edge_rows = lax.slice_in_dim(estimate_ext, reach - 1, reach + row_count + 1, axis=1)
+    new_ext = edge_rows * correction
+    new_estimate = lax.slice_in_dim(new_ext, 1, row_count + 1, axis=1)
 
-    halved = along_columns(new_estimate, pyr_cols)
-    halved = halo(halved, "tile", 1, 1, 1)
+    halved = along_columns(new_ext, pyr_cols)
     pyramid_level = along_rows(halved, pyr_rows)
     return (new_estimate, pyramid_level)
 

time: 89.6 us -> 84 us (0.938)
  the two profiles are of different devices: /device:TPU:1 before, /device:TPU:4 now
where the time goes in v3:
time: 84 us; the launch traced here: 83.7 us
  waiting for transfers between devices  44.1 us (52%)
  starting transfers between devices  24.2 us (29%)
  matrix products  10.5 us (12%)
  local copies, waits for them, and re-layouts  2.49 us (3%)
  other arithmetic  1.49 us (2%)
  between operations  0.93 us (1%)
    ppermute x4, waiting for transfers between devices, halo(): pieces_before.insert(0, lax.ppermute(piece, axis, up))  26.8 us
    ppermute x4, waiting for transfers between devices, halo(): pieces_after.append(lax.ppermute(piece, axis, down))  17.3 us
    ppermute x4, starting transfers between devices, halo(): pieces_after.append(lax.ppermute(piece, axis, down))  13.1 us
    ppermute x4, starting transfers between devices, halo(): pieces_before.insert(0, lax.ppermute(piece, axis, up))  11.1 us
    dot_general x3, matrix products, along_columns(): lax.dot_general(volume, matrix, (((2,), (contract,)), ((), ())), precisio...  4.84 us
    dot_general x2, matrix products, along_planes(): lax.dot_general(matrix.T, volume, (((1,), (0,)), ((), ())), precision=PRE...  2.9 us
    dot_general x3, matrix products, along_rows(): lax.dot_general(left, volume, (((2,), (1,)), ((0,), (0,))), precision=PRE...  2.79 us
  transfers between devices with their start and end apart: 8, of which 8 were waited for; matrix products, arithmetic and copies ran while one was open for 2% of the time, Pallas kernels for 0%

profile of v3, /device:TPU:4, one launch (start us, length us, event | category | flops | bytes accessed | tf_op | source)
XLA Modules:
  0.0 83.7 jit_solution(14823606013088273231)
XLA Ops:
  0.6 0.0 copy-start.2
  0.6 0.0 copy-start.3
  0.7 0.0 copy-start.4
  0.7 1.4 %fusion.60 = (f32[16,15,512]{2,1,0:T(8,128)S(1)}, f32[16,15,512]{2,1,0:T(8,128)S(1)}) fusion(f32[16,16,512]{2,1,0:T(8,128)} %param.5), kind=kLoop, calls=%fused_computation.80 | loop fusion | bytes 1966080 | tf_op jit(solution)/shard_map/slice | solution.py:18
  2.0 0.0 copy-start
  2.1 2.1 %collective-permute-start = (f32[16,15,512]{2,1,0:T(8,128)S(1)}, f32[16,15,512]{2,1,0:T(8,128)S(1)}, u32[]{:S(2)}, u32[]{:S(2)}) collective-permute-start(f32[16,15,512]{2,1,0:T(8,128)S(1)} %get-tuple-element.26), channel_id=1, source_target_pairs={{0,4},{4,8},{8,12},{12,16},{16,20},{20,24},{24,28},{1,5},{5,9},{9,... | collective-permute-start | bytes 1474568 | tf_op jit(solution)/shard_map/ppermute | solution.py:19
  4.1 4.5 %collective-permute-start.1 = (f32[16,15,512]{2,1,0:T(8,128)S(1)}, f32[16,15,512]{2,1,0:T(8,128)S(1)}, u32[]{:S(2)}, u32[]{:S(2)}) collective-permute-start(f32[16,15,512]{2,1,0:T(8,128)S(1)} %get-tuple-element.27), channel_id=1, source_target_pairs={{4,0},{8,4},{12,8},{16,12},{20,16},{24,20},{28,24},{5,1},{9,5},{13... | collective-permute-start | bytes 1474568 | tf_op jit(solution)/shard_map/ppermute | solution.py:23
  8.7 0.0 copy-done.2
  8.7 0.1 select_reduce_fusion.3
  8.9 0.0 copy-done.3
  8.9 0.2 select_reduce_fusion.5
  9.1 0.0 copy-done.4
  9.1 0.7 select_reduce_fusion.1
  9.8 0.1 maximum_maximum_fusion
  9.9 0.1 select_select_fusion.1
  9.9 0.1 select_select_fusion
  10.1 6.3 %collective-permute-done = f32[16,15,512]{2,1,0:T(8,128)S(1)} collective-permute-done((f32[16,15,512]{2,1,0:T(8,128)S(1)}, f32[16,15,512]{2,1,0:T(8,128)S(1)}, u32[]{:S(2)}, u32[]{:S(2)}) %collective-permute-start) | collective-permute-done | bytes 491552 | tf_op jit(solution)/shard_map/ppermute | solution.py:19
  16.4 0.9 %collective-permute-done.1 = f32[16,15,512]{2,1,0:T(8,128)S(1)} collective-permute-done((f32[16,15,512]{2,1,0:T(8,128)S(1)}, f32[16,15,512]{2,1,0:T(8,128)S(1)}, u32[]{:S(2)}, u32[]{:S(2)}) %collective-permute-start.1) | collective-permute-done | bytes 491552 | tf_op jit(solution)/shard_map/ppermute | solution.py:23
  17.3 0.0 copy-done
  17.3 2.7 %fusion = f32[16,46,512]{2,1,0:T(8,128)S(1)} fusion(f32[16,15,512]{2,1,0:T(8,128)S(1)} %collective-permute-done.1, f32[16,16,512]{2,1,0:T(8,128)S(1)} %copy-done, f32[16,15,512]{2,1,0:T(8,128)S(1)} %collective-permute-done, f32[512,512]{1,0:T(8,128)S(1)} %maximum_maximum_fusion), kind=kOutput, calls=%fused_computation.6 | convolution fusion | flops 2316009472 | bytes 4063232 | tf_op jit(solution)/shard_map/dot_general | solution.py:70
  20.0 0.9 %fusion.40 = f32[16,16,512]{2,1,0:T(8,128)S(1)} fusion(f32[16,46,512]{2,1,0:T(8,128)S(1)} %fusion, f32[16,46]{1,0:T(8,128)S(1)} %bitcast.21), kind=kOutput, calls=%fused_computation.52 | convolution fusion | flops 72351744 | bytes 2034560 | tf_op jit(solution)/shard_map/dot_general | solution.py:78
  20.9 0.1 fusion.59
  21.0 0.0 copy-start.1
  21.0 3.6 %collective-permute-start.2 = (f32[15,16,512]{2,1,0:T(8,128)S(1)}, f32[15,16,512]{2,1,0:T(8,128)S(1)}, u32[]{:S(2)}, u32[]{:S(2)}) collective-permute-start(f32[15,16,512]{2,1,0:T(8,128)S(1)} %get-tuple-element.24), channel_id=1, source_target_pairs={{0,1},{1,2},{2,3},{4,5},{5,6},{6,7},{8,9},{9,10},{10,11},{12,13},{... | collective-permute-start | bytes 1474568 | tf_op jit(solution)/shard_map/ppermute | solution.py:19
  24.7 1.3 %collective-permute-start.3 = (f32[15,16,512]{2,1,0:T(8,128)S(1)}, f32[15,16,512]{2,1,0:T(8,128)S(1)}, u32[]{:S(2)}, u32[]{:S(2)}) collective-permute-start(f32[15,16,512]{2,1,0:T(8,128)S(1)} %get-tuple-element.25), channel_id=1, source_target_pairs={{1,0},{2,1},{3,2},{5,4},{6,5},{7,6},{9,8},{10,9},{11,10},{13,12},{... | collective-permute-start | bytes 1474568 | tf_op jit(solution)/shard_map/ppermute | solution.py:23
  26.0 8.5 %collective-permute-done.2 = f32[15,16,512]{2,1,0:T(8,128)S(1)} collective-permute-done((f32[15,16,512]{2,1,0:T(8,128)S(1)}, f32[15,16,512]{2,1,0:T(8,128)S(1)}, u32[]{:S(2)}, u32[]{:S(2)}) %collective-permute-start.2) | collective-permute-done | bytes 491552 | tf_op jit(solution)/shard_map/ppermute | solution.py:19
  34.5 4.1 %collective-permute-done.3 = f32[15,16,512]{2,1,0:T(8,128)S(1)} collective-permute-done((f32[15,16,512]{2,1,0:T(8,128)S(1)}, f32[15,16,512]{2,1,0:T(8,128)S(1)}, u32[]{:S(2)}, u32[]{:S(2)}) %collective-permute-start.3) | collective-permute-done | bytes 491552 | tf_op jit(solution)/shard_map/ppermute | solution.py:23
  38.6 0.2 pad_maximum_fusion
  38.8 0.0 copy-done.1
  38.8 1.9 %fusion.20 = f32[16,16,512]{2,0,1:T(8,128)S(1)} fusion(f32[46,16,512]{2,1,0:T(8,128)S(1)} %pad_maximum_fusion, f32[16,16,512]{2,1,0:T(8,128)S(1)} %copy-done.1, f32[46,16]{0,1:T(8,128)S(1)} %get-tuple-element.11), kind=kOutput, calls=%fused_computation.27 | convolution fusion | flops 72482816 | bytes 2558848 | tf_op jit(solution)/shard_map/dot_general | solution.py:84
  40.8 0.1 fusion.58
  40.9 3.5 %collective-permute-start.4 = (f32[15,16,512]{2,0,1:T(8,128)S(1)}, f32[15,16,512]{2,0,1:T(8,128)S(1)}, u32[]{:S(2)}, u32[]{:S(2)}) collective-permute-start(f32[15,16,512]{2,0,1:T(8,128)S(1)} %get-tuple-element.22), channel_id=1, source_target_pairs={{0,1},{1,2},{2,3},{4,5},{5,6},{6,7},{8,9},{9,10},{10,11},{12,13},{... | collective-permute-start | bytes 1474568 | tf_op jit(solution)/shard_map/ppermute | solution.py:19
  44.3 1.3 %collective-permute-start.5 = (f32[15,16,512]{2,0,1:T(8,128)S(1)}, f32[15,16,512]{2,0,1:T(8,128)S(1)}, u32[]{:S(2)}, u32[]{:S(2)}) collective-permute-start(f32[15,16,512]{2,0,1:T(8,128)S(1)} %get-tuple-element.23), channel_id=1, source_target_pairs={{1,0},{2,1},{3,2},{5,4},{6,5},{7,6},{9,8},{10,9},{11,10},{13,12},{... | collective-permute-start | bytes 1474568 | tf_op jit(solution)/shard_map/ppermute | solution.py:23
  45.6 8.0 %collective-permute-done.4 = f32[15,16,512]{2,0,1:T(8,128)S(1)} collective-permute-done((f32[15,16,512]{2,0,1:T(8,128)S(1)}, f32[15,16,512]{2,0,1:T(8,128)S(1)}, u32[]{:S(2)}, u32[]{:S(2)}) %collective-permute-start.4) | collective-permute-done | bytes 491552 | tf_op jit(solution)/shard_map/ppermute | solution.py:19
  53.6 4.1 %collective-permute-done.5 = f32[15,16,512]{2,0,1:T(8,128)S(1)} collective-permute-done((f32[15,16,512]{2,0,1:T(8,128)S(1)}, f32[15,16,512]{2,0,1:T(8,128)S(1)}, u32[]{:S(2)}, u32[]{:S(2)}) %collective-permute-start.5) | collective-permute-done | bytes 491552 | tf_op jit(solution)/shard_map/ppermute | solution.py:23
  57.8 1.0 %fusion.6 = f32[16,16,512]{2,0,1:T(8,128)S(1)} fusion(f32[15,16,512]{2,0,1:T(8,128)S(1)} %collective-permute-done.5, f32[16,16,512]{2,0,1:T(8,128)S(1)} %fusion.20, f32[15,16,512]{2,0,1:T(8,128)S(1)} %collective-permute-done.4, f32[46,16]{0,1:T(8,128)S(1)} %get-tuple-element.10), kind=kOutput, calls=%fused_computation.12 | convolution fusion | flops 73105408 | bytes 2034560 | tf_op jit(solution)/shard_map/dot_general | solution.py:84
  58.8 1.3 %fusion.23 = f32[16,16,512]{2,1,0:T(8,128)S(1)} fusion(f32[512,512]{1,0:T(8,128)S(1)} %maximum_maximum_fusion, f32[16,16,512]{2,0,1:T(8,128)S(1)} %fusion.6), kind=kOutput, calls=%fused_computation.29 | convolution fusion | flops 805306368 | bytes 2097152 | tf_op jit(solution)/shard_map/dot_general | solution.py:70
  60.1 6.0 %collective-permute-start.7 = (f32[16,16,512]{2,1,0:T(8,128)S(1)}, f32[16,16,512]{2,1,0:T(8,128)S(1)}, u32[]{:S(2)}, u32[]{:S(2)}) collective-permute-start(f32[16,16,512]{2,1,0:T(8,128)S(1)} %fusion.23), channel_id=1, source_target_pairs={{4,0},{8,4},{12,8},{16,12},{20,16},{24,20},{28,24},{5,1},{9,5},{13... | collective-permute-start | bytes 1572872 | tf_op jit(solution)/shard_map/ppermute | solution.py:23
  66.1 1.9 %collective-permute-start.6 = (f32[16,16,512]{2,1,0:T(8,128)S(1)}, f32[16,16,512]{2,1,0:T(8,128)S(1)}, u32[]{:S(2)}, u32[]{:S(2)}) collective-permute-start(f32[16,16,512]{2,1,0:T(8,128)S(1)} %fusion.23), channel_id=1, source_target_pairs={{0,4},{4,8},{8,12},{12,16},{16,20},{20,24},{24,28},{1,5},{5,9},{9,... | collective-permute-start | bytes 1572872 | tf_op jit(solution)/shard_map/ppermute | solution.py:19
  68.0 8.0 %collective-permute-done.7 = f32[16,16,512]{2,1,0:T(8,128)S(1)} collective-permute-done((f32[16,16,512]{2,1,0:T(8,128)S(1)}, f32[16,16,512]{2,1,0:T(8,128)S(1)}, u32[]{:S(2)}, u32[]{:S(2)}) %collective-permute-start.7) | collective-permute-done | bytes 524320 | tf_op jit(solution)/shard_map/ppermute | solution.py:23
  76.1 4.0 %collective-permute-done.6 = f32[16,16,512]{2,1,0:T(8,128)S(1)} collective-permute-done((f32[16,16,512]{2,1,0:T(8,128)S(1)}, f32[16,16,512]{2,1,0:T(8,128)S(1)}, u32[]{:S(2)}, u32[]{:S(2)}) %collective-permute-start.6) | collective-permute-done | bytes 524320 | tf_op jit(solution)/shard_map/ppermute | solution.py:19
  80.1 1.0 %maximum_multiply_fusion = f32[16,18,512]{2,1,0:T(8,128)S(1)} fusion(f32[16,15,512]{2,1,0:T(8,128)S(1)} %collective-permute-done.1, f32[16,16,512]{2,1,0:T(8,128)S(1)} %copy-done, f32[16,15,512]{2,1,0:T(8,128)S(1)} %collective-permute-done, f32[16,16,512]{2,1,0:T(8,128)S(1)} %collective-permute-done.7, f32[16,16,512]{2,1,0:T(8,128)S(1)} %fusion.23, ...), kind=kOutput, calls=%fused_computation.32 | convolution fusion | flops 86163456 | bytes 3673472 | tf_op jit(solution)/shard_map/dot_general | solution.py:78
  81.1 0.9 %slice.36 = f32[16,16,512]{2,1,0:T(8,128)} slice(f32[16,18,512]{2,1,0:T(8,128)S(1)} %maximum_multiply_fusion), slice={[0:16], [1:17], [0:512]} | slice | bytes 1048576 | tf_op jit(solution)/shard_map/slice | solution.py:122
  81.9 0.8 fusion.26
  82.7 1.0 %fusion.45 = f32[16,8,256]{2,1,0:T(8,128)} fusion(f32[16,18,256]{2,1,0:T(8,128)S(1)} %fusion.26, f32[8,18]{1,0:T(8,128)S(1)} %bitcast.22), kind=kOutput, calls=%fused_computation.58 | convolution fusion | flops 7077888 | bytes 426560 | tf_op jit(solution)/shard_map/dot_general | solution.py:78
  (8 shorter events, 0.1 us)
Async XLA Ops:
  0.6 8.1 %copy-start.2 = (f32[31]{0:T(128)S(1)}, f32[31]{0:T(128)}, u32[]{:S(2)}) copy-start(f32[31]{0:T(128)} %param.7) | copy-start | bytes 376
  0.6 8.2 %copy-start.3 = (f32[31]{0:T(128)S(1)}, f32[31]{0:T(128)}, u32[]{:S(2)}) copy-start(f32[31]{0:T(128)} %param.9) | copy-start | bytes 376
  0.7 8.4 %copy-start.4 = (f32[31]{0:T(128)S(1)}, f32[31]{0:T(128)}, u32[]{:S(2)}) copy-start(f32[31]{0:T(128)} %param.8) | copy-start | bytes 376
  2.0 15.3 %copy-start = (f32[16,16,512]{2,1,0:T(8,128)S(1)}, f32[16,16,512]{2,1,0:T(8,128)}, u32[]{:S(2)}) copy-start(f32[16,16,512]{2,1,0:T(8,128)} %param.5) | copy-start | bytes 1572868
  2.1 14.3 %collective-permute-start = (f32[16,15,512]{2,1,0:T(8,128)S(1)}, f32[16,15,512]{2,1,0:T(8,128)S(1)}, u32[]{:S(2)}, u32[]{:S(2)}) collective-permute-start(f32[16,15,512]{2,1,0:T(8,128)S(1)} %get-tuple-element.26), channel_id=1, source_target_pairs={{0,4},{4,8},{8,12},{12,16},{16,20},{20,24},{24,28},{1,5},{5,9},{9,... | collective-permute-start | bytes 1474568 | tf_op jit(solution)/shard_map/ppermute | solution.py:19
  4.1 13.2 %collective-permute-start.1 = (f32[16,15,512]{2,1,0:T(8,128)S(1)}, f32[16,15,512]{2,1,0:T(8,128)S(1)}, u32[]{:S(2)}, u32[]{:S(2)}) collective-permute-start(f32[16,15,512]{2,1,0:T(8,128)S(1)} %get-tuple-element.27), channel_id=1, source_target_pairs={{4,0},{8,4},{12,8},{16,12},{20,16},{24,20},{28,24},{5,1},{9,5},{13... | collective-permute-start | bytes 1474568 | tf_op jit(solution)/shard_map/ppermute | solution.py:23
  21.0 17.8 %copy-start.1 = (f32[16,16,512]{2,1,0:T(8,128)S(1)}, f32[16,16,512]{2,1,0:T(8,128)}, u32[]{:S(2)}) copy-start(f32[16,16,512]{2,1,0:T(8,128)} %param.6) | copy-start | bytes 1572868
  21.0 13.4 %collective-permute-start.2 = (f32[15,16,512]{2,1,0:T(8,128)S(1)}, f32[15,16,512]{2,1,0:T(8,128)S(1)}, u32[]{:S(2)}, u32[]{:S(2)}) collective-permute-start(f32[15,16,512]{2,1,0:T(8,128)S(1)} %get-tuple-element.24), channel_id=1, source_target_pairs={{0,1},{1,2},{2,3},{4,5},{5,6},{6,7},{8,9},{9,10},{10,11},{12,13},{... | collective-permute-start | bytes 1474568 | tf_op jit(solution)/shard_map/ppermute | solution.py:19
  24.7 13.9 %collective-permute-start.3 = (f32[15,16,512]{2,1,0:T(8,128)S(1)}, f32[15,16,512]{2,1,0:T(8,128)S(1)}, u32[]{:S(2)}, u32[]{:S(2)}) collective-permute-start(f32[15,16,512]{2,1,0:T(8,128)S(1)} %get-tuple-element.25), channel_id=1, source_target_pairs={{1,0},{2,1},{3,2},{5,4},{6,5},{7,6},{9,8},{10,9},{11,10},{13,12},{... | collective-permute-start | bytes 1474568 | tf_op jit(solution)/shard_map/ppermute | solution.py:23
  40.9 12.8 %collective-permute-start.4 = (f32[15,16,512]{2,0,1:T(8,128)S(1)}, f32[15,16,512]{2,0,1:T(8,128)S(1)}, u32[]{:S(2)}, u32[]{:S(2)}) collective-permute-start(f32[15,16,512]{2,0,1:T(8,128)S(1)} %get-tuple-element.22), channel_id=1, source_target_pairs={{0,1},{1,2},{2,3},{4,5},{5,6},{6,7},{8,9},{9,10},{10,11},{12,13},{... | collective-permute-start | bytes 1474568 | tf_op jit(solution)/shard_map/ppermute | solution.py:19
  44.3 13.4 %collective-permute-start.5 = (f32[15,16,512]{2,0,1:T(8,128)S(1)}, f32[15,16,512]{2,0,1:T(8,128)S(1)}, u32[]{:S(2)}, u32[]{:S(2)}) collective-permute-start(f32[15,16,512]{2,0,1:T(8,128)S(1)} %get-tuple-element.23), channel_id=1, source_target_pairs={{1,0},{2,1},{3,2},{5,4},{6,5},{7,6},{9,8},{10,9},{11,10},{13,12},{... | collective-permute-start | bytes 1474568 | tf_op jit(solution)/shard_map/ppermute | solution.py:23
  60.1 16.0 %collective-permute-start.7 = (f32[16,16,512]{2,1,0:T(8,128)S(1)}, f32[16,16,512]{2,1,0:T(8,128)S(1)}, u32[]{:S(2)}, u32[]{:S(2)}) collective-permute-start(f32[16,16,512]{2,1,0:T(8,128)S(1)} %fusion.23), channel_id=1, source_target_pairs={{4,0},{8,4},{12,8},{16,12},{20,16},{24,20},{28,24},{5,1},{9,5},{13... | collective-permute-start | bytes 1572872 | tf_op jit(solution)/shard_map/ppermute | solution.py:23
  66.1 14.0 %collective-permute-start.6 = (f32[16,16,512]{2,1,0:T(8,128)S(1)}, f32[16,16,512]{2,1,0:T(8,128)S(1)}, u32[]{:S(2)}, u32[]{:S(2)}) collective-permute-start(f32[16,16,512]{2,1,0:T(8,128)S(1)} %fusion.23), channel_id=1, source_target_pairs={{0,4},{4,8},{8,12},{12,16},{16,20},{20,24},{24,28},{1,5},{5,9},{9,... | collective-permute-start | bytes 1572872 | tf_op jit(solution)/shard_map/ppermute | solution.py:19

commit v4 on v3

--- a/solution.py
+++ b/solution.py
@@ -4,6 +4,7 @@
 from jax.sharding import PartitionSpec as P
 
 PRECISE = lax.Precision.HIGHEST
+CHUNKS = 2
 
 
 def halo(shard, axis, dim, before_width, after_width):
@@ -104,20 +105,20 @@
     ))
     col_band, row_fwd, plane_fwd, plane_back, row_back, pyr_cols, pyr_rows = bands
 
-    estimate_ext = halo(estimate, "tile", 1, reach, reach)
-    blurred = along_columns(estimate_ext, col_band)
-    blurred = along_rows(blurred, row_fwd)
-    blurred = halo(blurred, "slab", 0, reach, reach)
-    blurred = along_planes(blurred, plane_fwd)
-
-    quotient = observed / blurred
-
-    spread = halo(quotient, "slab", 0, reach, reach)
-    spread = along_planes(spread, plane_back)
-    spread = along_columns(spread, col_band, transpose=True)
-    spread = halo(spread, "tile", 1, reach + 1, reach + 1)
-    correction = along_rows(spread, row_back)
-    edge_rows = lax.slice_in_dim(estimate_ext, reach - 1, reach + row_count + 1, axis=1)
+    filtered = along_columns(estimate, col_band)
+    chunk = col_count // CHUNKS
+    spreads = []
+    for index in range(CHUNKS):
+        part = lax.slice_in_dim(filtered, index * chunk, (index + 1) * chunk, axis=2)
+        seen = lax.slice_in_dim(observed, index * chunk, (index + 1) * chunk, axis=2)
+        blurred = along_planes(halo(part, "slab", 0, reach, reach), plane_fwd)
+        blurred = along_rows(halo(blurred, "tile", 1, reach, reach), row_fwd)
+        quotient = seen / blurred
+        spread = along_planes(halo(quotient, "slab", 0, reach, reach), plane_back)
+        spread = along_rows(halo(spread, "tile", 1, reach + 1, reach + 1), row_back)
+        spreads.append(spread)
+    correction = along_columns(jnp.concatenate(spreads, axis=2), col_band, transpose=True)
+    edge_rows = halo(estimate, "tile", 1, 1, 1)
     new_ext = edge_rows * correction
     new_estimate = lax.slice_in_dim(new_ext, 1, row_count + 1, axis=1)
 

time: 84 us -> 77.4 us (0.921)
  the two profiles are of different devices: /device:TPU:4 before, /device:TPU:11 now
where the time goes in v4:
time: 77.4 us; the launch traced here: 76 us
  starting transfers between devices  53.5 us (69%)
  matrix products  11.6 us (15%)
  waiting for transfers between devices  4.61 us (6%)
  other arithmetic  3.76 us (5%)
  local copies, waits for them, and re-layouts  1.31 us (2%)
  between operations  1.17 us (2%)
    ppermute x9, starting transfers between devices, halo(): pieces_before.insert(0, lax.ppermute(piece, axis, up))  35.7 us
    ppermute x9, starting transfers between devices, halo(): pieces_after.append(lax.ppermute(piece, axis, down))  17.8 us
    dot_general x5, matrix products, along_rows(): lax.dot_general(left, volume, (((2,), (1,)), ((0,), (0,))), precision=PRE...  4.64 us
    ppermute x9, waiting for transfers between devices, halo(): pieces_after.append(lax.ppermute(piece, axis, down))  4.1 us
    dot_general x4, matrix products, along_planes(): lax.dot_general(matrix.T, volume, (((1,), (0,)), ((), ())), precision=PRE...  3.61 us
    dot_general x3, matrix products, along_columns(): lax.dot_general(volume, matrix, (((2,), (contract,)), ((), ())), precisio...  3.38 us
    reduce_sum x3, other arithmetic, band(): return jnp.sum(picked, axis=2)  3.01 us
  transfers between devices with their start and end apart: 18, of which 5 were waited for; matrix products, arithmetic and copies ran while one was open for 11% of the time, Pallas kernels for 0%

profile of v4, /device:TPU:11, one launch (start us, length us, event | category | flops | bytes accessed | tf_op | source)
XLA Modules:
  0.0 76.0 jit_solution(14630832419657585480)
XLA Ops:
  0.7 0.1 select_select_fusion.1
  0.8 0.1 select_select_fusion
  0.9 0.8 %select_reduce_fusion.3 = f32[48,18]{0,1:T(8,128)S(1)} fusion(f32[31]{0:T(128)} %param.7, s32[48,18]{0,1:T(8,128)S(1)} %multiply_add_fusion), kind=kLoop, calls=%fused_computation.49 | loop fusion | flops 79488 | bytes 7036 | tf_op jit(solution)/shard_map/reduce_sum | solution.py:36
  1.7 0.0 copy-start
  1.7 0.9 %select_reduce_fusion.5 = (f32[46,16]{0,1:T(8,128)S(1)}, f32[46,16]{0,1:T(8,128)S(1)}, f32[46,16]{0,1:T(8,128)S(1)}) fusion(f32[31]{0:T(128)} %param.9, s32[46,16]{0,1:T(8,128)S(1)} %get-tuple-element.41, f32[31]{0:T(128)} %param.7, s32[46,16]{0,1:T(8,128)S(1)} %get-tuple-element.40), kind=kLoop, calls=%fused_computation.53 | loop fusion | flops 180320 | bytes 14968 | tf_op jit(solution)/shard_map/reduce_sum | solution.py:36
  2.6 1.3 %select_reduce_fusion.1 = (f32[128,128]{1,0:T(8,128)S(1)}, f32[128,128]{1,0:T(8,128)S(1)}, f32[128,128]{1,0:T(8,128)S(1)}) fusion(s32[128,128]{1,0:T(8,128)S(1)} %get-tuple-element.39, f32[31]{0:T(128)} %param.8, s32[128,128]{1,0:T(8,128)S(1)} %get-tuple-element.38, s32[128,128]{1,0:T(8,128)S(1)} %fusion.38), kind=kLoop, calls=%fused_computation.2 | loop fusion | flops 4521984 | bytes 393340 | tf_op jit(solution)/shard_map/reduce_sum | solution.py:36
  4.0 0.1 maximum_maximum_fusion
  4.1 1.1 %convolution_bitcast_fusion = f32[16,16,512]{2,1,0:T(8,128)S(1)} fusion(f32[16,16,512]{2,1,0:T(8,128)S(1)} %copy-done, f32[512,512]{1,0:T(8,128)S(1)} %maximum_maximum_fusion), kind=kOutput, calls=%fused_computation.6 | convolution fusion | flops 805306368 | bytes 2097152 | tf_op jit(solution)/shard_map/dot_general | solution.py:71
  5.2 0.1 fusion.52
  5.3 3.2 %collective-permute-start.2 = (f32[15,16,256]{2,1,0:T(8,128)S(1)}, f32[15,16,256]{2,1,0:T(8,128)S(1)}, u32[]{:S(2)}, u32[]{:S(2)}) collective-permute-start(f32[15,16,256]{2,1,0:T(8,128)S(1)} %get-tuple-element.22), channel_id=1, source_target_pairs={{0,1},{1,2},{2,3},{4,5},{5,6},{6,7},{8,9},{9,10},{10,11},{12,13},{... | collective-permute-start | bytes 737288 | tf_op jit(solution)/shard_map/ppermute | solution.py:20
  8.5 2.1 %collective-permute-start.3 = (f32[15,16,256]{2,1,0:T(8,128)S(1)}, f32[15,16,256]{2,1,0:T(8,128)S(1)}, u32[]{:S(2)}, u32[]{:S(2)}) collective-permute-start(f32[15,16,256]{2,1,0:T(8,128)S(1)} %get-tuple-element.25), channel_id=1, source_target_pairs={{1,0},{2,1},{3,2},{5,4},{6,5},{7,6},{9,8},{10,9},{11,10},{13,12},{... | collective-permute-start | bytes 737288 | tf_op jit(solution)/shard_map/ppermute | solution.py:24
  10.6 0.1 fusion.54
  10.7 4.2 %collective-permute-start = (f32[16,1,512]{2,1,0:T(1,128)S(1)}, f32[16,1,512]{2,1,0:T(1,128)S(1)}, u32[]{:S(2)}, u32[]{:S(2)}) collective-permute-start(f32[16,1,512]{2,1,0:T(1,128)S(1)} %get-tuple-element.28), channel_id=1, source_target_pairs={{0,4},{4,8},{8,12},{12,16},{16,20},{20,24},{24,28},{1,5},{5,9},{9,... | collective-permute-start | bytes 98312 | tf_op jit(solution)/shard_map/ppermute | solution.py:20
  14.9 1.9 %collective-permute-start.1 = (f32[16,1,512]{2,1,0:T(1,128)S(1)}, f32[16,1,512]{2,1,0:T(1,128)S(1)}, u32[]{:S(2)}, u32[]{:S(2)}) collective-permute-start(f32[16,1,512]{2,1,0:T(1,128)S(1)} %get-tuple-element.29), channel_id=1, source_target_pairs={{4,0},{8,4},{12,8},{16,12},{20,16},{24,20},{28,24},{5,1},{9,5},{13... | collective-permute-start | bytes 98312 | tf_op jit(solution)/shard_map/ppermute | solution.py:24
  16.9 1.9 %collective-permute-start.11 = (f32[15,16,256]{2,1,0:T(8,128)S(1)}, f32[15,16,256]{2,1,0:T(8,128)S(1)}, u32[]{:S(2)}, u32[]{:S(2)}) collective-permute-start(f32[15,16,256]{2,1,0:T(8,128)S(1)} %get-tuple-element.23), channel_id=1, source_target_pairs={{1,0},{2,1},{3,2},{5,4},{6,5},{7,6},{9,8},{10,9},{11,10},{13,12},{... | collective-permute-start | bytes 737288 | tf_op jit(solution)/shard_map/ppermute | solution.py:24
  18.8 0.1 fusion.53
  18.9 0.0 collective-permute-done.2
  18.9 3.4 %collective-permute-start.10 = (f32[15,16,256]{2,1,0:T(8,128)S(1)}, f32[15,16,256]{2,1,0:T(8,128)S(1)}, u32[]{:S(2)}, u32[]{:S(2)}) collective-permute-start(f32[15,16,256]{2,1,0:T(8,128)S(1)} %get-tuple-element.24), channel_id=1, source_target_pairs={{0,1},{1,2},{2,3},{4,5},{5,6},{6,7},{8,9},{9,10},{10,11},{12,13},{... | collective-permute-start | bytes 737288 | tf_op jit(solution)/shard_map/ppermute | solution.py:20
  22.3 0.1 pad_maximum_fusion.2
  22.3 0.9 %fusion.22 = f32[16,16,256]{2,0,1:T(8,128)S(1)} fusion(f32[46,16,256]{2,1,0:T(8,128)S(1)} %pad_maximum_fusion.2, f32[46,16]{0,1:T(8,128)S(1)} %get-tuple-element.12), kind=kOutput, calls=%fused_computation.31 | convolution fusion | flops 36175872 | bytes 1018752 | tf_op jit(solution)/shard_map/dot_general | solution.py:85
  23.3 5.1 %collective-permute-start.4 = (f32[16,15,256]{2,0,1:T(8,128)S(1)}, f32[16,15,256]{2,0,1:T(8,128)S(1)}, u32[]{:S(2)}, u32[]{:S(2)}) collective-permute-start(f32[16,15,256]{2,0,1:T(8,128)S(1)} %get-tuple-element.32), channel_id=1, source_target_pairs={{0,4},{4,8},{8,12},{12,16},{16,20},{20,24},{24,28},{1,5},{5,9},{9,... | collective-permute-start | bytes 737288 | tf_op jit(solution)/shard_map/ppermute | solution.py:20
  28.4 1.9 %collective-permute-start.5 = (f32[16,15,256]{2,0,1:T(8,128)S(1)}, f32[16,15,256]{2,0,1:T(8,128)S(1)}, u32[]{:S(2)}, u32[]{:S(2)}) collective-permute-start(f32[16,15,256]{2,0,1:T(8,128)S(1)} %get-tuple-element.33), channel_id=1, source_target_pairs={{4,0},{8,4},{12,8},{16,12},{20,16},{24,20},{28,24},{5,1},{9,5},{13... | collective-permute-start | bytes 737288 | tf_op jit(solution)/shard_map/ppermute | solution.py:24
  30.3 0.0 collective-permute-done.10
  30.3 0.1 pad_maximum_fusion.5
  30.4 0.9 %fusion.17 = f32[16,16,256]{2,0,1:T(8,128)S(1)} fusion(f32[46,16,256]{2,1,0:T(8,128)S(1)} %pad_maximum_fusion.5, f32[46,16]{0,1:T(8,128)S(1)} %get-tuple-element.12), kind=kOutput, calls=%fused_computation.26 | convolution fusion | flops 36175872 | bytes 1018752 | tf_op jit(solution)/shard_map/dot_general | solution.py:85
  31.3 0.0 copy-start.1
  31.3 0.1 fusion.58
  31.4 4.7 %collective-permute-start.12 = (f32[16,15,256]{2,0,1:T(8,128)S(1)}, f32[16,15,256]{2,0,1:T(8,128)S(1)}, u32[]{:S(2)}, u32[]{:S(2)}) collective-permute-start(f32[16,15,256]{2,0,1:T(8,128)S(1)} %get-tuple-element.36), channel_id=1, source_target_pairs={{0,4},{4,8},{8,12},{12,16},{16,20},{20,24},{24,28},{1,5},{5,9},{9,... | collective-permute-start | bytes 737288 | tf_op jit(solution)/shard_map/ppermute | solution.py:20
  36.1 1.9 %collective-permute-start.13 = (f32[16,15,256]{2,0,1:T(8,128)S(1)}, f32[16,15,256]{2,0,1:T(8,128)S(1)}, u32[]{:S(2)}, u32[]{:S(2)}) collective-permute-start(f32[16,15,256]{2,0,1:T(8,128)S(1)} %get-tuple-element.37), channel_id=1, source_target_pairs={{4,0},{8,4},{12,8},{16,12},{20,16},{24,20},{28,24},{5,1},{9,5},{13... | collective-permute-start | bytes 737288 | tf_op jit(solution)/shard_map/ppermute | solution.py:24
  38.0 0.0 collective-permute-done.5
  38.0 0.1 pad_maximum_fusion.3
  38.1 0.9 %convolution_divide_fusion.1 = f32[16,16,256]{2,1,0:T(8,128)S(1)} fusion(f32[16,46,256]{2,0,1:T(8,128)S(1)} %pad_maximum_fusion.3, f32[16,16,512]{2,1,0:T(8,128)S(1)} %copy-done.1, f32[16,46]{1,0:T(8,128)S(1)} %bitcast.30), kind=kOutput, calls=%fused_computation.8 | convolution fusion | flops 36241408 | bytes 1280896 | tf_op jit(solution)/shard_map/dot_general | solution.py:79
  39.0 3.2 %collective-permute-start.6 = (f32[15,16,256]{2,1,0:T(8,128)S(1)}, f32[15,16,256]{2,1,0:T(8,128)S(1)}, u32[]{:S(2)}, u32[]{:S(2)}) collective-permute-start(f32[15,16,256]{2,1,0:T(8,128)S(1)} %get-tuple-element.30), channel_id=1, source_target_pairs={{0,1},{1,2},{2,3},{4,5},{5,6},{6,7},{8,9},{9,10},{10,11},{12,13},{... | collective-permute-start | bytes 737288 | tf_op jit(solution)/shard_map/ppermute | solution.py:20
  42.3 0.0 collective-permute-done.12
  42.3 2.1 %collective-permute-start.7 = (f32[15,16,256]{2,1,0:T(8,128)S(1)}, f32[15,16,256]{2,1,0:T(8,128)S(1)}, u32[]{:S(2)}, u32[]{:S(2)}) collective-permute-start(f32[15,16,256]{2,1,0:T(8,128)S(1)} %get-tuple-element.31), channel_id=1, source_target_pairs={{1,0},{2,1},{3,2},{5,4},{6,5},{7,6},{9,8},{10,9},{11,10},{13,12},{... | collective-permute-start | bytes 737288 | tf_op jit(solution)/shard_map/ppermute | solution.py:24
  44.4 0.1 collective-permute-done.13
  44.5 0.1 pad_maximum_fusion.6
  44.5 0.9 %convolution_divide_fusion = f32[16,16,256]{2,1,0:T(8,128)S(1)} fusion(f32[16,46,256]{2,0,1:T(8,128)S(1)} %pad_maximum_fusion.6, f32[16,16,512]{2,1,0:T(8,128)S(1)} %copy-done.1, f32[16,46]{1,0:T(8,128)S(1)} %bitcast.31), kind=kOutput, calls=%fused_computation.7 | convolution fusion | flops 36241408 | bytes 1280896 | tf_op jit(solution)/shard_map/dot_general | solution.py:79
  45.5 0.1 fusion.57
  45.5 3.2 %collective-permute-start.14 = (f32[15,16,256]{2,1,0:T(8,128)S(1)}, f32[15,16,256]{2,1,0:T(8,128)S(1)}, u32[]{:S(2)}, u32[]{:S(2)}) collective-permute-start(f32[15,16,256]{2,1,0:T(8,128)S(1)} %get-tuple-element.34), channel_id=1, source_target_pairs={{0,1},{1,2},{2,3},{4,5},{5,6},{6,7},{8,9},{9,10},{10,11},{12,13},{... | collective-permute-start | bytes 737288 | tf_op jit(solution)/shard_map/ppermute | solution.py:20
  48.7 0.0 collective-permute-done.6
  48.7 2.1 %collective-permute-start.15 = (f32[15,16,256]{2,1,0:T(8,128)S(1)}, f32[15,16,256]{2,1,0:T(8,128)S(1)}, u32[]{:S(2)}, u32[]{:S(2)}) collective-permute-start(f32[15,16,256]{2,1,0:T(8,128)S(1)} %get-tuple-element.35), channel_id=1, source_target_pairs={{1,0},{2,1},{3,2},{5,4},{6,5},{7,6},{9,8},{10,9},{11,10},{13,12},{... | collective-permute-start | bytes 737288 | tf_op jit(solution)/shard_map/ppermute | solution.py:24
  50.8 0.9 %collective-permute-done.7 = f32[15,16,256]{2,1,0:T(8,128)S(1)} collective-permute-done((f32[15,16,256]{2,1,0:T(8,128)S(1)}, f32[15,16,256]{2,1,0:T(8,128)S(1)}, u32[]{:S(2)}, u32[]{:S(2)}) %collective-permute-start.7) | collective-permute-done | bytes 245792 | tf_op jit(solution)/shard_map/ppermute | solution.py:24
  51.7 0.1 pad_maximum_fusion.4
  51.8 0.9 %fusion.19 = f32[16,16,256]{2,0,1:T(8,128)S(1)} fusion(f32[46,16,256]{2,1,0:T(8,128)S(1)} %pad_maximum_fusion.4, f32[46,16]{0,1:T(8,128)S(1)} %get-tuple-element.10), kind=kOutput, calls=%fused_computation.28 | convolution fusion | flops 36175872 | bytes 1018752 | tf_op jit(solution)/shard_map/dot_general | solution.py:85
  52.7 2.0 %collective-permute-start.9 = (f32[16,16,256]{2,0,1:T(8,128)S(1)}, f32[16,16,256]{2,0,1:T(8,128)S(1)}, u32[]{:S(2)}, u32[]{:S(2)}) collective-permute-start(f32[16,16,256]{2,0,1:T(8,128)S(1)} %fusion.19), channel_id=1, source_target_pairs={{4,0},{8,4},{12,8},{16,12},{20,16},{24,20},{28,24},{5,1},{9,5},{13... | collective-permute-start | bytes 786440 | tf_op jit(solution)/shard_map/ppermute | solution.py:24
  54.7 0.5 collective-permute-done.14
  55.1 4.2 %collective-permute-start.8 = (f32[16,16,256]{2,0,1:T(8,128)S(1)}, f32[16,16,256]{2,0,1:T(8,128)S(1)}, u32[]{:S(2)}, u32[]{:S(2)}) collective-permute-start(f32[16,16,256]{2,0,1:T(8,128)S(1)} %fusion.19), channel_id=1, source_target_pairs={{0,4},{4,8},{8,12},{12,16},{16,20},{20,24},{24,28},{1,5},{5,9},{9,... | collective-permute-start | bytes 786440 | tf_op jit(solution)/shard_map/ppermute | solution.py:20
  59.3 0.1 pad_maximum_fusion.7
  59.4 0.9 %fusion.14 = f32[16,16,256]{2,0,1:T(8,128)S(1)} fusion(f32[46,16,256]{2,1,0:T(8,128)S(1)} %pad_maximum_fusion.7, f32[46,16]{0,1:T(8,128)S(1)} %get-tuple-element.10), kind=kOutput, calls=%fused_computation.23 | convolution fusion | flops 36175872 | bytes 1018752 | tf_op jit(solution)/shard_map/dot_general | solution.py:85
  60.3 1.9 %collective-permute-start.17 = (f32[16,16,256]{2,0,1:T(8,128)S(1)}, f32[16,16,256]{2,0,1:T(8,128)S(1)}, u32[]{:S(2)}, u32[]{:S(2)}) collective-permute-start(f32[16,16,256]{2,0,1:T(8,128)S(1)} %fusion.14), channel_id=1, source_target_pairs={{4,0},{8,4},{12,8},{16,12},{20,16},{24,20},{28,24},{5,1},{9,5},{13... | collective-permute-start | bytes 786440 | tf_op jit(solution)/shard_map/ppermute | solution.py:24
  62.2 0.2 collective-permute-done.9
  62.4 4.5 %collective-permute-start.16 = (f32[16,16,256]{2,0,1:T(8,128)S(1)}, f32[16,16,256]{2,0,1:T(8,128)S(1)}, u32[]{:S(2)}, u32[]{:S(2)}) collective-permute-start(f32[16,16,256]{2,0,1:T(8,128)S(1)} %fusion.14), channel_id=1, source_target_pairs={{0,4},{4,8},{8,12},{12,16},{16,20},{20,24},{24,28},{1,5},{5,9},{9,... | collective-permute-start | bytes 786440 | tf_op jit(solution)/shard_map/ppermute | solution.py:20
  67.0 0.0 collective-permute-done.8
  67.0 0.1 pad_maximum_fusion
  67.0 0.9 %fusion.12 = f32[16,18,256]{2,1,0:T(8,128)S(1)} fusion(f32[16,48,256]{2,0,1:T(8,128)S(1)} %pad_maximum_fusion, f32[18,48]{1,0:T(8,128)S(1)} %bitcast.28), kind=kOutput, calls=%fused_computation.21 | convolution fusion | flops 42467328 | bytes 1084800 | tf_op jit(solution)/shard_map/dot_general | solution.py:79
  68.0 2.9 %collective-permute-done.17 = f32[16,16,256]{2,0,1:T(8,128)S(1)} collective-permute-done((f32[16,16,256]{2,0,1:T(8,128)S(1)}, f32[16,16,256]{2,0,1:T(8,128)S(1)}, u32[]{:S(2)}, u32[]{:S(2)}) %collective-permute-start.17) | collective-permute-done | bytes 262176 | tf_op jit(solution)/shard_map/ppermute | solution.py:24
  70.9 0.1 pad_maximum_fusion.1
  70.9 0.9 %fusion.10 = f32[16,18,256]{2,1,0:T(8,128)S(1)} fusion(f32[16,48,256]{2,0,1:T(8,128)S(1)} %pad_maximum_fusion.1, f32[18,48]{1,0:T(8,128)S(1)} %bitcast.29), kind=kOutput, calls=%fused_computation.19 | convolution fusion | flops 42467328 | bytes 1084800 | tf_op jit(solution)/shard_map/dot_general | solution.py:79
  71.9 0.0 collective-permute-done.1
  71.9 1.5 %maximum_multiply_fusion = f32[16,18,512]{2,1,0:T(8,128)S(1)} fusion(f32[16,1,512]{2,1,0:T(1,128)S(1)} %collective-permute-done.1, f32[16,16,512]{2,1,0:T(8,128)S(1)} %copy-done, f32[16,1,512]{2,1,0:T(1,128)S(1)} %collective-permute-done, f32[512,512]{1,0:T(8,128)S(1)} %maximum_maximum_fusion, f32[16,18,256]{2,1,0:T(8,128)S(1)} %fusion.10, ...), kind=kOutput, calls=%fused_computation.13 | convolution fusion | flops 906559488 | bytes 2818048 | tf_op jit(solution)/shard_map/dot_general | solution.py:71
  73.4 0.9 %slice.94 = f32[16,16,512]{2,1,0:T(8,128)} slice(f32[16,18,512]{2,1,0:T(8,128)S(1)} %maximum_multiply_fusion), slice={[0:16], [1:17], [0:512]} | slice | bytes 1048576 | tf_op jit(solution)/shard_map/slice | solution.py:123
  74.2 0.8 %fusion.24 = f32[16,18,256]{2,1,0:T(8,128)S(1)} fusion(f32[16,18,512]{2,1,0:T(8,128)S(1)} %maximum_multiply_fusion, f32[512,256]{1,0:T(8,128)S(1)} %select_select_fusion), kind=kOutput, calls=%fused_computation.39 | convolution fusion | flops 452984832 | bytes 1409024 | tf_op jit(solution)/shard_map/dot_general | solution.py:71
  75.0 1.0 %fusion.39 = f32[16,8,256]{2,1,0:T(8,128)} fusion(f32[16,18,256]{2,1,0:T(8,128)S(1)} %fusion.24, f32[8,18]{1,0:T(8,128)S(1)} %bitcast.32), kind=kOutput, calls=%fused_computation.64 | convolution fusion | flops 7077888 | bytes 426560 | tf_op jit(solution)/shard_map/dot_general | solution.py:79
  (18 shorter events, 0.2 us)
Async XLA Ops:
  1.7 2.4 %copy-start = (f32[16,16,512]{2,1,0:T(8,128)S(1)}, f32[16,16,512]{2,1,0:T(8,128)}, u32[]{:S(2)}) copy-start(f32[16,16,512]{2,1,0:T(8,128)} %param.5) | copy-start | bytes 1572868
  5.3 13.5 %collective-permute-start.2 = (f32[15,16,256]{2,1,0:T(8,128)S(1)}, f32[15,16,256]{2,1,0:T(8,128)S(1)}, u32[]{:S(2)}, u32[]{:S(2)}) collective-permute-start(f32[15,16,256]{2,1,0:T(8,128)S(1)} %get-tuple-element.22), channel_id=1, source_target_pairs={{0,1},{1,2},{2,3},{4,5},{5,6},{6,7},{8,9},{9,10},{10,11},{12,13},{... | collective-permute-start | bytes 737288 | tf_op jit(solution)/shard_map/ppermute | solution.py:20
  8.5 13.7 %collective-permute-start.3 = (f32[15,16,256]{2,1,0:T(8,128)S(1)}, f32[15,16,256]{2,1,0:T(8,128)S(1)}, u32[]{:S(2)}, u32[]{:S(2)}) collective-permute-start(f32[15,16,256]{2,1,0:T(8,128)S(1)} %get-tuple-element.25), channel_id=1, source_target_pairs={{1,0},{2,1},{3,2},{5,4},{6,5},{7,6},{9,8},{10,9},{11,10},{13,12},{... | collective-permute-start | bytes 737288 | tf_op jit(solution)/shard_map/ppermute | solution.py:24
  10.7 61.2 %collective-permute-start = (f32[16,1,512]{2,1,0:T(1,128)S(1)}, f32[16,1,512]{2,1,0:T(1,128)S(1)}, u32[]{:S(2)}, u32[]{:S(2)}) collective-permute-start(f32[16,1,512]{2,1,0:T(1,128)S(1)} %get-tuple-element.28), channel_id=1, source_target_pairs={{0,4},{4,8},{8,12},{12,16},{16,20},{20,24},{24,28},{1,5},{5,9},{9,... | collective-permute-start | bytes 98312 | tf_op jit(solution)/shard_map/ppermute | solution.py:20
  14.9 56.9 %collective-permute-start.1 = (f32[16,1,512]{2,1,0:T(1,128)S(1)}, f32[16,1,512]{2,1,0:T(1,128)S(1)}, u32[]{:S(2)}, u32[]{:S(2)}) collective-permute-start(f32[16,1,512]{2,1,0:T(1,128)S(1)} %get-tuple-element.29), channel_id=1, source_target_pairs={{4,0},{8,4},{12,8},{16,12},{20,16},{24,20},{28,24},{5,1},{9,5},{13... | collective-permute-start | bytes 98312 | tf_op jit(solution)/shard_map/ppermute | solution.py:24
  16.9 11.5 %collective-permute-start.11 = (f32[15,16,256]{2,1,0:T(8,128)S(1)}, f32[15,16,256]{2,1,0:T(8,128)S(1)}, u32[]{:S(2)}, u32[]{:S(2)}) collective-permute-start(f32[15,16,256]{2,1,0:T(8,128)S(1)} %get-tuple-element.23), channel_id=1, source_target_pairs={{1,0},{2,1},{3,2},{5,4},{6,5},{7,6},{9,8},{10,9},{11,10},{13,12},{... | collective-permute-start | bytes 737288 | tf_op jit(solution)/shard_map/ppermute | solution.py:24
  18.9 11.5 %collective-permute-start.10 = (f32[15,16,256]{2,1,0:T(8,128)S(1)}, f32[15,16,256]{2,1,0:T(8,128)S(1)}, u32[]{:S(2)}, u32[]{:S(2)}) collective-permute-start(f32[15,16,256]{2,1,0:T(8,128)S(1)} %get-tuple-element.24), channel_id=1, source_target_pairs={{0,1},{1,2},{2,3},{4,5},{5,6},{6,7},{8,9},{9,10},{10,11},{12,13},{... | collective-permute-start | bytes 737288 | tf_op jit(solution)/shard_map/ppermute | solution.py:20
  23.3 12.8 %collective-permute-start.4 = (f32[16,15,256]{2,0,1:T(8,128)S(1)}, f32[16,15,256]{2,0,1:T(8,128)S(1)}, u32[]{:S(2)}, u32[]{:S(2)}) collective-permute-start(f32[16,15,256]{2,0,1:T(8,128)S(1)} %get-tuple-element.32), channel_id=1, source_target_pairs={{0,4},{4,8},{8,12},{12,16},{16,20},{20,24},{24,28},{1,5},{5,9},{9,... | collective-permute-start | bytes 737288 | tf_op jit(solution)/shard_map/ppermute | solution.py:20
  28.4 9.6 %collective-permute-start.5 = (f32[16,15,256]{2,0,1:T(8,128)S(1)}, f32[16,15,256]{2,0,1:T(8,128)S(1)}, u32[]{:S(2)}, u32[]{:S(2)}) collective-permute-start(f32[16,15,256]{2,0,1:T(8,128)S(1)} %get-tuple-element.33), channel_id=1, source_target_pairs={{4,0},{8,4},{12,8},{16,12},{20,16},{24,20},{28,24},{5,1},{9,5},{13... | collective-permute-start | bytes 737288 | tf_op jit(solution)/shard_map/ppermute | solution.py:24
  31.3 6.8 %copy-start.1 = (f32[16,16,512]{2,1,0:T(8,128)S(1)}, f32[16,16,512]{2,1,0:T(8,128)}, u32[]{:S(2)}) copy-start(f32[16,16,512]{2,1,0:T(8,128)} %param.6) | copy-start | bytes 1572868
  31.4 10.9 %collective-permute-start.12 = (f32[16,15,256]{2,0,1:T(8,128)S(1)}, f32[16,15,256]{2,0,1:T(8,128)S(1)}, u32[]{:S(2)}, u32[]{:S(2)}) collective-permute-start(f32[16,15,256]{2,0,1:T(8,128)S(1)} %get-tuple-element.36), channel_id=1, source_target_pairs={{0,4},{4,8},{8,12},{12,16},{16,20},{20,24},{24,28},{1,5},{5,9},{9,... | collective-permute-start | bytes 737288 | tf_op jit(solution)/shard_map/ppermute | solution.py:20
  36.1 8.4 %collective-permute-start.13 = (f32[16,15,256]{2,0,1:T(8,128)S(1)}, f32[16,15,256]{2,0,1:T(8,128)S(1)}, u32[]{:S(2)}, u32[]{:S(2)}) collective-permute-start(f32[16,15,256]{2,0,1:T(8,128)S(1)} %get-tuple-element.37), channel_id=1, source_target_pairs={{4,0},{8,4},{12,8},{16,12},{20,16},{24,20},{28,24},{5,1},{9,5},{13... | collective-permute-start | bytes 737288 | tf_op jit(solution)/shard_map/ppermute | solution.py:24
  39.0 9.7 %collective-permute-start.6 = (f32[15,16,256]{2,1,0:T(8,128)S(1)}, f32[15,16,256]{2,1,0:T(8,128)S(1)}, u32[]{:S(2)}, u32[]{:S(2)}) collective-permute-start(f32[15,16,256]{2,1,0:T(8,128)S(1)} %get-tuple-element.30), channel_id=1, source_target_pairs={{0,1},{1,2},{2,3},{4,5},{5,6},{6,7},{8,9},{9,10},{10,11},{12,13},{... | collective-permute-start | bytes 737288 | tf_op jit(solution)/shard_map/ppermute | solution.py:20
  42.3 9.4 %collective-permute-start.7 = (f32[15,16,256]{2,1,0:T(8,128)S(1)}, f32[15,16,256]{2,1,0:T(8,128)S(1)}, u32[]{:S(2)}, u32[]{:S(2)}) collective-permute-start(f32[15,16,256]{2,1,0:T(8,128)S(1)} %get-tuple-element.31), channel_id=1, source_target_pairs={{1,0},{2,1},{3,2},{5,4},{6,5},{7,6},{9,8},{10,9},{11,10},{13,12},{... | collective-permute-start | bytes 737288 | tf_op jit(solution)/shard_map/ppermute | solution.py:24
  45.5 9.6 %collective-permute-start.14 = (f32[15,16,256]{2,1,0:T(8,128)S(1)}, f32[15,16,256]{2,1,0:T(8,128)S(1)}, u32[]{:S(2)}, u32[]{:S(2)}) collective-permute-start(f32[15,16,256]{2,1,0:T(8,128)S(1)} %get-tuple-element.34), channel_id=1, source_target_pairs={{0,1},{1,2},{2,3},{4,5},{5,6},{6,7},{8,9},{9,10},{10,11},{12,13},{... | collective-permute-start | bytes 737288 | tf_op jit(solution)/shard_map/ppermute | solution.py:20
  48.7 10.6 %collective-permute-start.15 = (f32[15,16,256]{2,1,0:T(8,128)S(1)}, f32[15,16,256]{2,1,0:T(8,128)S(1)}, u32[]{:S(2)}, u32[]{:S(2)}) collective-permute-start(f32[15,16,256]{2,1,0:T(8,128)S(1)} %get-tuple-element.35), channel_id=1, source_target_pairs={{1,0},{2,1},{3,2},{5,4},{6,5},{7,6},{9,8},{10,9},{11,10},{13,12},{... | collective-permute-start | bytes 737288 | tf_op jit(solution)/shard_map/ppermute | solution.py:24
  52.7 9.7 %collective-permute-start.9 = (f32[16,16,256]{2,0,1:T(8,128)S(1)}, f32[16,16,256]{2,0,1:T(8,128)S(1)}, u32[]{:S(2)}, u32[]{:S(2)}) collective-permute-start(f32[16,16,256]{2,0,1:T(8,128)S(1)} %fusion.19), channel_id=1, source_target_pairs={{4,0},{8,4},{12,8},{16,12},{20,16},{24,20},{28,24},{5,1},{9,5},{13... | collective-permute-start | bytes 786440 | tf_op jit(solution)/shard_map/ppermute | solution.py:24
  55.1 11.8 %collective-permute-start.8 = (f32[16,16,256]{2,0,1:T(8,128)S(1)}, f32[16,16,256]{2,0,1:T(8,128)S(1)}, u32[]{:S(2)}, u32[]{:S(2)}) collective-permute-start(f32[16,16,256]{2,0,1:T(8,128)S(1)} %fusion.19), channel_id=1, source_target_pairs={{0,4},{4,8},{8,12},{12,16},{16,20},{20,24},{24,28},{1,5},{5,9},{9,... | collective-permute-start | bytes 786440 | tf_op jit(solution)/shard_map/ppermute | solution.py:20
  60.3 10.6 %collective-permute-start.17 = (f32[16,16,256]{2,0,1:T(8,128)S(1)}, f32[16,16,256]{2,0,1:T(8,128)S(1)}, u32[]{:S(2)}, u32[]{:S(2)}) collective-permute-start(f32[16,16,256]{2,0,1:T(8,128)S(1)} %fusion.14), channel_id=1, source_target_pairs={{4,0},{8,4},{12,8},{16,12},{20,16},{24,20},{28,24},{5,1},{9,5},{13... | collective-permute-start | bytes 786440 | tf_op jit(solution)/shard_map/ppermute | solution.py:24
  62.4 8.5 %collective-permute-start.16 = (f32[16,16,256]{2,0,1:T(8,128)S(1)}, f32[16,16,256]{2,0,1:T(8,128)S(1)}, u32[]{:S(2)}, u32[]{:S(2)}) collective-permute-start(f32[16,16,256]{2,0,1:T(8,128)S(1)} %fusion.14), channel_id=1, source_target_pairs={{0,4},{4,8},{8,12},{12,16},{16,20},{20,24},{24,28},{1,5},{5,9},{9,... | collective-permute-start | bytes 786440 | tf_op jit(solution)/shard_map/ppermute | solution.py:20

commit v5 on v4

--- a/solution.py
+++ b/solution.py
@@ -7,23 +7,38 @@
 CHUNKS = 2
 
 
-def halo(shard, axis, dim, before_width, after_width):
+def halo(shard, axis, dim, before_width, after_width, riders=None):
     devices, length = lax.axis_size(axis), shard.shape[dim]
     pieces_before, pieces_after = [], []
+    carried = None
     hop = 1
     while (hop - 1) * length < max(before_width, after_width):
         up = [(i, i + hop) for i in range(devices - hop)]
         down = [(i + hop, i) for i in range(devices - hop)]
+        start = max(0, hop * length - before_width)
+        stop = min(length, after_width - (hop - 1) * length)
+        send_up = lax.slice_in_dim(shard, start, length, axis=dim)
+        send_down = lax.slice_in_dim(shard, 0, stop, axis=dim)
+        if hop == 1 and riders is not None:
+            send_up = jnp.concatenate([send_up, riders[0]], axis=dim)
+            send_down = jnp.concatenate([send_down, riders[1]], axis=dim)
+        got_up = lax.ppermute(send_up, axis, up)
+        got_down = lax.ppermute(send_down, axis, down)
+        if hop == 1 and riders is not None:
+            width_up, width_down = length - start, stop
+            carried = (
+                lax.slice_in_dim(got_up, width_up, got_up.shape[dim], axis=dim),
+                lax.slice_in_dim(got_down, width_down, got_down.shape[dim], axis=dim),
+            )
+            got_up = lax.slice_in_dim(got_up, 0, width_up, axis=dim)
+            got_down = lax.slice_in_dim(got_down, 0, width_down, axis=dim)
         if (hop - 1) * length < before_width:
-            start = max(0, hop * length - before_width)
-            piece = lax.slice_in_dim(shard, start, length, axis=dim)
-            pieces_before.insert(0, lax.ppermute(piece, axis, up))
+            pieces_before.insert(0, got_up)
         if (hop - 1) * length < after_width:
-            stop = min(length, after_width - (hop - 1) * length)
-            piece = lax.slice_in_dim(shard, 0, stop, axis=dim)
-            pieces_after.append(lax.ppermute(piece, axis, down))
+            pieces_after.append(got_down)
         hop += 1
-    return jnp.concatenate(pieces_before + [shard] + pieces_after, axis=dim)
+    joined = jnp.concatenate(pieces_before + [shard] + pieces_after, axis=dim)
+    return joined if riders is None else (joined, carried)
 
 
 def band(kernel, n_in, n_out, sign, shift):
@@ -107,18 +122,30 @@
 
     filtered = along_columns(estimate, col_band)
     chunk = col_count // CHUNKS
+    planes = plane_count
+    last_row = lax.slice_in_dim(estimate, row_count - 1, row_count, axis=1)
+    first_row = lax.slice_in_dim(estimate, 0, 1, axis=1)
+    fold = (planes, CHUNKS, chunk)
+    riders = (last_row.reshape(fold), first_row.reshape(fold))
     spreads = []
     for index in range(CHUNKS):
         part = lax.slice_in_dim(filtered, index * chunk, (index + 1) * chunk, axis=2)
         seen = lax.slice_in_dim(observed, index * chunk, (index + 1) * chunk, axis=2)
         blurred = along_planes(halo(part, "slab", 0, reach, reach), plane_fwd)
-        blurred = along_rows(halo(blurred, "tile", 1, reach, reach), row_fwd)
+        if index == 0:
+            blurred, carried = halo(blurred, "tile", 1, reach, reach, riders)
+        else:
+            blurred = halo(blurred, "tile", 1, reach, reach)
+        blurred = along_rows(blurred, row_fwd)
         quotient = seen / blurred
         spread = along_planes(halo(quotient, "slab", 0, reach, reach), plane_back)
         spread = along_rows(halo(spread, "tile", 1, reach + 1, reach + 1), row_back)
         spreads.append(spread)
     correction = along_columns(jnp.concatenate(spreads, axis=2), col_band, transpose=True)
-    edge_rows = halo(estimate, "tile", 1, 1, 1)
+    unfold = (planes, 1, col_count)
+    edge_rows = jnp.concatenate(
+        [carried[0].reshape(unfold), estimate, carried[1].reshape(unfold)], axis=1
+    )
     new_ext = edge_rows * correction
     new_estimate = lax.slice_in_dim(new_ext, 1, row_count + 1, axis=1)
 

time: 77.4 us -> 76.6 us (0.990)
  starting transfers between devices: 53.5 us -> 47.6 us
  waiting for transfers between devices: 4.61 us -> 9.23 us
  local copies, waits for them, and re-layouts: 1.31 us -> 2.41 us
    ppermute x18 -> x16, starting transfers between devices: 53.5 us -> 47.6 us  [the longest x8 31 us: halo(): got_up = lax.ppermute(send_up, axis, up)]
    ppermute x18 -> x16, waiting for transfers between devices: 4.61 us -> 9.23 us  [the longest x8 9.21 us: halo(): got_down = lax.ppermute(send_down, axis, down)]
    slice x6 -> x12, local copies, waits for them, and re-layouts: 0.36 us -> 1.35 us  [the longest x5 1.09 us: halo(): send_up = lax.slice_in_dim(shard, start, length, axis=dim)]
  transfers between devices with their start and end apart: 18 -> 16, of which waited for: 5 -> 4; matrix products, arithmetic and copies ran while one was open for 11% -> 9% of each run, Pallas kernels for 0% -> 0%
where the time goes in v5:
time: 76.6 us; the launch traced here: 75.9 us
  starting transfers between devices  47.6 us (62%)
  matrix products  11.6 us (15%)
  waiting for transfers between devices  9.23 us (12%)
  other arithmetic  3.8 us (5%)
  local copies, waits for them, and re-layouts  2.41 us (3%)
  between operations  1.23 us (2%)
    ppermute x8, starting transfers between devices, halo(): got_up = lax.ppermute(send_up, axis, up)  31 us
    ppermute x8, starting transfers between devices, halo(): got_down = lax.ppermute(send_down, axis, down)  16.6 us
    ppermute x8, waiting for transfers between devices, halo(): got_down = lax.ppermute(send_down, axis, down)  9.21 us
    dot_general x5, matrix products, along_rows(): lax.dot_general(left, volume, (((2,), (1,)), ((0,), (0,))), precision=PRE...  4.63 us
    dot_general x4, matrix products, along_planes(): lax.dot_general(matrix.T, volume, (((1,), (0,)), ((), ())), precision=PRE...  3.61 us
    dot_general x3, matrix products, along_columns(): lax.dot_general(volume, matrix, (((2,), (contract,)), ((), ())), precisio...  3.33 us
    reduce_sum x3, other arithmetic, band(): return jnp.sum(picked, axis=2)  3.01 us
  transfers between devices with their start and end apart: 16, of which 4 were waited for; matrix products, arithmetic and copies ran while one was open for 9% of the time, Pallas kernels for 0%

profile of v5, /device:TPU:11, one launch (start us, length us, event | category | flops | bytes accessed | tf_op | source)
XLA Modules:
  0.0 75.9 jit_solution(4523903806023834913)
XLA Ops:
  0.7 0.1 select_select_fusion.1
  0.8 0.1 select_select_fusion
  0.9 0.8 %select_reduce_fusion.3 = f32[48,18]{0,1:T(8,128)S(1)} fusion(f32[31]{0:T(128)} %param.7, s32[48,18]{0,1:T(8,128)S(1)} %multiply_add_fusion), kind=kLoop, calls=%fused_computation.49 | loop fusion | flops 79488 | bytes 7036 | tf_op jit(solution)/shard_map/reduce_sum | solution.py:51
  1.7 0.0 copy-start
  1.7 0.9 %select_reduce_fusion.5 = (f32[46,16]{0,1:T(8,128)S(1)}, f32[46,16]{0,1:T(8,128)S(1)}, f32[46,16]{0,1:T(8,128)S(1)}) fusion(f32[31]{0:T(128)} %param.9, s32[46,16]{0,1:T(8,128)S(1)} %get-tuple-element.41, f32[31]{0:T(128)} %param.7, s32[46,16]{0,1:T(8,128)S(1)} %get-tuple-element.40), kind=kLoop, calls=%fused_computation.55 | loop fusion | flops 180320 | bytes 14968 | tf_op jit(solution)/shard_map/reduce_sum | solution.py:51
  2.6 1.3 %select_reduce_fusion.1 = (f32[128,128]{1,0:T(8,128)S(1)}, f32[128,128]{1,0:T(8,128)S(1)}, f32[128,128]{1,0:T(8,128)S(1)}) fusion(s32[128,128]{1,0:T(8,128)S(1)} %get-tuple-element.39, f32[31]{0:T(128)} %param.8, s32[128,128]{1,0:T(8,128)S(1)} %get-tuple-element.38, s32[128,128]{1,0:T(8,128)S(1)} %fusion.38), kind=kLoop, calls=%fused_computation.2 | loop fusion | flops 4521984 | bytes 393340 | tf_op jit(solution)/shard_map/reduce_sum | solution.py:51
  4.0 0.1 maximum_maximum_fusion
  4.1 1.1 %convolution_bitcast_fusion = f32[16,16,512]{2,1,0:T(8,128)S(1)} fusion(f32[16,16,512]{2,1,0:T(8,128)S(1)} %copy-done, f32[512,512]{1,0:T(8,128)S(1)} %maximum_maximum_fusion), kind=kOutput, calls=%fused_computation.6 | convolution fusion | flops 805306368 | bytes 2097152 | tf_op jit(solution)/shard_map/dot_general | solution.py:86
  5.2 0.1 fusion.52
  5.3 3.2 %collective-permute-start.8 = (f32[15,16,256]{2,1,0:T(8,128)S(1)}, f32[15,16,256]{2,1,0:T(8,128)S(1)}, u32[]{:S(2)}, u32[]{:S(2)}) collective-permute-start(f32[15,16,256]{2,1,0:T(8,128)S(1)} %get-tuple-element.24), channel_id=1, source_target_pairs={{0,1},{1,2},{2,3},{4,5},{5,6},{6,7},{8,9},{9,10},{10,11},{12,13},{... | collective-permute-start | bytes 737288 | tf_op jit(solution)/shard_map/ppermute | solution.py:25
  8.5 2.1 %collective-permute-start.9 = (f32[15,16,256]{2,1,0:T(8,128)S(1)}, f32[15,16,256]{2,1,0:T(8,128)S(1)}, u32[]{:S(2)}, u32[]{:S(2)}) collective-permute-start(f32[15,16,256]{2,1,0:T(8,128)S(1)} %get-tuple-element.25), channel_id=1, source_target_pairs={{1,0},{2,1},{3,2},{5,4},{6,5},{7,6},{9,8},{10,9},{11,10},{13,12},{... | collective-permute-start | bytes 737288 | tf_op jit(solution)/shard_map/ppermute | solution.py:26
  10.6 1.9 %collective-permute-start.1 = (f32[15,16,256]{2,1,0:T(8,128)S(1)}, f32[15,16,256]{2,1,0:T(8,128)S(1)}, u32[]{:S(2)}, u32[]{:S(2)}) collective-permute-start(f32[15,16,256]{2,1,0:T(8,128)S(1)} %get-tuple-element.26), channel_id=1, source_target_pairs={{1,0},{2,1},{3,2},{5,4},{6,5},{7,6},{9,8},{10,9},{11,10},{13,12},{... | collective-permute-start | bytes 737288 | tf_op jit(solution)/shard_map/ppermute | solution.py:26
  12.5 3.4 %collective-permute-start = (f32[15,16,256]{2,1,0:T(8,128)S(1)}, f32[15,16,256]{2,1,0:T(8,128)S(1)}, u32[]{:S(2)}, u32[]{:S(2)}) collective-permute-start(f32[15,16,256]{2,1,0:T(8,128)S(1)} %get-tuple-element.27), channel_id=1, source_target_pairs={{0,1},{1,2},{2,3},{4,5},{5,6},{6,7},{8,9},{9,10},{10,11},{12,13},{... | collective-permute-start | bytes 737288 | tf_op jit(solution)/shard_map/ppermute | solution.py:25
  15.9 0.2 slice_reduce_fusion.1
  16.1 0.1 fusion.53
  16.2 0.0 collective-permute-done.8
  16.2 0.7 collective-permute-done.9
  16.9 0.1 pad_maximum_fusion.5
  17.0 0.9 %fusion.15 = f32[16,16,256]{2,0,1:T(8,128)S(1)} fusion(f32[46,16,256]{2,1,0:T(8,128)S(1)} %pad_maximum_fusion.5, f32[46,16]{0,1:T(8,128)S(1)} %get-tuple-element.9), kind=kOutput, calls=%fused_computation.24 | convolution fusion | flops 36175872 | bytes 1018752 | tf_op jit(solution)/shard_map/dot_general | solution.py:100
  17.9 4.3 %collective-permute-done.1 = f32[15,16,256]{2,1,0:T(8,128)S(1)} collective-permute-done((f32[15,16,256]{2,1,0:T(8,128)S(1)}, f32[15,16,256]{2,1,0:T(8,128)S(1)}, u32[]{:S(2)}, u32[]{:S(2)}) %collective-permute-start.1) | collective-permute-done | bytes 245792 | tf_op jit(solution)/shard_map/ppermute | solution.py:26
  22.2 0.0 collective-permute-done
  22.2 0.1 pad_maximum_fusion.2
  22.2 0.9 %fusion.22 = f32[16,16,256]{2,0,1:T(8,128)S(1)} fusion(f32[46,16,256]{2,1,0:T(8,128)S(1)} %pad_maximum_fusion.2, f32[46,16]{0,1:T(8,128)S(1)} %get-tuple-element.9), kind=kOutput, calls=%fused_computation.31 | convolution fusion | flops 36175872 | bytes 1018752 | tf_op jit(solution)/shard_map/dot_general | solution.py:100
  23.2 0.1 fusion.56
  23.2 4.9 %collective-permute-start.10 = (f32[16,15,256]{2,0,1:T(8,128)S(1)}, f32[16,15,256]{2,0,1:T(8,128)S(1)}, u32[]{:S(2)}, u32[]{:S(2)}) collective-permute-start(f32[16,15,256]{2,0,1:T(8,128)S(1)} %get-tuple-element.34), channel_id=1, source_target_pairs={{0,4},{4,8},{8,12},{12,16},{16,20},{20,24},{24,28},{1,5},{5,9},{9,... | collective-permute-start | bytes 737288 | tf_op jit(solution)/shard_map/ppermute | solution.py:25
  28.1 1.9 %collective-permute-start.11 = (f32[16,15,256]{2,0,1:T(8,128)S(1)}, f32[16,15,256]{2,0,1:T(8,128)S(1)}, u32[]{:S(2)}, u32[]{:S(2)}) collective-permute-start(f32[16,15,256]{2,0,1:T(8,128)S(1)} %get-tuple-element.35), channel_id=1, source_target_pairs={{4,0},{8,4},{12,8},{16,12},{20,16},{24,20},{28,24},{5,1},{9,5},{13... | collective-permute-start | bytes 737288 | tf_op jit(solution)/shard_map/ppermute | solution.py:26
  30.0 0.1 fusion.57
  30.1 0.0 copy-start.1
  30.1 2.7 %collective-permute-start.3 = (f32[16,17,256]{2,0,1:T(8,128)S(1)}, f32[16,17,256]{2,0,1:T(8,128)S(1)}, u32[]{:S(2)}, u32[]{:S(2)}) collective-permute-start(f32[16,17,256]{2,0,1:T(8,128)S(1)} %pad_maximum_fusion.9), channel_id=1, source_target_pairs={{4,0},{8,4},{12,8},{16,12},{20,16},{24,20},{28,24},{5,1},{9,5},{13... | collective-permute-start | bytes 835592 | tf_op jit(solution)/shard_map/ppermute | solution.py:26
  32.8 3.9 %collective-permute-start.2 = (f32[16,17,256]{2,0,1:T(8,128)S(1)}, f32[16,17,256]{2,0,1:T(8,128)S(1)}, u32[]{:S(2)}, u32[]{:S(2)}) collective-permute-start(f32[16,17,256]{2,0,1:T(8,128)S(1)} %pad_maximum_fusion.8), channel_id=1, source_target_pairs={{0,4},{4,8},{8,12},{12,16},{16,20},{20,24},{24,28},{1,5},{5,9},{9,... | collective-permute-start | bytes 835592 | tf_op jit(solution)/shard_map/ppermute | solution.py:25
  36.8 0.0 collective-permute-done.10
  36.8 0.0 collective-permute-done.11
  36.8 0.1 pad_maximum_fusion.6
  36.8 0.9 %convolution_divide_fusion = f32[16,16,256]{2,1,0:T(8,128)S(1)} fusion(f32[16,46,256]{2,0,1:T(8,128)S(1)} %pad_maximum_fusion.6, f32[16,16,512]{2,1,0:T(8,128)S(1)} %copy-done.1, f32[16,46]{1,0:T(8,128)S(1)} %bitcast.42), kind=kOutput, calls=%fused_computation.7 | convolution fusion | flops 36241408 | bytes 1280896 | tf_op jit(solution)/shard_map/dot_general | solution.py:94
  37.8 0.8 %fusion.55 = (f32[15,16,256]{2,1,0:T(8,128)}, f32[15,16,256]{2,1,0:T(8,128)}) fusion(f32[16,16,256]{2,1,0:T(8,128)S(1)} %convolution_divide_fusion), kind=kLoop, calls=%fused_computation.93 | loop fusion | bytes 983040 | tf_op jit(solution)/shard_map/slice | solution.py:20
  38.6 3.2 %collective-permute-start.12 = (f32[15,16,256]{2,1,0:T(8,128)}, f32[15,16,256]{2,1,0:T(8,128)S(1)}, u32[]{:S(2)}, u32[]{:S(2)}) collective-permute-start(f32[15,16,256]{2,1,0:T(8,128)} %get-tuple-element.32), channel_id=1, source_target_pairs={{0,1},{1,2},{2,3},{4,5},{5,6},{6,7},{8,9},{9,10},{10,11},{12,13},{... | collective-permute-start | bytes 737288 | tf_op jit(solution)/shard_map/ppermute | solution.py:25
  41.8 2.1 %collective-permute-start.13 = (f32[15,16,256]{2,1,0:T(8,128)}, f32[15,16,256]{2,1,0:T(8,128)S(1)}, u32[]{:S(2)}, u32[]{:S(2)}) collective-permute-start(f32[15,16,256]{2,1,0:T(8,128)} %get-tuple-element.33), channel_id=1, source_target_pairs={{1,0},{2,1},{3,2},{5,4},{6,5},{7,6},{9,8},{10,9},{11,10},{13,12},{... | collective-permute-start | bytes 737288 | tf_op jit(solution)/shard_map/ppermute | solution.py:26
  43.9 0.0 collective-permute-done.2
  44.0 0.1 pad_maximum_fusion.3
  44.0 0.9 %convolution_divide_fusion.1 = f32[16,16,256]{2,1,0:T(8,128)S(1)} fusion(f32[16,46,256]{2,0,1:T(8,128)S(1)} %pad_maximum_fusion.3, f32[16,16,512]{2,1,0:T(8,128)S(1)} %copy-done.1, f32[16,46]{1,0:T(8,128)S(1)} %bitcast.43), kind=kOutput, calls=%fused_computation.8 | convolution fusion | flops 36241408 | bytes 1280896 | tf_op jit(solution)/shard_map/dot_general | solution.py:94
  45.0 0.1 reshape.71
  45.1 0.1 reshape.70
  45.2 3.2 %collective-permute-start.4 = (f32[15,16,256]{2,1,0:T(8,128)S(1)}, f32[15,16,256]{2,1,0:T(8,128)S(1)}, u32[]{:S(2)}, u32[]{:S(2)}) collective-permute-start(f32[15,16,256]{2,1,0:T(8,128)S(1)} %get-tuple-element.30), channel_id=1, source_target_pairs={{0,1},{1,2},{2,3},{4,5},{5,6},{6,7},{8,9},{9,10},{10,11},{12,13},{... | collective-permute-start | bytes 737288 | tf_op jit(solution)/shard_map/ppermute | solution.py:25
  48.4 2.1 %collective-permute-start.5 = (f32[15,16,256]{2,1,0:T(8,128)S(1)}, f32[15,16,256]{2,1,0:T(8,128)S(1)}, u32[]{:S(2)}, u32[]{:S(2)}) collective-permute-start(f32[15,16,256]{2,1,0:T(8,128)S(1)} %get-tuple-element.31), channel_id=1, source_target_pairs={{1,0},{2,1},{3,2},{5,4},{6,5},{7,6},{9,8},{10,9},{11,10},{13,12},{... | collective-permute-start | bytes 737288 | tf_op jit(solution)/shard_map/ppermute | solution.py:26
  50.5 0.6 collective-permute-done.13
  51.1 0.1 pad_maximum_fusion.7
  51.2 0.9 %fusion.12 = f32[16,16,256]{2,0,1:T(8,128)S(1)} fusion(f32[46,16,256]{2,1,0:T(8,128)S(1)} %pad_maximum_fusion.7, f32[46,16]{0,1:T(8,128)S(1)} %get-tuple-element.12), kind=kOutput, calls=%fused_computation.21 | convolution fusion | flops 36175872 | bytes 1018752 | tf_op jit(solution)/shard_map/dot_general | solution.py:100
  52.1 1.9 %collective-permute-start.15 = (f32[16,16,256]{2,0,1:T(8,128)S(1)}, f32[16,16,256]{2,0,1:T(8,128)S(1)}, u32[]{:S(2)}, u32[]{:S(2)}) collective-permute-start(f32[16,16,256]{2,0,1:T(8,128)S(1)} %fusion.12), channel_id=1, source_target_pairs={{4,0},{8,4},{12,8},{16,12},{20,16},{24,20},{28,24},{5,1},{9,5},{13... | collective-permute-start | bytes 786440 | tf_op jit(solution)/shard_map/ppermute | solution.py:26
  54.0 4.5 %collective-permute-start.14 = (f32[16,16,256]{2,0,1:T(8,128)S(1)}, f32[16,16,256]{2,0,1:T(8,128)S(1)}, u32[]{:S(2)}, u32[]{:S(2)}) collective-permute-start(f32[16,16,256]{2,0,1:T(8,128)S(1)} %fusion.12), channel_id=1, source_target_pairs={{0,4},{4,8},{8,12},{12,16},{16,20},{20,24},{24,28},{1,5},{5,9},{9,... | collective-permute-start | bytes 786440 | tf_op jit(solution)/shard_map/ppermute | solution.py:25
  58.6 0.0 collective-permute-done.4
  58.6 0.1 pad_maximum_fusion.4
  58.6 0.9 %fusion.19 = f32[16,16,256]{2,0,1:T(8,128)S(1)} fusion(f32[46,16,256]{2,1,0:T(8,128)S(1)} %pad_maximum_fusion.4, f32[46,16]{0,1:T(8,128)S(1)} %get-tuple-element.12), kind=kOutput, calls=%fused_computation.28 | convolution fusion | flops 36175872 | bytes 1018752 | tf_op jit(solution)/shard_map/dot_general | solution.py:100
  59.5 1.9 %collective-permute-start.7 = (f32[16,16,256]{2,0,1:T(8,128)S(1)}, f32[16,16,256]{2,0,1:T(8,128)S(1)}, u32[]{:S(2)}, u32[]{:S(2)}) collective-permute-start(f32[16,16,256]{2,0,1:T(8,128)S(1)} %fusion.19), channel_id=1, source_target_pairs={{4,0},{8,4},{12,8},{16,12},{20,16},{24,20},{28,24},{5,1},{9,5},{13... | collective-permute-start | bytes 786440 | tf_op jit(solution)/shard_map/ppermute | solution.py:26
  61.5 4.7 %collective-permute-start.6 = (f32[16,16,256]{2,0,1:T(8,128)S(1)}, f32[16,16,256]{2,0,1:T(8,128)S(1)}, u32[]{:S(2)}, u32[]{:S(2)}) collective-permute-start(f32[16,16,256]{2,0,1:T(8,128)S(1)} %fusion.19), channel_id=1, source_target_pairs={{0,4},{4,8},{8,12},{12,16},{16,20},{20,24},{24,28},{1,5},{5,9},{9,... | collective-permute-start | bytes 786440 | tf_op jit(solution)/shard_map/ppermute | solution.py:25
  66.2 0.0 collective-permute-done.15
  66.2 0.1 pad_maximum_fusion.1
  66.3 0.9 %fusion.10 = f32[16,18,256]{2,1,0:T(8,128)S(1)} fusion(f32[16,48,256]{2,0,1:T(8,128)S(1)} %pad_maximum_fusion.1, f32[18,48]{1,0:T(8,128)S(1)} %bitcast.40), kind=kOutput, calls=%fused_computation.19 | convolution fusion | flops 42467328 | bytes 1084800 | tf_op jit(solution)/shard_map/dot_general | solution.py:94
  67.2 3.6 %collective-permute-done.7 = f32[16,16,256]{2,0,1:T(8,128)S(1)} collective-permute-done((f32[16,16,256]{2,0,1:T(8,128)S(1)}, f32[16,16,256]{2,0,1:T(8,128)S(1)}, u32[]{:S(2)}, u32[]{:S(2)}) %collective-permute-start.7) | collective-permute-done | bytes 262176 | tf_op jit(solution)/shard_map/ppermute | solution.py:26
  70.8 0.1 pad_maximum_fusion
  70.8 0.9 %fusion.17 = f32[16,18,256]{2,1,0:T(8,128)S(1)} fusion(f32[16,48,256]{2,0,1:T(8,128)S(1)} %pad_maximum_fusion, f32[18,48]{1,0:T(8,128)S(1)} %bitcast.41), kind=kOutput, calls=%fused_computation.26 | convolution fusion | flops 42467328 | bytes 1084800 | tf_op jit(solution)/shard_map/dot_general | solution.py:94
  71.8 1.5 %maximum_multiply_fusion = f32[16,18,512]{2,1,0:T(8,128)S(1)} fusion(f32[16,1,512]{2,1,0:T(1,128)S(1)} %reshape.71, f32[16,16,512]{2,1,0:T(8,128)S(1)} %copy-done, f32[16,1,512]{2,1,0:T(1,128)S(1)} %reshape.70, f32[512,512]{1,0:T(8,128)S(1)} %maximum_maximum_fusion, f32[16,18,256]{2,1,0:T(8,128)S(1)} %fusion.10, f32[16,18,256]{2,1,0:T(8,128)S(1)} %fusion.17), kind=kOutput, calls=%fused_computation.13 | convolution fusion | flops 906559488 | bytes 2818048 | tf_op jit(solution)/shard_map/dot_general | solution.py:86
  73.2 0.9 %slice.114 = f32[16,16,512]{2,1,0:T(8,128)} slice(f32[16,18,512]{2,1,0:T(8,128)S(1)} %maximum_multiply_fusion), slice={[0:16], [1:17], [0:512]} | slice | bytes 1048576 | tf_op jit(solution)/shard_map/slice | solution.py:150
  74.1 0.8 %fusion.24 = f32[16,18,256]{2,1,0:T(8,128)S(1)} fusion(f32[16,18,512]{2,1,0:T(8,128)S(1)} %maximum_multiply_fusion, f32[512,256]{1,0:T(8,128)S(1)} %select_select_fusion), kind=kOutput, calls=%fused_computation.39 | convolution fusion | flops 452984832 | bytes 1409024 | tf_op jit(solution)/shard_map/dot_general | solution.py:86
  74.9 1.0 %fusion.39 = f32[16,8,256]{2,1,0:T(8,128)} fusion(f32[16,18,256]{2,1,0:T(8,128)S(1)} %fusion.24, f32[8,18]{1,0:T(8,128)S(1)} %bitcast.44), kind=kOutput, calls=%fused_computation.68 | convolution fusion | flops 7077888 | bytes 426560 | tf_op jit(solution)/shard_map/dot_general | solution.py:94
  (26 shorter events, 0.3 us)
Async XLA Ops:
  1.7 2.4 %copy-start = (f32[16,16,512]{2,1,0:T(8,128)S(1)}, f32[16,16,512]{2,1,0:T(8,128)}, u32[]{:S(2)}) copy-start(f32[16,16,512]{2,1,0:T(8,128)} %param.5) | copy-start | bytes 1572868
  5.3 10.9 %collective-permute-start.8 = (f32[15,16,256]{2,1,0:T(8,128)S(1)}, f32[15,16,256]{2,1,0:T(8,128)S(1)}, u32[]{:S(2)}, u32[]{:S(2)}) collective-permute-start(f32[15,16,256]{2,1,0:T(8,128)S(1)} %get-tuple-element.24), channel_id=1, source_target_pairs={{0,1},{1,2},{2,3},{4,5},{5,6},{6,7},{8,9},{9,10},{10,11},{12,13},{... | collective-permute-start | bytes 737288 | tf_op jit(solution)/shard_map/ppermute | solution.py:25
  8.5 8.4 %collective-permute-start.9 = (f32[15,16,256]{2,1,0:T(8,128)S(1)}, f32[15,16,256]{2,1,0:T(8,128)S(1)}, u32[]{:S(2)}, u32[]{:S(2)}) collective-permute-start(f32[15,16,256]{2,1,0:T(8,128)S(1)} %get-tuple-element.25), channel_id=1, source_target_pairs={{1,0},{2,1},{3,2},{5,4},{6,5},{7,6},{9,8},{10,9},{11,10},{13,12},{... | collective-permute-start | bytes 737288 | tf_op jit(solution)/shard_map/ppermute | solution.py:26
  10.6 11.6 %collective-permute-start.1 = (f32[15,16,256]{2,1,0:T(8,128)S(1)}, f32[15,16,256]{2,1,0:T(8,128)S(1)}, u32[]{:S(2)}, u32[]{:S(2)}) collective-permute-start(f32[15,16,256]{2,1,0:T(8,128)S(1)} %get-tuple-element.26), channel_id=1, source_target_pairs={{1,0},{2,1},{3,2},{5,4},{6,5},{7,6},{9,8},{10,9},{11,10},{13,12},{... | collective-permute-start | bytes 737288 | tf_op jit(solution)/shard_map/ppermute | solution.py:26
  12.5 9.6 %collective-permute-start = (f32[15,16,256]{2,1,0:T(8,128)S(1)}, f32[15,16,256]{2,1,0:T(8,128)S(1)}, u32[]{:S(2)}, u32[]{:S(2)}) collective-permute-start(f32[15,16,256]{2,1,0:T(8,128)S(1)} %get-tuple-element.27), channel_id=1, source_target_pairs={{0,1},{1,2},{2,3},{4,5},{5,6},{6,7},{8,9},{9,10},{10,11},{12,13},{... | collective-permute-start | bytes 737288 | tf_op jit(solution)/shard_map/ppermute | solution.py:25
  23.2 13.5 %collective-permute-start.10 = (f32[16,15,256]{2,0,1:T(8,128)S(1)}, f32[16,15,256]{2,0,1:T(8,128)S(1)}, u32[]{:S(2)}, u32[]{:S(2)}) collective-permute-start(f32[16,15,256]{2,0,1:T(8,128)S(1)} %get-tuple-element.34), channel_id=1, source_target_pairs={{0,4},{4,8},{8,12},{12,16},{16,20},{20,24},{24,28},{1,5},{5,9},{9,... | collective-permute-start | bytes 737288 | tf_op jit(solution)/shard_map/ppermute | solution.py:25
  28.1 8.7 %collective-permute-start.11 = (f32[16,15,256]{2,0,1:T(8,128)S(1)}, f32[16,15,256]{2,0,1:T(8,128)S(1)}, u32[]{:S(2)}, u32[]{:S(2)}) collective-permute-start(f32[16,15,256]{2,0,1:T(8,128)S(1)} %get-tuple-element.35), channel_id=1, source_target_pairs={{4,0},{8,4},{12,8},{16,12},{20,16},{24,20},{28,24},{5,1},{9,5},{13... | collective-permute-start | bytes 737288 | tf_op jit(solution)/shard_map/ppermute | solution.py:26
  30.1 6.7 %copy-start.1 = (f32[16,16,512]{2,1,0:T(8,128)S(1)}, f32[16,16,512]{2,1,0:T(8,128)}, u32[]{:S(2)}) copy-start(f32[16,16,512]{2,1,0:T(8,128)} %param.6) | copy-start | bytes 1572868
  30.1 13.8 %collective-permute-start.3 = (f32[16,17,256]{2,0,1:T(8,128)S(1)}, f32[16,17,256]{2,0,1:T(8,128)S(1)}, u32[]{:S(2)}, u32[]{:S(2)}) collective-permute-start(f32[16,17,256]{2,0,1:T(8,128)S(1)} %pad_maximum_fusion.9), channel_id=1, source_target_pairs={{4,0},{8,4},{12,8},{16,12},{20,16},{24,20},{28,24},{5,1},{9,5},{13... | collective-permute-start | bytes 835592 | tf_op jit(solution)/shard_map/ppermute | solution.py:26
  32.8 11.1 %collective-permute-start.2 = (f32[16,17,256]{2,0,1:T(8,128)S(1)}, f32[16,17,256]{2,0,1:T(8,128)S(1)}, u32[]{:S(2)}, u32[]{:S(2)}) collective-permute-start(f32[16,17,256]{2,0,1:T(8,128)S(1)} %pad_maximum_fusion.8), channel_id=1, source_target_pairs={{0,4},{4,8},{8,12},{12,16},{16,20},{20,24},{24,28},{1,5},{5,9},{9,... | collective-permute-start | bytes 835592 | tf_op jit(solution)/shard_map/ppermute | solution.py:25
  38.6 11.9 %collective-permute-start.12 = (f32[15,16,256]{2,1,0:T(8,128)}, f32[15,16,256]{2,1,0:T(8,128)S(1)}, u32[]{:S(2)}, u32[]{:S(2)}) collective-permute-start(f32[15,16,256]{2,1,0:T(8,128)} %get-tuple-element.32), channel_id=1, source_target_pairs={{0,1},{1,2},{2,3},{4,5},{5,6},{6,7},{8,9},{9,10},{10,11},{12,13},{... | collective-permute-start | bytes 737288 | tf_op jit(solution)/shard_map/ppermute | solution.py:25
  41.8 9.3 %collective-permute-start.13 = (f32[15,16,256]{2,1,0:T(8,128)}, f32[15,16,256]{2,1,0:T(8,128)S(1)}, u32[]{:S(2)}, u32[]{:S(2)}) collective-permute-start(f32[15,16,256]{2,1,0:T(8,128)} %get-tuple-element.33), channel_id=1, source_target_pairs={{1,0},{2,1},{3,2},{5,4},{6,5},{7,6},{9,8},{10,9},{11,10},{13,12},{... | collective-permute-start | bytes 737288 | tf_op jit(solution)/shard_map/ppermute | solution.py:26
  45.2 13.4 %collective-permute-start.4 = (f32[15,16,256]{2,1,0:T(8,128)S(1)}, f32[15,16,256]{2,1,0:T(8,128)S(1)}, u32[]{:S(2)}, u32[]{:S(2)}) collective-permute-start(f32[15,16,256]{2,1,0:T(8,128)S(1)} %get-tuple-element.30), channel_id=1, source_target_pairs={{0,1},{1,2},{2,3},{4,5},{5,6},{6,7},{8,9},{9,10},{10,11},{12,13},{... | collective-permute-start | bytes 737288 | tf_op jit(solution)/shard_map/ppermute | solution.py:25
  48.4 10.2 %collective-permute-start.5 = (f32[15,16,256]{2,1,0:T(8,128)S(1)}, f32[15,16,256]{2,1,0:T(8,128)S(1)}, u32[]{:S(2)}, u32[]{:S(2)}) collective-permute-start(f32[15,16,256]{2,1,0:T(8,128)S(1)} %get-tuple-element.31), channel_id=1, source_target_pairs={{1,0},{2,1},{3,2},{5,4},{6,5},{7,6},{9,8},{10,9},{11,10},{13,12},{... | collective-permute-start | bytes 737288 | tf_op jit(solution)/shard_map/ppermute | solution.py:26
  52.1 14.1 %collective-permute-start.15 = (f32[16,16,256]{2,0,1:T(8,128)S(1)}, f32[16,16,256]{2,0,1:T(8,128)S(1)}, u32[]{:S(2)}, u32[]{:S(2)}) collective-permute-start(f32[16,16,256]{2,0,1:T(8,128)S(1)} %fusion.12), channel_id=1, source_target_pairs={{4,0},{8,4},{12,8},{16,12},{20,16},{24,20},{28,24},{5,1},{9,5},{13... | collective-permute-start | bytes 786440 | tf_op jit(solution)/shard_map/ppermute | solution.py:26
  54.0 12.2 %collective-permute-start.14 = (f32[16,16,256]{2,0,1:T(8,128)S(1)}, f32[16,16,256]{2,0,1:T(8,128)S(1)}, u32[]{:S(2)}, u32[]{:S(2)}) collective-permute-start(f32[16,16,256]{2,0,1:T(8,128)S(1)} %fusion.12), channel_id=1, source_target_pairs={{0,4},{4,8},{8,12},{12,16},{16,20},{20,24},{24,28},{1,5},{5,9},{9,... | collective-permute-start | bytes 786440 | tf_op jit(solution)/shard_map/ppermute | solution.py:25
  59.5 11.2 %collective-permute-start.7 = (f32[16,16,256]{2,0,1:T(8,128)S(1)}, f32[16,16,256]{2,0,1:T(8,128)S(1)}, u32[]{:S(2)}, u32[]{:S(2)}) collective-permute-start(f32[16,16,256]{2,0,1:T(8,128)S(1)} %fusion.19), channel_id=1, source_target_pairs={{4,0},{8,4},{12,8},{16,12},{20,16},{24,20},{28,24},{5,1},{9,5},{13... | collective-permute-start | bytes 786440 | tf_op jit(solution)/shard_map/ppermute | solution.py:26
  61.5 9.3 %collective-permute-start.6 = (f32[16,16,256]{2,0,1:T(8,128)S(1)}, f32[16,16,256]{2,0,1:T(8,128)S(1)}, u32[]{:S(2)}, u32[]{:S(2)}) collective-permute-start(f32[16,16,256]{2,0,1:T(8,128)S(1)} %fusion.19), channel_id=1, source_target_pairs={{0,4},{4,8},{8,12},{12,16},{16,20},{20,24},{24,28},{1,5},{5,9},{9,... | collective-permute-start | bytes 786440 | tf_op jit(solution)/shard_map/ppermute | solution.py:25

commit v6 on v5

--- a/solution.py
+++ b/solution.py
@@ -3,7 +3,7 @@
 from jax import lax
 from jax.sharding import PartitionSpec as P
 
-PRECISE = lax.Precision.HIGHEST
+PRECISE = lax.Precision.HIGH
 CHUNKS = 2
 
 

time: 76.6 us -> 74.1 us (0.967)
  matrix products: 11.6 us -> 8.48 us
  waiting for transfers between devices: 9.23 us -> 10 us
    dot_general x3, matrix products: 3.33 us -> 1.93 us  [along_columns(): lax.dot_general(volume, matrix, (((2,), (contract,)), ((), ())), precisio...]
    dot_general x5, matrix products: 4.63 us -> 3.75 us  [along_rows(): lax.dot_general(left, volume, (((2,), (1,)), ((0,), (0,))), precision=PRE...]
    dot_general x4, matrix products: 3.61 us -> 2.8 us  [along_planes(): lax.dot_general(matrix.T, volume, (((1,), (0,)), ((), ())), precision=PRE...]
    ppermute x8, waiting for transfers between devices: 9.21 us -> 9.98 us  [halo(): got_down = lax.ppermute(send_down, axis, down)]
  transfers between devices with their start and end apart: 16 -> 16, of which waited for: 4 -> 4; matrix products, arithmetic and copies ran while one was open for 9% -> 8% of each run, Pallas kernels for 0% -> 0%
where the time goes in v6:
time: 74.1 us; the launch traced here: 73.4 us
  starting transfers between devices  47.5 us (64%)
  waiting for transfers between devices  10 us (13%)
  matrix products  8.48 us (11%)
  other arithmetic  3.8 us (5%)
  local copies, waits for them, and re-layouts  2.41 us (3%)
  between operations  1.23 us (2%)
    ppermute x8, starting transfers between devices, halo(): got_up = lax.ppermute(send_up, axis, up)  30.8 us
    ppermute x8, starting transfers between devices, halo(): got_down = lax.ppermute(send_down, axis, down)  16.6 us
    ppermute x8, waiting for transfers between devices, halo(): got_down = lax.ppermute(send_down, axis, down)  9.98 us
    dot_general x5, matrix products, along_rows(): lax.dot_general(left, volume, (((2,), (1,)), ((0,), (0,))), precision=PRE...  3.75 us
    reduce_sum x3, other arithmetic, band(): return jnp.sum(picked, axis=2)  3.01 us
    dot_general x4, matrix products, along_planes(): lax.dot_general(matrix.T, volume, (((1,), (0,)), ((), ())), precision=PRE...  2.8 us
    dot_general x3, matrix products, along_columns(): lax.dot_general(volume, matrix, (((2,), (contract,)), ((), ())), precisio...  1.93 us
  transfers between devices with their start and end apart: 16, of which 4 were waited for; matrix products, arithmetic and copies ran while one was open for 8% of the time, Pallas kernels for 0%

profile of v6, /device:TPU:11, one launch (start us, length us, event | category | flops | bytes accessed | tf_op | source)
XLA Modules:
  0.0 73.4 jit_solution(18003481280098472578)
XLA Ops:
  0.7 0.1 select_select_fusion.1
  0.8 0.1 select_select_fusion
  0.9 0.8 %select_reduce_fusion.3 = f32[48,18]{0,1:T(8,128)S(1)} fusion(f32[31]{0:T(128)} %param.7, s32[48,18]{0,1:T(8,128)S(1)} %multiply_add_fusion), kind=kLoop, calls=%fused_computation.49 | loop fusion | flops 79488 | bytes 7036 | tf_op jit(solution)/shard_map/reduce_sum | solution.py:51
  1.7 0.0 copy-start
  1.7 0.9 %select_reduce_fusion.5 = (f32[46,16]{0,1:T(8,128)S(1)}, f32[46,16]{0,1:T(8,128)S(1)}, f32[46,16]{0,1:T(8,128)S(1)}) fusion(f32[31]{0:T(128)} %param.9, s32[46,16]{0,1:T(8,128)S(1)} %get-tuple-element.41, f32[31]{0:T(128)} %param.7, s32[46,16]{0,1:T(8,128)S(1)} %get-tuple-element.40), kind=kLoop, calls=%fused_computation.55 | loop fusion | flops 180320 | bytes 14968 | tf_op jit(solution)/shard_map/reduce_sum | solution.py:51
  2.6 1.3 %select_reduce_fusion.1 = (f32[128,128]{1,0:T(8,128)S(1)}, f32[128,128]{1,0:T(8,128)S(1)}, f32[128,128]{1,0:T(8,128)S(1)}) fusion(s32[128,128]{1,0:T(8,128)S(1)} %get-tuple-element.39, f32[31]{0:T(128)} %param.8, s32[128,128]{1,0:T(8,128)S(1)} %get-tuple-element.38, s32[128,128]{1,0:T(8,128)S(1)} %fusion.38), kind=kLoop, calls=%fused_computation.2 | loop fusion | flops 4521984 | bytes 393340 | tf_op jit(solution)/shard_map/reduce_sum | solution.py:51
  4.0 0.1 maximum_maximum_fusion
  4.1 0.6 convolution_bitcast_fusion
  4.7 0.1 fusion.52
  4.8 3.2 %collective-permute-start.8 = (f32[15,16,256]{2,1,0:T(8,128)S(1)}, f32[15,16,256]{2,1,0:T(8,128)S(1)}, u32[]{:S(2)}, u32[]{:S(2)}) collective-permute-start(f32[15,16,256]{2,1,0:T(8,128)S(1)} %get-tuple-element.24), channel_id=1, source_target_pairs={{0,1},{1,2},{2,3},{4,5},{5,6},{6,7},{8,9},{9,10},{10,11},{12,13},{... | collective-permute-start | bytes 737288 | tf_op jit(solution)/shard_map/ppermute | solution.py:25
  8.0 2.1 %collective-permute-start.9 = (f32[15,16,256]{2,1,0:T(8,128)S(1)}, f32[15,16,256]{2,1,0:T(8,128)S(1)}, u32[]{:S(2)}, u32[]{:S(2)}) collective-permute-start(f32[15,16,256]{2,1,0:T(8,128)S(1)} %get-tuple-element.25), channel_id=1, source_target_pairs={{1,0},{2,1},{3,2},{5,4},{6,5},{7,6},{9,8},{10,9},{11,10},{13,12},{... | collective-permute-start | bytes 737288 | tf_op jit(solution)/shard_map/ppermute | solution.py:26
  10.1 1.9 %collective-permute-start.1 = (f32[15,16,256]{2,1,0:T(8,128)S(1)}, f32[15,16,256]{2,1,0:T(8,128)S(1)}, u32[]{:S(2)}, u32[]{:S(2)}) collective-permute-start(f32[15,16,256]{2,1,0:T(8,128)S(1)} %get-tuple-element.26), channel_id=1, source_target_pairs={{1,0},{2,1},{3,2},{5,4},{6,5},{7,6},{9,8},{10,9},{11,10},{13,12},{... | collective-permute-start | bytes 737288 | tf_op jit(solution)/shard_map/ppermute | solution.py:26
  12.1 3.4 %collective-permute-start = (f32[15,16,256]{2,1,0:T(8,128)S(1)}, f32[15,16,256]{2,1,0:T(8,128)S(1)}, u32[]{:S(2)}, u32[]{:S(2)}) collective-permute-start(f32[15,16,256]{2,1,0:T(8,128)S(1)} %get-tuple-element.27), channel_id=1, source_target_pairs={{0,1},{1,2},{2,3},{4,5},{5,6},{6,7},{8,9},{9,10},{10,11},{12,13},{... | collective-permute-start | bytes 737288 | tf_op jit(solution)/shard_map/ppermute | solution.py:25
  15.4 0.2 slice_reduce_fusion.1
  15.6 0.1 fusion.53
  15.7 0.0 collective-permute-done.8
  15.7 0.7 collective-permute-done.9
  16.4 0.1 pad_maximum_fusion.5
  16.5 0.7 fusion.15
  17.2 4.5 %collective-permute-done.1 = f32[15,16,256]{2,1,0:T(8,128)S(1)} collective-permute-done((f32[15,16,256]{2,1,0:T(8,128)S(1)}, f32[15,16,256]{2,1,0:T(8,128)S(1)}, u32[]{:S(2)}, u32[]{:S(2)}) %collective-permute-start.1) | collective-permute-done | bytes 245792 | tf_op jit(solution)/shard_map/ppermute | solution.py:26
  21.7 0.0 collective-permute-done
  21.7 0.1 pad_maximum_fusion.2
  21.8 0.7 fusion.22
  22.5 0.1 fusion.56
  22.5 4.9 %collective-permute-start.10 = (f32[16,15,256]{2,0,1:T(8,128)S(1)}, f32[16,15,256]{2,0,1:T(8,128)S(1)}, u32[]{:S(2)}, u32[]{:S(2)}) collective-permute-start(f32[16,15,256]{2,0,1:T(8,128)S(1)} %get-tuple-element.34), channel_id=1, source_target_pairs={{0,4},{4,8},{8,12},{12,16},{16,20},{20,24},{24,28},{1,5},{5,9},{9,... | collective-permute-start | bytes 737288 | tf_op jit(solution)/shard_map/ppermute | solution.py:25
  27.4 1.9 %collective-permute-start.11 = (f32[16,15,256]{2,0,1:T(8,128)S(1)}, f32[16,15,256]{2,0,1:T(8,128)S(1)}, u32[]{:S(2)}, u32[]{:S(2)}) collective-permute-start(f32[16,15,256]{2,0,1:T(8,128)S(1)} %get-tuple-element.35), channel_id=1, source_target_pairs={{4,0},{8,4},{12,8},{16,12},{20,16},{24,20},{28,24},{5,1},{9,5},{13... | collective-permute-start | bytes 737288 | tf_op jit(solution)/shard_map/ppermute | solution.py:26
  29.3 0.1 fusion.57
  29.4 0.0 copy-start.1
  29.4 2.7 %collective-permute-start.3 = (f32[16,17,256]{2,0,1:T(8,128)S(1)}, f32[16,17,256]{2,0,1:T(8,128)S(1)}, u32[]{:S(2)}, u32[]{:S(2)}) collective-permute-start(f32[16,17,256]{2,0,1:T(8,128)S(1)} %pad_maximum_fusion.9), channel_id=1, source_target_pairs={{4,0},{8,4},{12,8},{16,12},{20,16},{24,20},{28,24},{5,1},{9,5},{13... | collective-permute-start | bytes 835592 | tf_op jit(solution)/shard_map/ppermute | solution.py:26
  32.2 3.9 %collective-permute-start.2 = (f32[16,17,256]{2,0,1:T(8,128)S(1)}, f32[16,17,256]{2,0,1:T(8,128)S(1)}, u32[]{:S(2)}, u32[]{:S(2)}) collective-permute-start(f32[16,17,256]{2,0,1:T(8,128)S(1)} %pad_maximum_fusion.8), channel_id=1, source_target_pairs={{0,4},{4,8},{8,12},{12,16},{16,20},{20,24},{24,28},{1,5},{5,9},{9,... | collective-permute-start | bytes 835592 | tf_op jit(solution)/shard_map/ppermute | solution.py:25
  36.1 0.0 collective-permute-done.10
  36.1 0.1 pad_maximum_fusion.6
  36.2 0.7 convolution_divide_fusion
  36.9 0.8 %fusion.55 = (f32[15,16,256]{2,1,0:T(8,128)}, f32[15,16,256]{2,1,0:T(8,128)}) fusion(f32[16,16,256]{2,1,0:T(8,128)S(1)} %convolution_divide_fusion), kind=kLoop, calls=%fused_computation.93 | loop fusion | bytes 983040 | tf_op jit(solution)/shard_map/slice | solution.py:20
  37.7 3.2 %collective-permute-start.12 = (f32[15,16,256]{2,1,0:T(8,128)}, f32[15,16,256]{2,1,0:T(8,128)S(1)}, u32[]{:S(2)}, u32[]{:S(2)}) collective-permute-start(f32[15,16,256]{2,1,0:T(8,128)} %get-tuple-element.32), channel_id=1, source_target_pairs={{0,1},{1,2},{2,3},{4,5},{5,6},{6,7},{8,9},{9,10},{10,11},{12,13},{... | collective-permute-start | bytes 737288 | tf_op jit(solution)/shard_map/ppermute | solution.py:25
  40.9 2.1 %collective-permute-start.13 = (f32[15,16,256]{2,1,0:T(8,128)}, f32[15,16,256]{2,1,0:T(8,128)S(1)}, u32[]{:S(2)}, u32[]{:S(2)}) collective-permute-start(f32[15,16,256]{2,1,0:T(8,128)} %get-tuple-element.33), channel_id=1, source_target_pairs={{1,0},{2,1},{3,2},{5,4},{6,5},{7,6},{9,8},{10,9},{11,10},{13,12},{... | collective-permute-start | bytes 737288 | tf_op jit(solution)/shard_map/ppermute | solution.py:26
  43.0 0.0 collective-permute-done.3
  43.0 0.0 collective-permute-done.2
  43.1 0.1 pad_maximum_fusion.3
  43.1 0.7 convolution_divide_fusion.1
  43.9 0.1 reshape.71
  44.0 0.1 reshape.70
  44.1 3.2 %collective-permute-start.4 = (f32[15,16,256]{2,1,0:T(8,128)S(1)}, f32[15,16,256]{2,1,0:T(8,128)S(1)}, u32[]{:S(2)}, u32[]{:S(2)}) collective-permute-start(f32[15,16,256]{2,1,0:T(8,128)S(1)} %get-tuple-element.30), channel_id=1, source_target_pairs={{0,1},{1,2},{2,3},{4,5},{5,6},{6,7},{8,9},{9,10},{10,11},{12,13},{... | collective-permute-start | bytes 737288 | tf_op jit(solution)/shard_map/ppermute | solution.py:25
  47.3 2.1 %collective-permute-start.5 = (f32[15,16,256]{2,1,0:T(8,128)S(1)}, f32[15,16,256]{2,1,0:T(8,128)S(1)}, u32[]{:S(2)}, u32[]{:S(2)}) collective-permute-start(f32[15,16,256]{2,1,0:T(8,128)S(1)} %get-tuple-element.31), channel_id=1, source_target_pairs={{1,0},{2,1},{3,2},{5,4},{6,5},{7,6},{9,8},{10,9},{11,10},{13,12},{... | collective-permute-start | bytes 737288 | tf_op jit(solution)/shard_map/ppermute | solution.py:26
  49.4 0.0 collective-permute-done.12
  49.4 0.8 %collective-permute-done.13 = f32[15,16,256]{2,1,0:T(8,128)S(1)} collective-permute-done((f32[15,16,256]{2,1,0:T(8,128)}, f32[15,16,256]{2,1,0:T(8,128)S(1)}, u32[]{:S(2)}, u32[]{:S(2)}) %collective-permute-start.13) | collective-permute-done | bytes 245792 | tf_op jit(solution)/shard_map/ppermute | solution.py:26
  50.2 0.1 pad_maximum_fusion.7
  50.3 0.7 fusion.12
  51.0 1.9 %collective-permute-start.15 = (f32[16,16,256]{2,0,1:T(8,128)S(1)}, f32[16,16,256]{2,0,1:T(8,128)S(1)}, u32[]{:S(2)}, u32[]{:S(2)}) collective-permute-start(f32[16,16,256]{2,0,1:T(8,128)S(1)} %fusion.12), channel_id=1, source_target_pairs={{4,0},{8,4},{12,8},{16,12},{20,16},{24,20},{28,24},{5,1},{9,5},{13... | collective-permute-start | bytes 786440 | tf_op jit(solution)/shard_map/ppermute | solution.py:26
  52.9 4.5 %collective-permute-start.14 = (f32[16,16,256]{2,0,1:T(8,128)S(1)}, f32[16,16,256]{2,0,1:T(8,128)S(1)}, u32[]{:S(2)}, u32[]{:S(2)}) collective-permute-start(f32[16,16,256]{2,0,1:T(8,128)S(1)} %fusion.12), channel_id=1, source_target_pairs={{0,4},{4,8},{8,12},{12,16},{16,20},{20,24},{24,28},{1,5},{5,9},{9,... | collective-permute-start | bytes 786440 | tf_op jit(solution)/shard_map/ppermute | solution.py:25
  57.5 0.0 collective-permute-done.5
  57.5 0.1 pad_maximum_fusion.4
  57.6 0.7 fusion.19
  58.3 1.9 %collective-permute-start.7 = (f32[16,16,256]{2,0,1:T(8,128)S(1)}, f32[16,16,256]{2,0,1:T(8,128)S(1)}, u32[]{:S(2)}, u32[]{:S(2)}) collective-permute-start(f32[16,16,256]{2,0,1:T(8,128)S(1)} %fusion.19), channel_id=1, source_target_pairs={{4,0},{8,4},{12,8},{16,12},{20,16},{24,20},{28,24},{5,1},{9,5},{13... | collective-permute-start | bytes 786440 | tf_op jit(solution)/shard_map/ppermute | solution.py:26
  60.2 4.5 %collective-permute-start.6 = (f32[16,16,256]{2,0,1:T(8,128)S(1)}, f32[16,16,256]{2,0,1:T(8,128)S(1)}, u32[]{:S(2)}, u32[]{:S(2)}) collective-permute-start(f32[16,16,256]{2,0,1:T(8,128)S(1)} %fusion.19), channel_id=1, source_target_pairs={{0,4},{4,8},{8,12},{12,16},{16,20},{20,24},{24,28},{1,5},{5,9},{9,... | collective-permute-start | bytes 786440 | tf_op jit(solution)/shard_map/ppermute | solution.py:25
  64.8 0.1 pad_maximum_fusion.1
  64.8 0.7 fusion.10
  65.6 3.9 %collective-permute-done.7 = f32[16,16,256]{2,0,1:T(8,128)S(1)} collective-permute-done((f32[16,16,256]{2,0,1:T(8,128)S(1)}, f32[16,16,256]{2,0,1:T(8,128)S(1)}, u32[]{:S(2)}, u32[]{:S(2)}) %collective-permute-start.7) | collective-permute-done | bytes 262176 | tf_op jit(solution)/shard_map/ppermute | solution.py:26
  69.5 0.1 pad_maximum_fusion
  69.6 0.7 fusion.17
  70.3 0.8 %maximum_multiply_fusion = f32[16,18,512]{2,1,0:T(8,128)S(1)} fusion(f32[16,1,512]{2,1,0:T(1,128)S(1)} %reshape.71, f32[16,16,512]{2,1,0:T(8,128)S(1)} %copy-done, f32[16,1,512]{2,1,0:T(1,128)S(1)} %reshape.70, f32[512,512]{1,0:T(8,128)S(1)} %maximum_maximum_fusion, f32[16,18,256]{2,1,0:T(8,128)S(1)} %fusion.10, f32[16,18,256]{2,1,0:T(8,128)S(1)} %fusion.17), kind=kOutput, calls=%fused_computation.13 | convolution fusion | flops 453574656 | bytes 2818048 | tf_op jit(solution)/shard_map/dot_general | solution.py:86
  71.1 0.9 %slice.114 = f32[16,16,512]{2,1,0:T(8,128)} slice(f32[16,18,512]{2,1,0:T(8,128)S(1)} %maximum_multiply_fusion), slice={[0:16], [1:17], [0:512]} | slice | bytes 1048576 | tf_op jit(solution)/shard_map/slice | solution.py:150
  72.0 0.5 fusion.24
  72.5 0.9 %fusion.39 = f32[16,8,256]{2,1,0:T(8,128)} fusion(f32[16,18,256]{2,1,0:T(8,128)S(1)} %fusion.24, f32[8,18]{1,0:T(8,128)S(1)} %bitcast.44), kind=kOutput, calls=%fused_computation.68 | convolution fusion | flops 3538944 | bytes 426560 | tf_op jit(solution)/shard_map/dot_general | solution.py:94
  (26 shorter events, 0.3 us)
Async XLA Ops:
  1.7 2.4 %copy-start = (f32[16,16,512]{2,1,0:T(8,128)S(1)}, f32[16,16,512]{2,1,0:T(8,128)}, u32[]{:S(2)}) copy-start(f32[16,16,512]{2,1,0:T(8,128)} %param.5) | copy-start | bytes 1572868
  4.8 10.9 %collective-permute-start.8 = (f32[15,16,256]{2,1,0:T(8,128)S(1)}, f32[15,16,256]{2,1,0:T(8,128)S(1)}, u32[]{:S(2)}, u32[]{:S(2)}) collective-permute-start(f32[15,16,256]{2,1,0:T(8,128)S(1)} %get-tuple-element.24), channel_id=1, source_target_pairs={{0,1},{1,2},{2,3},{4,5},{5,6},{6,7},{8,9},{9,10},{10,11},{12,13},{... | collective-permute-start | bytes 737288 | tf_op jit(solution)/shard_map/ppermute | solution.py:25
  8.0 8.4 %collective-permute-start.9 = (f32[15,16,256]{2,1,0:T(8,128)S(1)}, f32[15,16,256]{2,1,0:T(8,128)S(1)}, u32[]{:S(2)}, u32[]{:S(2)}) collective-permute-start(f32[15,16,256]{2,1,0:T(8,128)S(1)} %get-tuple-element.25), channel_id=1, source_target_pairs={{1,0},{2,1},{3,2},{5,4},{6,5},{7,6},{9,8},{10,9},{11,10},{13,12},{... | collective-permute-start | bytes 737288 | tf_op jit(solution)/shard_map/ppermute | solution.py:26
  10.1 11.6 %collective-permute-start.1 = (f32[15,16,256]{2,1,0:T(8,128)S(1)}, f32[15,16,256]{2,1,0:T(8,128)S(1)}, u32[]{:S(2)}, u32[]{:S(2)}) collective-permute-start(f32[15,16,256]{2,1,0:T(8,128)S(1)} %get-tuple-element.26), channel_id=1, source_target_pairs={{1,0},{2,1},{3,2},{5,4},{6,5},{7,6},{9,8},{10,9},{11,10},{13,12},{... | collective-permute-start | bytes 737288 | tf_op jit(solution)/shard_map/ppermute | solution.py:26
  12.1 9.6 %collective-permute-start = (f32[15,16,256]{2,1,0:T(8,128)S(1)}, f32[15,16,256]{2,1,0:T(8,128)S(1)}, u32[]{:S(2)}, u32[]{:S(2)}) collective-permute-start(f32[15,16,256]{2,1,0:T(8,128)S(1)} %get-tuple-element.27), channel_id=1, source_target_pairs={{0,1},{1,2},{2,3},{4,5},{5,6},{6,7},{8,9},{9,10},{10,11},{12,13},{... | collective-permute-start | bytes 737288 | tf_op jit(solution)/shard_map/ppermute | solution.py:25
  22.5 13.5 %collective-permute-start.10 = (f32[16,15,256]{2,0,1:T(8,128)S(1)}, f32[16,15,256]{2,0,1:T(8,128)S(1)}, u32[]{:S(2)}, u32[]{:S(2)}) collective-permute-start(f32[16,15,256]{2,0,1:T(8,128)S(1)} %get-tuple-element.34), channel_id=1, source_target_pairs={{0,4},{4,8},{8,12},{12,16},{16,20},{20,24},{24,28},{1,5},{5,9},{9,... | collective-permute-start | bytes 737288 | tf_op jit(solution)/shard_map/ppermute | solution.py:25
  27.4 8.7 %collective-permute-start.11 = (f32[16,15,256]{2,0,1:T(8,128)S(1)}, f32[16,15,256]{2,0,1:T(8,128)S(1)}, u32[]{:S(2)}, u32[]{:S(2)}) collective-permute-start(f32[16,15,256]{2,0,1:T(8,128)S(1)} %get-tuple-element.35), channel_id=1, source_target_pairs={{4,0},{8,4},{12,8},{16,12},{20,16},{24,20},{28,24},{5,1},{9,5},{13... | collective-permute-start | bytes 737288 | tf_op jit(solution)/shard_map/ppermute | solution.py:26
  29.4 6.7 %copy-start.1 = (f32[16,16,512]{2,1,0:T(8,128)S(1)}, f32[16,16,512]{2,1,0:T(8,128)}, u32[]{:S(2)}) copy-start(f32[16,16,512]{2,1,0:T(8,128)} %param.6) | copy-start | bytes 1572868
  29.4 13.6 %collective-permute-start.3 = (f32[16,17,256]{2,0,1:T(8,128)S(1)}, f32[16,17,256]{2,0,1:T(8,128)S(1)}, u32[]{:S(2)}, u32[]{:S(2)}) collective-permute-start(f32[16,17,256]{2,0,1:T(8,128)S(1)} %pad_maximum_fusion.9), channel_id=1, source_target_pairs={{4,0},{8,4},{12,8},{16,12},{20,16},{24,20},{28,24},{5,1},{9,5},{13... | collective-permute-start | bytes 835592 | tf_op jit(solution)/shard_map/ppermute | solution.py:26
  32.2 10.9 %collective-permute-start.2 = (f32[16,17,256]{2,0,1:T(8,128)S(1)}, f32[16,17,256]{2,0,1:T(8,128)S(1)}, u32[]{:S(2)}, u32[]{:S(2)}) collective-permute-start(f32[16,17,256]{2,0,1:T(8,128)S(1)} %pad_maximum_fusion.8), channel_id=1, source_target_pairs={{0,4},{4,8},{8,12},{12,16},{16,20},{20,24},{24,28},{1,5},{5,9},{9,... | collective-permute-start | bytes 835592 | tf_op jit(solution)/shard_map/ppermute | solution.py:25
  37.7 11.7 %collective-permute-start.12 = (f32[15,16,256]{2,1,0:T(8,128)}, f32[15,16,256]{2,1,0:T(8,128)S(1)}, u32[]{:S(2)}, u32[]{:S(2)}) collective-permute-start(f32[15,16,256]{2,1,0:T(8,128)} %get-tuple-element.32), channel_id=1, source_target_pairs={{0,1},{1,2},{2,3},{4,5},{5,6},{6,7},{8,9},{9,10},{10,11},{12,13},{... | collective-permute-start | bytes 737288 | tf_op jit(solution)/shard_map/ppermute | solution.py:25
  40.9 9.3 %collective-permute-start.13 = (f32[15,16,256]{2,1,0:T(8,128)}, f32[15,16,256]{2,1,0:T(8,128)S(1)}, u32[]{:S(2)}, u32[]{:S(2)}) collective-permute-start(f32[15,16,256]{2,1,0:T(8,128)} %get-tuple-element.33), channel_id=1, source_target_pairs={{1,0},{2,1},{3,2},{5,4},{6,5},{7,6},{9,8},{10,9},{11,10},{13,12},{... | collective-permute-start | bytes 737288 | tf_op jit(solution)/shard_map/ppermute | solution.py:26
  44.1 13.4 %collective-permute-start.4 = (f32[15,16,256]{2,1,0:T(8,128)S(1)}, f32[15,16,256]{2,1,0:T(8,128)S(1)}, u32[]{:S(2)}, u32[]{:S(2)}) collective-permute-start(f32[15,16,256]{2,1,0:T(8,128)S(1)} %get-tuple-element.30), channel_id=1, source_target_pairs={{0,1},{1,2},{2,3},{4,5},{5,6},{6,7},{8,9},{9,10},{10,11},{12,13},{... | collective-permute-start | bytes 737288 | tf_op jit(solution)/shard_map/ppermute | solution.py:25
  47.3 10.2 %collective-permute-start.5 = (f32[15,16,256]{2,1,0:T(8,128)S(1)}, f32[15,16,256]{2,1,0:T(8,128)S(1)}, u32[]{:S(2)}, u32[]{:S(2)}) collective-permute-start(f32[15,16,256]{2,1,0:T(8,128)S(1)} %get-tuple-element.31), channel_id=1, source_target_pairs={{1,0},{2,1},{3,2},{5,4},{6,5},{7,6},{9,8},{10,9},{11,10},{13,12},{... | collective-permute-start | bytes 737288 | tf_op jit(solution)/shard_map/ppermute | solution.py:26
  51.0 13.7 %collective-permute-start.15 = (f32[16,16,256]{2,0,1:T(8,128)S(1)}, f32[16,16,256]{2,0,1:T(8,128)S(1)}, u32[]{:S(2)}, u32[]{:S(2)}) collective-permute-start(f32[16,16,256]{2,0,1:T(8,128)S(1)} %fusion.12), channel_id=1, source_target_pairs={{4,0},{8,4},{12,8},{16,12},{20,16},{24,20},{28,24},{5,1},{9,5},{13... | collective-permute-start | bytes 786440 | tf_op jit(solution)/shard_map/ppermute | solution.py:26
  52.9 11.8 %collective-permute-start.14 = (f32[16,16,256]{2,0,1:T(8,128)S(1)}, f32[16,16,256]{2,0,1:T(8,128)S(1)}, u32[]{:S(2)}, u32[]{:S(2)}) collective-permute-start(f32[16,16,256]{2,0,1:T(8,128)S(1)} %fusion.12), channel_id=1, source_target_pairs={{0,4},{4,8},{8,12},{12,16},{16,20},{20,24},{24,28},{1,5},{5,9},{9,... | collective-permute-start | bytes 786440 | tf_op jit(solution)/shard_map/ppermute | solution.py:25
  58.3 11.2 %collective-permute-start.7 = (f32[16,16,256]{2,0,1:T(8,128)S(1)}, f32[16,16,256]{2,0,1:T(8,128)S(1)}, u32[]{:S(2)}, u32[]{:S(2)}) collective-permute-start(f32[16,16,256]{2,0,1:T(8,128)S(1)} %fusion.19), channel_id=1, source_target_pairs={{4,0},{8,4},{12,8},{16,12},{20,16},{24,20},{28,24},{5,1},{9,5},{13... | collective-permute-start | bytes 786440 | tf_op jit(solution)/shard_map/ppermute | solution.py:26
  60.2 9.3 %collective-permute-start.6 = (f32[16,16,256]{2,0,1:T(8,128)S(1)}, f32[16,16,256]{2,0,1:T(8,128)S(1)}, u32[]{:S(2)}, u32[]{:S(2)}) collective-permute-start(f32[16,16,256]{2,0,1:T(8,128)S(1)} %fusion.19), channel_id=1, source_target_pairs={{0,4},{4,8},{8,12},{12,16},{16,20},{20,24},{24,28},{1,5},{5,9},{9,... | collective-permute-start | bytes 786440 | tf_op jit(solution)/shard_map/ppermute | solution.py:25

commit v7 on v6

--- a/solution.py
+++ b/solution.py
@@ -109,7 +109,7 @@
 
     rows_ext = row_count + 2 * reach
     planes_ext = plane_count + 2 * reach
-    bands = lax.optimization_barrier((
+    bands = [
         band_square(kernel_columns, col_count, reach),
         band(kernel_rows, rows_ext, row_count, 1, 0),
         band(kernel_planes, planes_ext, plane_count, 1, 0),
@@ -117,7 +117,8 @@
         band(kernel_rows, rows_ext + 2, row_count + 2, -1, 2 * reach),
         pyramid_matrix(col_count, col_count // 2, 1),
         pyramid_matrix(row_count + 2, row_count // 2, 0),
-    ))
+    ]
+    bands = [lax.optimization_barrier(matrix) for matrix in bands]
     col_band, row_fwd, plane_fwd, plane_back, row_back, pyr_cols, pyr_rows = bands
 
     filtered = along_columns(estimate, col_band)
@@ -140,14 +141,18 @@
         quotient = seen / blurred
         spread = along_planes(halo(quotient, "slab", 0, reach, reach), plane_back)
         spread = along_rows(halo(spread, "tile", 1, reach + 1, reach + 1), row_back)
-        spreads.append(spread)
-    correction = along_columns(jnp.concatenate(spreads, axis=2), col_band, transpose=True)
+        cols_of = lax.slice_in_dim(col_band, index * chunk, (index + 1) * chunk, axis=1)
+        share = along_columns(spread, cols_of, transpose=True)
+        spreads.append(share)
+    correction = spreads[0]
+    for share in spreads[1:]:
+        correction = correction + share
     unfold = (planes, 1, col_count)
     edge_rows = jnp.concatenate(
         [carried[0].reshape(unfold), estimate, carried[1].reshape(unfold)], axis=1
     )
     new_ext = edge_rows * correction
-    new_estimate = lax.slice_in_dim(new_ext, 1, row_count + 1, axis=1)
+    new_estimate = estimate * lax.slice_in_dim(correction, 1, row_count + 1, axis=1)
 
     halved = along_columns(new_ext, pyr_cols)
     pyramid_level = along_rows(halved, pyr_rows)

time: 74.1 us -> 72.6 us (0.980)
  waiting for transfers between devices: 10 us -> 5.82 us
  starting transfers between devices: 47.5 us -> 49.4 us
    ppermute x8, waiting for transfers between devices: 9.98 us -> 2.95 us  [halo(): got_down = lax.ppermute(send_down, axis, down)]
    ppermute x8, waiting for transfers between devices: 0.02 us -> 2.87 us  [halo(): got_up = lax.ppermute(send_up, axis, up)]
    ppermute x8, starting transfers between devices: 30.8 us -> 32.5 us  [halo(): got_up = lax.ppermute(send_up, axis, up)]
    reduce_sum x3, other arithmetic: 3.01 us -> 1.67 us  [band(): return jnp.sum(picked, axis=2)]
    concatenate x8, other arithmetic: 0.41 us -> 1.48 us  [halo(): joined = jnp.concatenate(pieces_before + [shard] + pieces_after, axis=dim)]
    mul x0 -> x1, other arithmetic: none -> 0.92 us  [shards(): estimate * lax.slice_in_dim(correction, 1, row_count + 1, axis=1)]
    slice x1 -> x0, local copies, waits for them, and re-layouts: 0.86 us -> none  [shards(): new_estimate = lax.slice_in_dim(new_ext, 1, row_count + 1, axis=1)]
    slice x5, local copies, waits for them, and re-layouts: 1.09 us -> 1.89 us  [halo(): send_up = lax.slice_in_dim(shard, start, length, axis=dim)]
  transfers between devices with their start and end apart: 16 -> 16, of which waited for: 4 -> 3; matrix products, arithmetic and copies ran while one was open for 8% -> 13% of each run, Pallas kernels for 0% -> 0%
where the time goes in v7:
time: 72.6 us; the launch traced here: 72.1 us
  starting transfers between devices  49.4 us (68%)
  matrix products  8.76 us (12%)
  waiting for transfers between devices  5.82 us (8%)
  other arithmetic  4.45 us (6%)
  local copies, waits for them, and re-layouts  2.37 us (3%)
  between operations  1.27 us (2%)
    ppermute x8, starting transfers between devices, halo(): got_up = lax.ppermute(send_up, axis, up)  32.5 us
    ppermute x8, starting transfers between devices, halo(): got_down = lax.ppermute(send_down, axis, down)  16.9 us
    dot_general x5, matrix products, along_rows(): lax.dot_general(left, volume, (((2,), (1,)), ((0,), (0,))), precision=PRE...  3.75 us
    ppermute x8, waiting for transfers between devices, halo(): got_down = lax.ppermute(send_down, axis, down)  2.95 us
    ppermute x8, waiting for transfers between devices, halo(): got_up = lax.ppermute(send_up, axis, up)  2.87 us
    dot_general x4, matrix products, along_planes(): lax.dot_general(matrix.T, volume, (((1,), (0,)), ((), ())), precision=PRE...  2.8 us
    dot_general x4, matrix products, along_columns(): lax.dot_general(volume, matrix, (((2,), (contract,)), ((), ())), precisio...  2.21 us
    slice x5, local copies, waits for them, and re-layouts, halo(): send_up = lax.slice_in_dim(shard, start, length, axis=dim)  1.89 us
  transfers between devices with their start and end apart: 16, of which 3 were waited for; matrix products, arithmetic and copies ran while one was open for 13% of the time, Pallas kernels for 0%

profile of v7, /device:TPU:11, one launch (start us, length us, event | category | flops | bytes accessed | tf_op | source)
XLA Modules:
  0.0 72.1 jit_solution(3996600826441552105)
XLA Ops:
  0.6 0.0 copy-start
  0.7 1.4 %select_reduce_fusion.1 = (f32[128,128]{1,0:T(8,128)S(1)}, f32[128,128]{1,0:T(8,128)S(1)}, f32[128,128]{1,0:T(8,128)S(1)}) fusion(s32[128,128]{1,0:T(8,128)S(1)} %get-tuple-element.25, f32[31]{0:T(128)} %param.8, s32[128,128]{1,0:T(8,128)S(1)} %get-tuple-element.24, s32[128,128]{1,0:T(8,128)S(1)} %fusion.32), kind=kLoop, calls=%fused_computation.2 | loop fusion | flops 4521984 | bytes 393340 | tf_op jit(solution)/shard_map/reduce_sum | solution.py:51
  2.1 0.1 maximum_maximum_fusion
  2.2 0.6 convolution_bitcast_fusion
  2.8 0.0 copy-start.2
  2.8 0.0 copy-start.3
  2.8 0.1 fusion.48
  2.9 3.2 %collective-permute-start.8 = (f32[15,16,256]{2,1,0:T(8,128)S(1)}, f32[15,16,256]{2,1,0:T(8,128)S(1)}, u32[]{:S(2)}, u32[]{:S(2)}) collective-permute-start(f32[15,16,256]{2,1,0:T(8,128)S(1)} %get-tuple-element.10), channel_id=1, source_target_pairs={{0,1},{1,2},{2,3},{4,5},{5,6},{6,7},{8,9},{9,10},{10,11},{12,13},{... | collective-permute-start | bytes 737288 | tf_op jit(solution)/shard_map/ppermute | solution.py:25
  6.2 2.1 %collective-permute-start.9 = (f32[15,16,256]{2,1,0:T(8,128)S(1)}, f32[15,16,256]{2,1,0:T(8,128)S(1)}, u32[]{:S(2)}, u32[]{:S(2)}) collective-permute-start(f32[15,16,256]{2,1,0:T(8,128)S(1)} %get-tuple-element.11), channel_id=1, source_target_pairs={{1,0},{2,1},{3,2},{5,4},{6,5},{7,6},{9,8},{10,9},{11,10},{13,12},{... | collective-permute-start | bytes 737288 | tf_op jit(solution)/shard_map/ppermute | solution.py:26
  8.3 3.2 %collective-permute-start = (f32[15,16,256]{2,1,0:T(8,128)S(1)}, f32[15,16,256]{2,1,0:T(8,128)S(1)}, u32[]{:S(2)}, u32[]{:S(2)}) collective-permute-start(f32[15,16,256]{2,1,0:T(8,128)S(1)} %get-tuple-element.13), channel_id=1, source_target_pairs={{0,1},{1,2},{2,3},{4,5},{5,6},{6,7},{8,9},{9,10},{10,11},{12,13},{... | collective-permute-start | bytes 737288 | tf_op jit(solution)/shard_map/ppermute | solution.py:25
  11.5 2.1 %collective-permute-start.1 = (f32[15,16,256]{2,1,0:T(8,128)S(1)}, f32[15,16,256]{2,1,0:T(8,128)S(1)}, u32[]{:S(2)}, u32[]{:S(2)}) collective-permute-start(f32[15,16,256]{2,1,0:T(8,128)S(1)} %get-tuple-element.12), channel_id=1, source_target_pairs={{1,0},{2,1},{3,2},{5,4},{6,5},{7,6},{9,8},{10,9},{11,10},{13,12},{... | collective-permute-start | bytes 737288 | tf_op jit(solution)/shard_map/ppermute | solution.py:26
  13.6 0.2 slice_reduce_fusion.1
  13.8 0.2 select_select_fusion
  13.9 0.1 select_select_fusion.1
  14.0 0.2 select_reduce_fusion.5
  14.2 0.1 select_reduce_fusion.3
  14.3 0.1 fusion.49
  14.4 0.0 collective-permute-done.8
  14.4 0.1 collective-permute-done.9
  14.6 0.1 pad_maximum_fusion.5
  14.6 0.7 fusion.11
  15.4 4.9 %collective-permute-start.10 = (f32[16,15,256]{2,0,1:T(8,128)S(1)}, f32[16,15,256]{2,0,1:T(8,128)S(1)}, u32[]{:S(2)}, u32[]{:S(2)}) collective-permute-start(f32[16,15,256]{2,0,1:T(8,128)S(1)} %get-tuple-element.18), channel_id=1, source_target_pairs={{0,4},{4,8},{8,12},{12,16},{16,20},{20,24},{24,28},{1,5},{5,9},{9,... | collective-permute-start | bytes 737288 | tf_op jit(solution)/shard_map/ppermute | solution.py:25
  20.3 1.9 %collective-permute-start.11 = (f32[16,15,256]{2,0,1:T(8,128)S(1)}, f32[16,15,256]{2,0,1:T(8,128)S(1)}, u32[]{:S(2)}, u32[]{:S(2)}) collective-permute-start(f32[16,15,256]{2,0,1:T(8,128)S(1)} %get-tuple-element.19), channel_id=1, source_target_pairs={{4,0},{8,4},{12,8},{16,12},{20,16},{24,20},{28,24},{5,1},{9,5},{13... | collective-permute-start | bytes 737288 | tf_op jit(solution)/shard_map/ppermute | solution.py:26
  22.2 0.0 collective-permute-done.1
  22.2 0.1 pad_maximum_fusion.2
  22.3 0.7 fusion.18
  23.1 0.0 copy-start.1
  23.1 4.7 %collective-permute-start.2 = (f32[16,17,256]{2,0,1:T(8,128)S(1)}, f32[16,17,256]{2,0,1:T(8,128)S(1)}, u32[]{:S(2)}, u32[]{:S(2)}) collective-permute-start(f32[16,17,256]{2,0,1:T(8,128)S(1)} %pad_maximum_fusion.8), channel_id=1, source_target_pairs={{0,4},{4,8},{8,12},{12,16},{16,20},{20,24},{24,28},{1,5},{5,9},{9,... | collective-permute-start | bytes 835592 | tf_op jit(solution)/shard_map/ppermute | solution.py:25
  27.8 1.9 %collective-permute-start.3 = (f32[16,17,256]{2,0,1:T(8,128)S(1)}, f32[16,17,256]{2,0,1:T(8,128)S(1)}, u32[]{:S(2)}, u32[]{:S(2)}) collective-permute-start(f32[16,17,256]{2,0,1:T(8,128)S(1)} %pad_maximum_fusion.9), channel_id=1, source_target_pairs={{4,0},{8,4},{12,8},{16,12},{20,16},{24,20},{28,24},{5,1},{9,5},{13... | collective-permute-start | bytes 835592 | tf_op jit(solution)/shard_map/ppermute | solution.py:26
  29.7 0.0 collective-permute-done.10
  29.7 0.1 pad_maximum_fusion.6
  29.8 0.7 convolution_divide_fusion
  30.5 0.8 %fusion.50 = (f32[15,16,256]{2,1,0:T(8,128)}, f32[15,16,256]{2,1,0:T(8,128)}) fusion(f32[16,16,256]{2,1,0:T(8,128)S(1)} %convolution_divide_fusion), kind=kLoop, calls=%fused_computation.96 | loop fusion | bytes 983040 | tf_op jit(solution)/shard_map/slice | solution.py:20
  31.4 3.2 %collective-permute-start.12 = (f32[15,16,256]{2,1,0:T(8,128)}, f32[15,16,256]{2,1,0:T(8,128)S(1)}, u32[]{:S(2)}, u32[]{:S(2)}) collective-permute-start(f32[15,16,256]{2,1,0:T(8,128)} %get-tuple-element.16), channel_id=1, source_target_pairs={{0,1},{1,2},{2,3},{4,5},{5,6},{6,7},{8,9},{9,10},{10,11},{12,13},{... | collective-permute-start | bytes 737288 | tf_op jit(solution)/shard_map/ppermute | solution.py:25
  34.6 2.1 %collective-permute-start.13 = (f32[15,16,256]{2,1,0:T(8,128)}, f32[15,16,256]{2,1,0:T(8,128)S(1)}, u32[]{:S(2)}, u32[]{:S(2)}) collective-permute-start(f32[15,16,256]{2,1,0:T(8,128)} %get-tuple-element.17), channel_id=1, source_target_pairs={{1,0},{2,1},{3,2},{5,4},{6,5},{7,6},{9,8},{10,9},{11,10},{13,12},{... | collective-permute-start | bytes 737288 | tf_op jit(solution)/shard_map/ppermute | solution.py:26
  36.7 0.0 collective-permute-done.2
  36.7 0.1 pad_maximum_fusion.3
  36.8 0.7 convolution_divide_fusion.1
  37.5 0.8 %fusion.52 = (f32[15,16,256]{2,1,0:T(8,128)}, f32[15,16,256]{2,1,0:T(8,128)}) fusion(f32[16,16,256]{2,1,0:T(8,128)S(1)} %convolution_divide_fusion.1), kind=kLoop, calls=%fused_computation.98 | loop fusion | bytes 983040 | tf_op jit(solution)/shard_map/slice | solution.py:20
  38.3 3.2 %collective-permute-start.4 = (f32[15,16,256]{2,1,0:T(8,128)}, f32[15,16,256]{2,1,0:T(8,128)}, u32[]{:S(2)}, u32[]{:S(2)}) collective-permute-start(f32[15,16,256]{2,1,0:T(8,128)} %get-tuple-element.20), channel_id=1, source_target_pairs={{0,1},{1,2},{2,3},{4,5},{5,6},{6,7},{8,9},{9,10},{10,11},{12,13},{... | collective-permute-start | bytes 737288 | tf_op jit(solution)/shard_map/ppermute | solution.py:25
  41.5 2.8 %collective-permute-start.5 = (f32[15,16,256]{2,1,0:T(8,128)}, f32[15,16,256]{2,1,0:T(8,128)}, u32[]{:S(2)}, u32[]{:S(2)}) collective-permute-start(f32[15,16,256]{2,1,0:T(8,128)} %get-tuple-element.21), channel_id=1, source_target_pairs={{1,0},{2,1},{3,2},{5,4},{6,5},{7,6},{9,8},{10,9},{11,10},{13,12},{... | collective-permute-start | bytes 737288 | tf_op jit(solution)/shard_map/ppermute | solution.py:26
  44.3 0.1 reshape.72
  44.4 0.1 reshape.73
  44.5 0.0 collective-permute-done.12
  44.5 0.1 pad_maximum_fusion.7
  44.6 0.7 fusion.8
  45.3 5.7 %collective-permute-start.14 = (f32[16,16,256]{2,0,1:T(8,128)S(1)}, f32[16,16,256]{2,0,1:T(8,128)S(1)}, u32[]{:S(2)}, u32[]{:S(2)}) collective-permute-start(f32[16,16,256]{2,0,1:T(8,128)S(1)} %fusion.8), channel_id=1, source_target_pairs={{0,4},{4,8},{8,12},{12,16},{16,20},{20,24},{24,28},{1,5},{5,9},{9,... | collective-permute-start | bytes 786440 | tf_op jit(solution)/shard_map/ppermute | solution.py:25
  51.0 1.9 %collective-permute-start.15 = (f32[16,16,256]{2,0,1:T(8,128)S(1)}, f32[16,16,256]{2,0,1:T(8,128)S(1)}, u32[]{:S(2)}, u32[]{:S(2)}) collective-permute-start(f32[16,16,256]{2,0,1:T(8,128)S(1)} %fusion.8), channel_id=1, source_target_pairs={{4,0},{8,4},{12,8},{16,12},{20,16},{24,20},{28,24},{5,1},{9,5},{13... | collective-permute-start | bytes 786440 | tf_op jit(solution)/shard_map/ppermute | solution.py:26
  52.9 0.0 collective-permute-done.5
  52.9 1.1 %pad_maximum_fusion.4 = f32[46,16,256]{2,1,0:T(8,128)S(1)} fusion(f32[15,16,256]{2,1,0:T(8,128)} %collective-permute-done.5, f32[16,16,256]{2,1,0:T(8,128)S(1)} %convolution_divide_fusion.1, f32[15,16,256]{2,1,0:T(8,128)} %collective-permute-done.4), kind=kLoop, calls=%fused_computation.36 | loop fusion | flops 376832 | bytes 1507328 | tf_op jit(solution)/shard_map/concatenate | solution.py:40
  54.0 0.7 fusion.15
  54.7 4.5 %collective-permute-start.6 = (f32[16,16,256]{2,0,1:T(8,128)S(1)}, f32[16,16,256]{2,0,1:T(8,128)S(1)}, u32[]{:S(2)}, u32[]{:S(2)}) collective-permute-start(f32[16,16,256]{2,0,1:T(8,128)S(1)} %fusion.15), channel_id=1, source_target_pairs={{0,4},{4,8},{8,12},{12,16},{16,20},{20,24},{24,28},{1,5},{5,9},{9,... | collective-permute-start | bytes 786440 | tf_op jit(solution)/shard_map/ppermute | solution.py:25
  59.3 2.1 %collective-permute-start.7 = (f32[16,16,256]{2,0,1:T(8,128)S(1)}, f32[16,16,256]{2,0,1:T(8,128)S(1)}, u32[]{:S(2)}, u32[]{:S(2)}) collective-permute-start(f32[16,16,256]{2,0,1:T(8,128)S(1)} %fusion.15), channel_id=1, source_target_pairs={{4,0},{8,4},{12,8},{16,12},{20,16},{24,20},{28,24},{5,1},{9,5},{13... | collective-permute-start | bytes 786440 | tf_op jit(solution)/shard_map/ppermute | solution.py:26
  61.4 0.1 pad_maximum_fusion.1
  61.5 0.7 %fusion.6 = f32[16,18,256]{2,1,0:T(8,128)S(1)} fusion(f32[16,48,256]{2,0,1:T(8,128)S(1)} %pad_maximum_fusion.1, f32[18,48]{1,0:T(8,128)S(1)} %bitcast.43), kind=kOutput, calls=%fused_computation.20 | convolution fusion | flops 21233664 | bytes 1084800 | tf_op jit(solution)/shard_map/dot_general | solution.py:94
  62.2 2.9 %collective-permute-done.6 = f32[16,16,256]{2,0,1:T(8,128)S(1)} collective-permute-done((f32[16,16,256]{2,0,1:T(8,128)S(1)}, f32[16,16,256]{2,0,1:T(8,128)S(1)}, u32[]{:S(2)}, u32[]{:S(2)}) %collective-permute-start.6) | collective-permute-done | bytes 262176 | tf_op jit(solution)/shard_map/ppermute | solution.py:25
  65.1 2.8 %collective-permute-done.7 = f32[16,16,256]{2,0,1:T(8,128)S(1)} collective-permute-done((f32[16,16,256]{2,0,1:T(8,128)S(1)}, f32[16,16,256]{2,0,1:T(8,128)S(1)}, u32[]{:S(2)}, u32[]{:S(2)}) %collective-permute-start.7) | collective-permute-done | bytes 262176 | tf_op jit(solution)/shard_map/ppermute | solution.py:26
  67.9 0.1 pad_maximum_fusion
  67.9 0.7 %fusion.13 = f32[16,18,256]{2,1,0:T(8,128)S(1)} fusion(f32[16,48,256]{2,0,1:T(8,128)S(1)} %pad_maximum_fusion, f32[18,48]{1,0:T(8,128)S(1)} %bitcast.44), kind=kOutput, calls=%fused_computation.27 | convolution fusion | flops 21233664 | bytes 1084800 | tf_op jit(solution)/shard_map/dot_general | solution.py:94
  68.7 0.5 fusion.20
  69.2 0.5 convolution_add_fusion
  69.7 0.9 %slice_multiply_fusion = f32[16,16,512]{2,1,0:T(8,128)} fusion(f32[16,16,512]{2,1,0:T(8,128)S(1)} %copy-done, f32[16,18,512]{2,1,0:T(8,128)S(1)} %convolution_add_fusion), kind=kLoop, calls=%fused_computation.40 | loop fusion | flops 131072 | bytes 1572864 | tf_op jit(solution)/shard_map/mul | solution.py:155
  70.6 0.6 fusion.1
  71.2 0.9 %fusion.35 = f32[16,8,256]{2,1,0:T(8,128)} fusion(f32[16,18,256]{2,1,0:T(8,128)S(1)} %fusion.1, f32[8,18]{1,0:T(8,128)S(1)} %bitcast.47), kind=kOutput, calls=%fused_computation.72 | convolution fusion | flops 3538944 | bytes 426560 | tf_op jit(solution)/shard_map/dot_general | solution.py:94
  (31 shorter events, 0.3 us)
Async XLA Ops:
  0.6 1.5 %copy-start = (f32[16,16,512]{2,1,0:T(8,128)S(1)}, f32[16,16,512]{2,1,0:T(8,128)}, u32[]{:S(2)}) copy-start(f32[16,16,512]{2,1,0:T(8,128)} %param.5) | copy-start | bytes 1572868
  2.8 11.2 %copy-start.2 = (f32[31]{0:T(128)S(1)}, f32[31]{0:T(128)}, u32[]{:S(2)}) copy-start(f32[31]{0:T(128)} %param.7) | copy-start | bytes 376
  2.8 11.2 %copy-start.3 = (f32[31]{0:T(128)S(1)}, f32[31]{0:T(128)}, u32[]{:S(2)}) copy-start(f32[31]{0:T(128)} %param.9) | copy-start | bytes 376
  2.9 11.5 %collective-permute-start.8 = (f32[15,16,256]{2,1,0:T(8,128)S(1)}, f32[15,16,256]{2,1,0:T(8,128)S(1)}, u32[]{:S(2)}, u32[]{:S(2)}) collective-permute-start(f32[15,16,256]{2,1,0:T(8,128)S(1)} %get-tuple-element.10), channel_id=1, source_target_pairs={{0,1},{1,2},{2,3},{4,5},{5,6},{6,7},{8,9},{9,10},{10,11},{12,13},{... | collective-permute-start | bytes 737288 | tf_op jit(solution)/shard_map/ppermute | solution.py:25
  6.2 8.4 %collective-permute-start.9 = (f32[15,16,256]{2,1,0:T(8,128)S(1)}, f32[15,16,256]{2,1,0:T(8,128)S(1)}, u32[]{:S(2)}, u32[]{:S(2)}) collective-permute-start(f32[15,16,256]{2,1,0:T(8,128)S(1)} %get-tuple-element.11), channel_id=1, source_target_pairs={{1,0},{2,1},{3,2},{5,4},{6,5},{7,6},{9,8},{10,9},{11,10},{13,12},{... | collective-permute-start | bytes 737288 | tf_op jit(solution)/shard_map/ppermute | solution.py:26
  8.3 13.9 %collective-permute-start = (f32[15,16,256]{2,1,0:T(8,128)S(1)}, f32[15,16,256]{2,1,0:T(8,128)S(1)}, u32[]{:S(2)}, u32[]{:S(2)}) collective-permute-start(f32[15,16,256]{2,1,0:T(8,128)S(1)} %get-tuple-element.13), channel_id=1, source_target_pairs={{0,1},{1,2},{2,3},{4,5},{5,6},{6,7},{8,9},{9,10},{10,11},{12,13},{... | collective-permute-start | bytes 737288 | tf_op jit(solution)/shard_map/ppermute | solution.py:25
  11.5 10.7 %collective-permute-start.1 = (f32[15,16,256]{2,1,0:T(8,128)S(1)}, f32[15,16,256]{2,1,0:T(8,128)S(1)}, u32[]{:S(2)}, u32[]{:S(2)}) collective-permute-start(f32[15,16,256]{2,1,0:T(8,128)S(1)} %get-tuple-element.12), channel_id=1, source_target_pairs={{1,0},{2,1},{3,2},{5,4},{6,5},{7,6},{9,8},{10,9},{11,10},{13,12},{... | collective-permute-start | bytes 737288 | tf_op jit(solution)/shard_map/ppermute | solution.py:26
  15.4 14.3 %collective-permute-start.10 = (f32[16,15,256]{2,0,1:T(8,128)S(1)}, f32[16,15,256]{2,0,1:T(8,128)S(1)}, u32[]{:S(2)}, u32[]{:S(2)}) collective-permute-start(f32[16,15,256]{2,0,1:T(8,128)S(1)} %get-tuple-element.18), channel_id=1, source_target_pairs={{0,4},{4,8},{8,12},{12,16},{16,20},{20,24},{24,28},{1,5},{5,9},{9,... | collective-permute-start | bytes 737288 | tf_op jit(solution)/shard_map/ppermute | solution.py:25
  20.3 9.5 %collective-permute-start.11 = (f32[16,15,256]{2,0,1:T(8,128)S(1)}, f32[16,15,256]{2,0,1:T(8,128)S(1)}, u32[]{:S(2)}, u32[]{:S(2)}) collective-permute-start(f32[16,15,256]{2,0,1:T(8,128)S(1)} %get-tuple-element.19), channel_id=1, source_target_pairs={{4,0},{8,4},{12,8},{16,12},{20,16},{24,20},{28,24},{5,1},{9,5},{13... | collective-permute-start | bytes 737288 | tf_op jit(solution)/shard_map/ppermute | solution.py:26
  23.1 6.7 %copy-start.1 = (f32[16,16,512]{2,1,0:T(8,128)S(1)}, f32[16,16,512]{2,1,0:T(8,128)}, u32[]{:S(2)}) copy-start(f32[16,16,512]{2,1,0:T(8,128)} %param.6) | copy-start | bytes 1572868
  23.1 13.6 %collective-permute-start.2 = (f32[16,17,256]{2,0,1:T(8,128)S(1)}, f32[16,17,256]{2,0,1:T(8,128)S(1)}, u32[]{:S(2)}, u32[]{:S(2)}) collective-permute-start(f32[16,17,256]{2,0,1:T(8,128)S(1)} %pad_maximum_fusion.8), channel_id=1, source_target_pairs={{0,4},{4,8},{8,12},{12,16},{16,20},{20,24},{24,28},{1,5},{5,9},{9,... | collective-permute-start | bytes 835592 | tf_op jit(solution)/shard_map/ppermute | solution.py:25
  27.8 8.9 %collective-permute-start.3 = (f32[16,17,256]{2,0,1:T(8,128)S(1)}, f32[16,17,256]{2,0,1:T(8,128)S(1)}, u32[]{:S(2)}, u32[]{:S(2)}) collective-permute-start(f32[16,17,256]{2,0,1:T(8,128)S(1)} %pad_maximum_fusion.9), channel_id=1, source_target_pairs={{4,0},{8,4},{12,8},{16,12},{20,16},{24,20},{28,24},{5,1},{9,5},{13... | collective-permute-start | bytes 835592 | tf_op jit(solution)/shard_map/ppermute | solution.py:26
  31.4 13.1 %collective-permute-start.12 = (f32[15,16,256]{2,1,0:T(8,128)}, f32[15,16,256]{2,1,0:T(8,128)S(1)}, u32[]{:S(2)}, u32[]{:S(2)}) collective-permute-start(f32[15,16,256]{2,1,0:T(8,128)} %get-tuple-element.16), channel_id=1, source_target_pairs={{0,1},{1,2},{2,3},{4,5},{5,6},{6,7},{8,9},{9,10},{10,11},{12,13},{... | collective-permute-start | bytes 737288 | tf_op jit(solution)/shard_map/ppermute | solution.py:25
  34.6 10.0 %collective-permute-start.13 = (f32[15,16,256]{2,1,0:T(8,128)}, f32[15,16,256]{2,1,0:T(8,128)S(1)}, u32[]{:S(2)}, u32[]{:S(2)}) collective-permute-start(f32[15,16,256]{2,1,0:T(8,128)} %get-tuple-element.17), channel_id=1, source_target_pairs={{1,0},{2,1},{3,2},{5,4},{6,5},{7,6},{9,8},{10,9},{11,10},{13,12},{... | collective-permute-start | bytes 737288 | tf_op jit(solution)/shard_map/ppermute | solution.py:26
  38.3 14.6 %collective-permute-start.4 = (f32[15,16,256]{2,1,0:T(8,128)}, f32[15,16,256]{2,1,0:T(8,128)}, u32[]{:S(2)}, u32[]{:S(2)}) collective-permute-start(f32[15,16,256]{2,1,0:T(8,128)} %get-tuple-element.20), channel_id=1, source_target_pairs={{0,1},{1,2},{2,3},{4,5},{5,6},{6,7},{8,9},{9,10},{10,11},{12,13},{... | collective-permute-start | bytes 737288 | tf_op jit(solution)/shard_map/ppermute | solution.py:25
  41.5 11.4 %collective-permute-start.5 = (f32[15,16,256]{2,1,0:T(8,128)}, f32[15,16,256]{2,1,0:T(8,128)}, u32[]{:S(2)}, u32[]{:S(2)}) collective-permute-start(f32[15,16,256]{2,1,0:T(8,128)} %get-tuple-element.21), channel_id=1, source_target_pairs={{1,0},{2,1},{3,2},{5,4},{6,5},{7,6},{9,8},{10,9},{11,10},{13,12},{... | collective-permute-start | bytes 737288 | tf_op jit(solution)/shard_map/ppermute | solution.py:26
  45.3 16.1 %collective-permute-start.14 = (f32[16,16,256]{2,0,1:T(8,128)S(1)}, f32[16,16,256]{2,0,1:T(8,128)S(1)}, u32[]{:S(2)}, u32[]{:S(2)}) collective-permute-start(f32[16,16,256]{2,0,1:T(8,128)S(1)} %fusion.8), channel_id=1, source_target_pairs={{0,4},{4,8},{8,12},{12,16},{16,20},{20,24},{24,28},{1,5},{5,9},{9,... | collective-permute-start | bytes 786440 | tf_op jit(solution)/shard_map/ppermute | solution.py:25
  51.0 10.4 %collective-permute-start.15 = (f32[16,16,256]{2,0,1:T(8,128)S(1)}, f32[16,16,256]{2,0,1:T(8,128)S(1)}, u32[]{:S(2)}, u32[]{:S(2)}) collective-permute-start(f32[16,16,256]{2,0,1:T(8,128)S(1)} %fusion.8), channel_id=1, source_target_pairs={{4,0},{8,4},{12,8},{16,12},{20,16},{24,20},{28,24},{5,1},{9,5},{13... | collective-permute-start | bytes 786440 | tf_op jit(solution)/shard_map/ppermute | solution.py:26
  54.7 10.3 %collective-permute-start.6 = (f32[16,16,256]{2,0,1:T(8,128)S(1)}, f32[16,16,256]{2,0,1:T(8,128)S(1)}, u32[]{:S(2)}, u32[]{:S(2)}) collective-permute-start(f32[16,16,256]{2,0,1:T(8,128)S(1)} %fusion.15), channel_id=1, source_target_pairs={{0,4},{4,8},{8,12},{12,16},{16,20},{20,24},{24,28},{1,5},{5,9},{9,... | collective-permute-start | bytes 786440 | tf_op jit(solution)/shard_map/ppermute | solution.py:25
  59.3 8.6 %collective-permute-start.7 = (f32[16,16,256]{2,0,1:T(8,128)S(1)}, f32[16,16,256]{2,0,1:T(8,128)S(1)}, u32[]{:S(2)}, u32[]{:S(2)}) collective-permute-start(f32[16,16,256]{2,0,1:T(8,128)S(1)} %fusion.15), channel_id=1, source_target_pairs={{4,0},{8,4},{12,8},{16,12},{20,16},{24,20},{28,24},{5,1},{9,5},{13... | collective-permute-start | bytes 786440 | tf_op jit(solution)/shard_map/ppermute | solution.py:26

commit v8 on v7

--- a/solution.py
+++ b/solution.py
@@ -132,15 +132,23 @@
     for index in range(CHUNKS):
         part = lax.slice_in_dim(filtered, index * chunk, (index + 1) * chunk, axis=2)
         seen = lax.slice_in_dim(observed, index * chunk, (index + 1) * chunk, axis=2)
-        blurred = along_planes(halo(part, "slab", 0, reach, reach), plane_fwd)
-        if index == 0:
-            blurred, carried = halo(blurred, "tile", 1, reach, reach, riders)
-        else:
-            blurred = halo(blurred, "tile", 1, reach, reach)
-        blurred = along_rows(blurred, row_fwd)
+        z_first = index % 2 == 0
+        blurred = part
+        for along_z in ((True, False) if z_first else (False, True)):
+            if along_z:
+                blurred = along_planes(halo(blurred, "slab", 0, reach, reach), plane_fwd)
+            elif index == 0:
+                blurred, carried = halo(blurred, "tile", 1, reach, reach, riders)
+                blurred = along_rows(blurred, row_fwd)
+            else:
+                blurred = along_rows(halo(blurred, "tile", 1, reach, reach), row_fwd)
         quotient = seen / blurred
-        spread = along_planes(halo(quotient, "slab", 0, reach, reach), plane_back)
-        spread = along_rows(halo(spread, "tile", 1, reach + 1, reach + 1), row_back)
+        spread = quotient
+        for along_z in ((True, False) if z_first else (False, True)):
+            if along_z:
+                spread = along_planes(halo(spread, "slab", 0, reach, reach), plane_back)
+            else:
+                spread = along_rows(halo(spread, "tile", 1, reach + 1, reach + 1), row_back)
         cols_of = lax.slice_in_dim(col_band, index * chunk, (index + 1) * chunk, axis=1)
         share = along_columns(spread, cols_of, transpose=True)
         spreads.append(share)

time: 72.6 us -> 71.6 us (0.986)
  waiting for transfers between devices: 5.82 us -> 7.04 us
  starting transfers between devices: 49.4 us -> 48.3 us
  local copies, waits for them, and re-layouts: 2.37 us -> 1.5 us
    ppermute x8, waiting for transfers between devices: 2.95 us -> 5.03 us  [halo(): got_down = lax.ppermute(send_down, axis, down)]
    ppermute x8, starting transfers between devices: 32.5 us -> 30.8 us  [halo(): got_up = lax.ppermute(send_up, axis, up)]
    ppermute x8, waiting for transfers between devices: 2.87 us -> 2.01 us  [halo(): got_up = lax.ppermute(send_up, axis, up)]
    slice x5 -> x6, local copies, waits for them, and re-layouts: 1.89 us -> 1.04 us  [halo(): send_up = lax.slice_in_dim(shard, start, length, axis=dim)]
    concatenate x8 -> x7, other arithmetic: 1.48 us -> 1.45 us  [halo(): joined = jnp.concatenate(pieces_before + [shard] + pieces_after, axis=dim)]
  transfers between devices with their start and end apart: 16 -> 16, of which waited for: 3 -> 6; matrix products, arithmetic and copies ran while one was open for 13% -> 11% of each run, Pallas kernels for 0% -> 0%
where the time goes in v8:
time: 71.6 us; the launch traced here: 71 us
  starting transfers between devices  48.3 us (67%)
  matrix products  8.41 us (12%)
  waiting for transfers between devices  7.04 us (10%)
  other arithmetic  4.44 us (6%)
  local copies, waits for them, and re-layouts  1.5 us (2%)
  between operations  1.27 us (2%)
    ppermute x8, starting transfers between devices, halo(): got_up = lax.ppermute(send_up, axis, up)  30.8 us
    ppermute x8, starting transfers between devices, halo(): got_down = lax.ppermute(send_down, axis, down)  17.6 us
    ppermute x8, waiting for transfers between devices, halo(): got_down = lax.ppermute(send_down, axis, down)  5.03 us
    dot_general x5, matrix products, along_rows(): lax.dot_general(left, volume, (((2,), (1,)), ((0,), (0,))), precision=PRE...  3.4 us
    dot_general x4, matrix products, along_planes(): lax.dot_general(matrix.T, volume, (((1,), (0,)), ((), ())), precision=PRE...  2.74 us
    dot_general x4, matrix products, along_columns(): lax.dot_general(volume, matrix, (((2,), (contract,)), ((), ())), precisio...  2.27 us
    ppermute x8, waiting for transfers between devices, halo(): got_up = lax.ppermute(send_up, axis, up)  2.01 us
    reduce_sum x3, other arithmetic, band(): return jnp.sum(picked, axis=2)  1.67 us
  transfers between devices with their start and end apart: 16, of which 6 were waited for; matrix products, arithmetic and copies ran while one was open for 11% of the time, Pallas kernels for 0%

profile of v8, /device:TPU:11, one launch (start us, length us, event | category | flops | bytes accessed | tf_op | source)
XLA Modules:
  0.0 71.0 jit_solution(4109143653363626237)
XLA Ops:
  0.7 1.4 %select_reduce_fusion.1 = (f32[128,128]{1,0:T(8,128)S(1)}, f32[128,128]{1,0:T(8,128)S(1)}, f32[128,128]{1,0:T(8,128)S(1)}) fusion(s32[128,128]{1,0:T(8,128)S(1)} %get-tuple-element.25, f32[31]{0:T(128)} %param.8, s32[128,128]{1,0:T(8,128)S(1)} %get-tuple-element.24, s32[128,128]{1,0:T(8,128)S(1)} %fusion.37), kind=kLoop, calls=%fused_computation.2 | loop fusion | flops 4521984 | bytes 393340 | tf_op jit(solution)/shard_map/reduce_sum | solution.py:51
  2.1 0.1 maximum_maximum_fusion
  2.2 0.6 convolution_bitcast_fusion
  2.8 0.0 copy-start.2
  2.8 0.0 copy-start.3
  2.9 3.7 %collective-permute-start.8 = (f32[16,15,256]{2,1,0:T(8,128)S(1)}, f32[16,15,256]{2,1,0:T(8,128)S(1)}, u32[]{:S(2)}, u32[]{:S(2)}) collective-permute-start(f32[16,15,256]{2,1,0:T(8,128)S(1)} %get-tuple-element.10), channel_id=1, source_target_pairs={{0,4},{4,8},{8,12},{12,16},{16,20},{20,24},{24,28},{1,5},{5,9},{9,... | collective-permute-start | bytes 737288 | tf_op jit(solution)/shard_map/ppermute | solution.py:25
  6.6 1.9 %collective-permute-start.9 = (f32[16,15,256]{2,1,0:T(8,128)S(1)}, f32[16,15,256]{2,1,0:T(8,128)S(1)}, u32[]{:S(2)}, u32[]{:S(2)}) collective-permute-start(f32[16,15,256]{2,1,0:T(8,128)S(1)} %get-tuple-element.11), channel_id=1, source_target_pairs={{4,0},{8,4},{12,8},{16,12},{20,16},{24,20},{28,24},{5,1},{9,5},{13... | collective-permute-start | bytes 737288 | tf_op jit(solution)/shard_map/ppermute | solution.py:26
  8.5 3.2 %collective-permute-start = (f32[15,16,256]{2,1,0:T(8,128)S(1)}, f32[15,16,256]{2,1,0:T(8,128)S(1)}, u32[]{:S(2)}, u32[]{:S(2)}) collective-permute-start(f32[15,16,256]{2,1,0:T(8,128)S(1)} %get-tuple-element.14), channel_id=1, source_target_pairs={{0,1},{1,2},{2,3},{4,5},{5,6},{6,7},{8,9},{9,10},{10,11},{12,13},{... | collective-permute-start | bytes 737288 | tf_op jit(solution)/shard_map/ppermute | solution.py:25
  11.7 2.1 %collective-permute-start.1 = (f32[15,16,256]{2,1,0:T(8,128)S(1)}, f32[15,16,256]{2,1,0:T(8,128)S(1)}, u32[]{:S(2)}, u32[]{:S(2)}) collective-permute-start(f32[15,16,256]{2,1,0:T(8,128)S(1)} %get-tuple-element.15), channel_id=1, source_target_pairs={{1,0},{2,1},{3,2},{5,4},{6,5},{7,6},{9,8},{10,9},{11,10},{13,12},{... | collective-permute-start | bytes 737288 | tf_op jit(solution)/shard_map/ppermute | solution.py:26
  13.9 0.2 slice_reduce_fusion.1
  14.1 0.2 select_select_fusion
  14.2 0.1 select_select_fusion.1
  14.3 0.2 select_reduce_fusion.5
  14.5 0.1 select_reduce_fusion.3
  14.7 0.0 collective-permute-done.8
  14.7 0.5 collective-permute-done.9
  15.2 0.4 fusion.3
  15.5 0.1 fusion.58
  15.6 3.2 %collective-permute-start.10 = (f32[15,16,256]{2,1,0:T(8,128)S(1)}, f32[15,16,256]{2,1,0:T(8,128)S(1)}, u32[]{:S(2)}, u32[]{:S(2)}) collective-permute-start(f32[15,16,256]{2,1,0:T(8,128)S(1)} %get-tuple-element.18), channel_id=1, source_target_pairs={{0,1},{1,2},{2,3},{4,5},{5,6},{6,7},{8,9},{9,10},{10,11},{12,13},{... | collective-permute-start | bytes 737288 | tf_op jit(solution)/shard_map/ppermute | solution.py:25
  18.8 2.1 %collective-permute-start.11 = (f32[15,16,256]{2,1,0:T(8,128)S(1)}, f32[15,16,256]{2,1,0:T(8,128)S(1)}, u32[]{:S(2)}, u32[]{:S(2)}) collective-permute-start(f32[15,16,256]{2,1,0:T(8,128)S(1)} %get-tuple-element.19), channel_id=1, source_target_pairs={{1,0},{2,1},{3,2},{5,4},{6,5},{7,6},{9,8},{10,9},{11,10},{13,12},{... | collective-permute-start | bytes 737288 | tf_op jit(solution)/shard_map/ppermute | solution.py:26
  20.9 0.0 collective-permute-done
  20.9 0.1 pad_maximum_fusion.3
  21.0 0.7 fusion.22
  21.7 0.0 slice-start
  21.8 5.3 %collective-permute-start.2 = (f32[16,17,256]{2,0,1:T(8,128)S(1)}, f32[16,17,256]{2,0,1:T(8,128)S(1)}, u32[]{:S(2)}, u32[]{:S(2)}) collective-permute-start(f32[16,17,256]{2,0,1:T(8,128)S(1)} %pad_maximum_fusion.7), channel_id=1, source_target_pairs={{0,4},{4,8},{8,12},{12,16},{16,20},{20,24},{24,28},{1,5},{5,9},{9,... | collective-permute-start | bytes 835592 | tf_op jit(solution)/shard_map/ppermute | solution.py:25
  27.1 1.9 %collective-permute-start.3 = (f32[16,17,256]{2,0,1:T(8,128)S(1)}, f32[16,17,256]{2,0,1:T(8,128)S(1)}, u32[]{:S(2)}, u32[]{:S(2)}) collective-permute-start(f32[16,17,256]{2,0,1:T(8,128)S(1)} %pad_maximum_fusion.8), channel_id=1, source_target_pairs={{4,0},{8,4},{12,8},{16,12},{20,16},{24,20},{28,24},{5,1},{9,5},{13... | collective-permute-start | bytes 835592 | tf_op jit(solution)/shard_map/ppermute | solution.py:26
  29.1 0.0 collective-permute-done.10
  29.1 0.0 collective-permute-done.11
  29.1 0.1 pad_maximum_fusion.6
  29.1 0.8 %convolution_divide_fusion = f32[16,16,256]{2,0,1:T(8,128)S(1)} fusion(f32[46,16,256]{2,1,0:T(8,128)S(1)} %pad_maximum_fusion.6, f32[16,16,256]{2,1,0:T(8,128)S(1)} %slice-done, f32[46,16]{0,1:T(8,128)S(1)} %get-tuple-element.5), kind=kOutput, calls=%fused_computation.8 | convolution fusion | flops 18153472 | bytes 1280896 | tf_op jit(solution)/shard_map/dot_general | solution.py:100
  29.9 0.0 copy-start.1
  29.9 4.7 %collective-permute-start.12 = (f32[16,16,256]{2,0,1:T(8,128)S(1)}, f32[16,16,256]{2,0,1:T(8,128)S(1)}, u32[]{:S(2)}, u32[]{:S(2)}) collective-permute-start(f32[16,16,256]{2,0,1:T(8,128)S(1)} %convolution_divide_fusion), channel_id=1, source_target_pairs={{0,4},{4,8},{8,12},{12,16},{16,20},{20,24},{24,28},{1,5},{5,9},{9,... | collective-permute-start | bytes 786440 | tf_op jit(solution)/shard_map/ppermute | solution.py:25
  34.6 1.9 %collective-permute-start.13 = (f32[16,16,256]{2,0,1:T(8,128)S(1)}, f32[16,16,256]{2,0,1:T(8,128)S(1)}, u32[]{:S(2)}, u32[]{:S(2)}) collective-permute-start(f32[16,16,256]{2,0,1:T(8,128)S(1)} %convolution_divide_fusion), channel_id=1, source_target_pairs={{4,0},{8,4},{12,8},{16,12},{20,16},{24,20},{28,24},{5,1},{9,5},{13... | collective-permute-start | bytes 786440 | tf_op jit(solution)/shard_map/ppermute | solution.py:26
  36.6 0.2 collective-permute-done.3
  36.8 0.1 pad_maximum_fusion.4
  36.8 0.7 convolution_divide_fusion.1
  37.6 0.8 %fusion.59 = (f32[15,16,256]{2,1,0:T(8,128)}, f32[15,16,256]{2,1,0:T(8,128)}) fusion(f32[16,16,256]{2,1,0:T(8,128)S(1)} %convolution_divide_fusion.1), kind=kLoop, calls=%fused_computation.104 | loop fusion | bytes 983040 | tf_op jit(solution)/shard_map/slice | solution.py:20
  38.4 3.2 %collective-permute-start.4 = (f32[15,16,256]{2,1,0:T(8,128)}, f32[15,16,256]{2,1,0:T(8,128)}, u32[]{:S(2)}, u32[]{:S(2)}) collective-permute-start(f32[15,16,256]{2,1,0:T(8,128)} %get-tuple-element.20), channel_id=1, source_target_pairs={{0,1},{1,2},{2,3},{4,5},{5,6},{6,7},{8,9},{9,10},{10,11},{12,13},{... | collective-permute-start | bytes 737288 | tf_op jit(solution)/shard_map/ppermute | solution.py:25
  41.6 2.8 %collective-permute-start.5 = (f32[15,16,256]{2,1,0:T(8,128)}, f32[15,16,256]{2,1,0:T(8,128)}, u32[]{:S(2)}, u32[]{:S(2)}) collective-permute-start(f32[15,16,256]{2,1,0:T(8,128)} %get-tuple-element.21), channel_id=1, source_target_pairs={{1,0},{2,1},{3,2},{5,4},{6,5},{7,6},{9,8},{10,9},{11,10},{13,12},{... | collective-permute-start | bytes 737288 | tf_op jit(solution)/shard_map/ppermute | solution.py:26
  44.4 0.1 reshape.72
  44.5 0.1 reshape.73
  44.6 0.0 collective-permute-done.13
  44.6 0.1 pad_maximum_fusion.2
  44.6 0.7 %fusion.14 = f32[16,18,256]{2,1,0:T(8,128)S(1)} fusion(f32[16,48,256]{2,0,1:T(8,128)S(1)} %pad_maximum_fusion.2, f32[18,48]{1,0:T(8,128)S(1)} %bitcast.42), kind=kOutput, calls=%fused_computation.29 | convolution fusion | flops 21233664 | bytes 1084800 | tf_op jit(solution)/shard_map/dot_general | solution.py:94
  45.4 0.1 fusion.57
  45.4 2.5 %collective-permute-start.14 = (f32[15,18,256]{2,1,0:T(8,128)S(1)}, f32[15,18,256]{2,1,0:T(8,128)S(1)}, u32[]{:S(2)}, u32[]{:S(2)}) collective-permute-start(f32[15,18,256]{2,1,0:T(8,128)S(1)} %get-tuple-element.16), channel_id=1, source_target_pairs={{0,1},{1,2},{2,3},{4,5},{5,6},{6,7},{8,9},{9,10},{10,11},{12,13},{... | collective-permute-start | bytes 829448 | tf_op jit(solution)/shard_map/ppermute | solution.py:25
  48.0 2.8 %collective-permute-start.15 = (f32[15,18,256]{2,1,0:T(8,128)S(1)}, f32[15,18,256]{2,1,0:T(8,128)S(1)}, u32[]{:S(2)}, u32[]{:S(2)}) collective-permute-start(f32[15,18,256]{2,1,0:T(8,128)S(1)} %get-tuple-element.17), channel_id=1, source_target_pairs={{1,0},{2,1},{3,2},{5,4},{6,5},{7,6},{9,8},{10,9},{11,10},{13,12},{... | collective-permute-start | bytes 829448 | tf_op jit(solution)/shard_map/ppermute | solution.py:26
  50.8 0.6 collective-permute-done.5
  51.3 1.1 %pad_maximum_fusion.5 = f32[46,16,256]{2,1,0:T(8,128)S(1)} fusion(f32[15,16,256]{2,1,0:T(8,128)} %collective-permute-done.5, f32[16,16,256]{2,1,0:T(8,128)S(1)} %convolution_divide_fusion.1, f32[15,16,256]{2,1,0:T(8,128)} %collective-permute-done.4), kind=kLoop, calls=%fused_computation.41 | loop fusion | flops 376832 | bytes 1507328 | tf_op jit(solution)/shard_map/concatenate | solution.py:40
  52.4 0.7 fusion.19
  53.2 5.0 %collective-permute-start.6 = (f32[16,16,256]{2,0,1:T(8,128)S(1)}, f32[16,16,256]{2,0,1:T(8,128)S(1)}, u32[]{:S(2)}, u32[]{:S(2)}) collective-permute-start(f32[16,16,256]{2,0,1:T(8,128)S(1)} %fusion.19), channel_id=1, source_target_pairs={{0,4},{4,8},{8,12},{12,16},{16,20},{20,24},{24,28},{1,5},{5,9},{9,... | collective-permute-start | bytes 786440 | tf_op jit(solution)/shard_map/ppermute | solution.py:25
  58.1 2.1 %collective-permute-start.7 = (f32[16,16,256]{2,0,1:T(8,128)S(1)}, f32[16,16,256]{2,0,1:T(8,128)S(1)}, u32[]{:S(2)}, u32[]{:S(2)}) collective-permute-start(f32[16,16,256]{2,0,1:T(8,128)S(1)} %fusion.19), channel_id=1, source_target_pairs={{4,0},{8,4},{12,8},{16,12},{20,16},{24,20},{28,24},{5,1},{9,5},{13... | collective-permute-start | bytes 786440 | tf_op jit(solution)/shard_map/ppermute | solution.py:26
  60.2 0.4 collective-permute-done.15
  60.6 0.1 pad_maximum_fusion
  60.7 0.6 fusion.1
  61.3 2.0 %collective-permute-done.6 = f32[16,16,256]{2,0,1:T(8,128)S(1)} collective-permute-done((f32[16,16,256]{2,0,1:T(8,128)S(1)}, f32[16,16,256]{2,0,1:T(8,128)S(1)}, u32[]{:S(2)}, u32[]{:S(2)}) %collective-permute-start.6) | collective-permute-done | bytes 262176 | tf_op jit(solution)/shard_map/ppermute | solution.py:25
  63.3 3.4 %collective-permute-done.7 = f32[16,16,256]{2,0,1:T(8,128)S(1)} collective-permute-done((f32[16,16,256]{2,0,1:T(8,128)S(1)}, f32[16,16,256]{2,0,1:T(8,128)S(1)}, u32[]{:S(2)}, u32[]{:S(2)}) %collective-permute-start.7) | collective-permute-done | bytes 262176 | tf_op jit(solution)/shard_map/ppermute | solution.py:26
  66.7 0.1 pad_maximum_fusion.1
  66.8 0.7 %fusion.17 = f32[16,18,256]{2,1,0:T(8,128)S(1)} fusion(f32[16,48,256]{2,0,1:T(8,128)S(1)} %pad_maximum_fusion.1, f32[18,48]{1,0:T(8,128)S(1)} %bitcast.43), kind=kOutput, calls=%fused_computation.32 | convolution fusion | flops 21233664 | bytes 1084800 | tf_op jit(solution)/shard_map/dot_general | solution.py:94
  67.5 0.5 fusion.24
  68.0 0.6 convolution_add_fusion
  68.6 0.9 %slice_multiply_fusion = f32[16,16,512]{2,1,0:T(8,128)} fusion(f32[16,16,512]{2,1,0:T(8,128)S(1)} %copy-done, f32[16,18,512]{2,1,0:T(8,128)S(1)} %convolution_add_fusion), kind=kLoop, calls=%fused_computation.43 | loop fusion | flops 131072 | bytes 1572864 | tf_op jit(solution)/shard_map/mul | solution.py:163
  69.6 0.6 fusion.9
  70.1 0.9 %fusion.40 = f32[16,8,256]{2,1,0:T(8,128)} fusion(f32[16,18,256]{2,1,0:T(8,128)S(1)} %fusion.9, f32[8,18]{1,0:T(8,128)S(1)} %bitcast.46), kind=kOutput, calls=%fused_computation.76 | convolution fusion | flops 3538944 | bytes 426560 | tf_op jit(solution)/shard_map/dot_general | solution.py:94
  (33 shorter events, 0.4 us)
Async XLA Ops:
  0.6 1.6 %copy-start = (f32[16,16,512]{2,1,0:T(8,128)S(1)}, f32[16,16,512]{2,1,0:T(8,128)}, u32[]{:S(2)}) copy-start(f32[16,16,512]{2,1,0:T(8,128)} %param.5) | copy-start | bytes 1572868
  2.8 11.5 %copy-start.2 = (f32[31]{0:T(128)S(1)}, f32[31]{0:T(128)}, u32[]{:S(2)}) copy-start(f32[31]{0:T(128)} %param.7) | copy-start | bytes 376
  2.8 11.5 %copy-start.3 = (f32[31]{0:T(128)S(1)}, f32[31]{0:T(128)}, u32[]{:S(2)}) copy-start(f32[31]{0:T(128)} %param.9) | copy-start | bytes 376
  2.9 11.8 %collective-permute-start.8 = (f32[16,15,256]{2,1,0:T(8,128)S(1)}, f32[16,15,256]{2,1,0:T(8,128)S(1)}, u32[]{:S(2)}, u32[]{:S(2)}) collective-permute-start(f32[16,15,256]{2,1,0:T(8,128)S(1)} %get-tuple-element.10), channel_id=1, source_target_pairs={{0,4},{4,8},{8,12},{12,16},{16,20},{20,24},{24,28},{1,5},{5,9},{9,... | collective-permute-start | bytes 737288 | tf_op jit(solution)/shard_map/ppermute | solution.py:25
  6.6 8.6 %collective-permute-start.9 = (f32[16,15,256]{2,1,0:T(8,128)S(1)}, f32[16,15,256]{2,1,0:T(8,128)S(1)}, u32[]{:S(2)}, u32[]{:S(2)}) collective-permute-start(f32[16,15,256]{2,1,0:T(8,128)S(1)} %get-tuple-element.11), channel_id=1, source_target_pairs={{4,0},{8,4},{12,8},{16,12},{20,16},{24,20},{28,24},{5,1},{9,5},{13... | collective-permute-start | bytes 737288 | tf_op jit(solution)/shard_map/ppermute | solution.py:26
  8.5 12.4 %collective-permute-start = (f32[15,16,256]{2,1,0:T(8,128)S(1)}, f32[15,16,256]{2,1,0:T(8,128)S(1)}, u32[]{:S(2)}, u32[]{:S(2)}) collective-permute-start(f32[15,16,256]{2,1,0:T(8,128)S(1)} %get-tuple-element.14), channel_id=1, source_target_pairs={{0,1},{1,2},{2,3},{4,5},{5,6},{6,7},{8,9},{9,10},{10,11},{12,13},{... | collective-permute-start | bytes 737288 | tf_op jit(solution)/shard_map/ppermute | solution.py:25
  11.7 9.2 %collective-permute-start.1 = (f32[15,16,256]{2,1,0:T(8,128)S(1)}, f32[15,16,256]{2,1,0:T(8,128)S(1)}, u32[]{:S(2)}, u32[]{:S(2)}) collective-permute-start(f32[15,16,256]{2,1,0:T(8,128)S(1)} %get-tuple-element.15), channel_id=1, source_target_pairs={{1,0},{2,1},{3,2},{5,4},{6,5},{7,6},{9,8},{10,9},{11,10},{13,12},{... | collective-permute-start | bytes 737288 | tf_op jit(solution)/shard_map/ppermute | solution.py:26
  15.6 13.5 %collective-permute-start.10 = (f32[15,16,256]{2,1,0:T(8,128)S(1)}, f32[15,16,256]{2,1,0:T(8,128)S(1)}, u32[]{:S(2)}, u32[]{:S(2)}) collective-permute-start(f32[15,16,256]{2,1,0:T(8,128)S(1)} %get-tuple-element.18), channel_id=1, source_target_pairs={{0,1},{1,2},{2,3},{4,5},{5,6},{6,7},{8,9},{9,10},{10,11},{12,13},{... | collective-permute-start | bytes 737288 | tf_op jit(solution)/shard_map/ppermute | solution.py:25
  18.8 10.3 %collective-permute-start.11 = (f32[15,16,256]{2,1,0:T(8,128)S(1)}, f32[15,16,256]{2,1,0:T(8,128)S(1)}, u32[]{:S(2)}, u32[]{:S(2)}) collective-permute-start(f32[15,16,256]{2,1,0:T(8,128)S(1)} %get-tuple-element.19), channel_id=1, source_target_pairs={{1,0},{2,1},{3,2},{5,4},{6,5},{7,6},{9,8},{10,9},{11,10},{13,12},{... | collective-permute-start | bytes 737288 | tf_op jit(solution)/shard_map/ppermute | solution.py:26
  21.7 7.4 %slice-start = ((f32[16,16,512]{2,1,0:T(8,128)}), f32[16,16,256]{2,1,0:T(8,128)S(1)}, s32[]{:S(2)}) async-start(f32[16,16,512]{2,1,0:T(8,128)} %param.6), calls=%async_computation | async-start | bytes 524288 | tf_op jit(solution)/shard_map/slice | solution.py:134
  21.8 14.8 %collective-permute-start.2 = (f32[16,17,256]{2,0,1:T(8,128)S(1)}, f32[16,17,256]{2,0,1:T(8,128)S(1)}, u32[]{:S(2)}, u32[]{:S(2)}) collective-permute-start(f32[16,17,256]{2,0,1:T(8,128)S(1)} %pad_maximum_fusion.7), channel_id=1, source_target_pairs={{0,4},{4,8},{8,12},{12,16},{16,20},{20,24},{24,28},{1,5},{5,9},{9,... | collective-permute-start | bytes 835592 | tf_op jit(solution)/shard_map/ppermute | solution.py:25
  27.1 9.6 %collective-permute-start.3 = (f32[16,17,256]{2,0,1:T(8,128)S(1)}, f32[16,17,256]{2,0,1:T(8,128)S(1)}, u32[]{:S(2)}, u32[]{:S(2)}) collective-permute-start(f32[16,17,256]{2,0,1:T(8,128)S(1)} %pad_maximum_fusion.8), channel_id=1, source_target_pairs={{4,0},{8,4},{12,8},{16,12},{20,16},{24,20},{28,24},{5,1},{9,5},{13... | collective-permute-start | bytes 835592 | tf_op jit(solution)/shard_map/ppermute | solution.py:26
  29.9 6.9 %copy-start.1 = (f32[16,16,512]{2,1,0:T(8,128)S(1)}, f32[16,16,512]{2,1,0:T(8,128)}, u32[]{:S(2)}) copy-start(f32[16,16,512]{2,1,0:T(8,128)} %param.6) | copy-start | bytes 1572868
  29.9 14.6 %collective-permute-start.12 = (f32[16,16,256]{2,0,1:T(8,128)S(1)}, f32[16,16,256]{2,0,1:T(8,128)S(1)}, u32[]{:S(2)}, u32[]{:S(2)}) collective-permute-start(f32[16,16,256]{2,0,1:T(8,128)S(1)} %convolution_divide_fusion), channel_id=1, source_target_pairs={{0,4},{4,8},{8,12},{12,16},{16,20},{20,24},{24,28},{1,5},{5,9},{9,... | collective-permute-start | bytes 786440 | tf_op jit(solution)/shard_map/ppermute | solution.py:25
  34.6 10.0 %collective-permute-start.13 = (f32[16,16,256]{2,0,1:T(8,128)S(1)}, f32[16,16,256]{2,0,1:T(8,128)S(1)}, u32[]{:S(2)}, u32[]{:S(2)}) collective-permute-start(f32[16,16,256]{2,0,1:T(8,128)S(1)} %convolution_divide_fusion), channel_id=1, source_target_pairs={{4,0},{8,4},{12,8},{16,12},{20,16},{24,20},{28,24},{5,1},{9,5},{13... | collective-permute-start | bytes 786440 | tf_op jit(solution)/shard_map/ppermute | solution.py:26
  38.4 12.4 %collective-permute-start.4 = (f32[15,16,256]{2,1,0:T(8,128)}, f32[15,16,256]{2,1,0:T(8,128)}, u32[]{:S(2)}, u32[]{:S(2)}) collective-permute-start(f32[15,16,256]{2,1,0:T(8,128)} %get-tuple-element.20), channel_id=1, source_target_pairs={{0,1},{1,2},{2,3},{4,5},{5,6},{6,7},{8,9},{9,10},{10,11},{12,13},{... | collective-permute-start | bytes 737288 | tf_op jit(solution)/shard_map/ppermute | solution.py:25
  41.6 9.8 %collective-permute-start.5 = (f32[15,16,256]{2,1,0:T(8,128)}, f32[15,16,256]{2,1,0:T(8,128)}, u32[]{:S(2)}, u32[]{:S(2)}) collective-permute-start(f32[15,16,256]{2,1,0:T(8,128)} %get-tuple-element.21), channel_id=1, source_target_pairs={{1,0},{2,1},{3,2},{5,4},{6,5},{7,6},{9,8},{10,9},{11,10},{13,12},{... | collective-permute-start | bytes 737288 | tf_op jit(solution)/shard_map/ppermute | solution.py:26
  45.4 14.8 %collective-permute-start.14 = (f32[15,18,256]{2,1,0:T(8,128)S(1)}, f32[15,18,256]{2,1,0:T(8,128)S(1)}, u32[]{:S(2)}, u32[]{:S(2)}) collective-permute-start(f32[15,18,256]{2,1,0:T(8,128)S(1)} %get-tuple-element.16), channel_id=1, source_target_pairs={{0,1},{1,2},{2,3},{4,5},{5,6},{6,7},{8,9},{9,10},{10,11},{12,13},{... | collective-permute-start | bytes 829448 | tf_op jit(solution)/shard_map/ppermute | solution.py:25
  48.0 12.6 %collective-permute-start.15 = (f32[15,18,256]{2,1,0:T(8,128)S(1)}, f32[15,18,256]{2,1,0:T(8,128)S(1)}, u32[]{:S(2)}, u32[]{:S(2)}) collective-permute-start(f32[15,18,256]{2,1,0:T(8,128)S(1)} %get-tuple-element.17), channel_id=1, source_target_pairs={{1,0},{2,1},{3,2},{5,4},{6,5},{7,6},{9,8},{10,9},{11,10},{13,12},{... | collective-permute-start | bytes 829448 | tf_op jit(solution)/shard_map/ppermute | solution.py:26
  53.2 10.1 %collective-permute-start.6 = (f32[16,16,256]{2,0,1:T(8,128)S(1)}, f32[16,16,256]{2,0,1:T(8,128)S(1)}, u32[]{:S(2)}, u32[]{:S(2)}) collective-permute-start(f32[16,16,256]{2,0,1:T(8,128)S(1)} %fusion.19), channel_id=1, source_target_pairs={{0,4},{4,8},{8,12},{12,16},{16,20},{20,24},{24,28},{1,5},{5,9},{9,... | collective-permute-start | bytes 786440 | tf_op jit(solution)/shard_map/ppermute | solution.py:25
  58.1 8.6 %collective-permute-start.7 = (f32[16,16,256]{2,0,1:T(8,128)S(1)}, f32[16,16,256]{2,0,1:T(8,128)S(1)}, u32[]{:S(2)}, u32[]{:S(2)}) collective-permute-start(f32[16,16,256]{2,0,1:T(8,128)S(1)} %fusion.19), channel_id=1, source_target_pairs={{4,0},{8,4},{12,8},{16,12},{20,16},{24,20},{28,24},{5,1},{9,5},{13... | collective-permute-start | bytes 786440 | tf_op jit(solution)/shard_map/ppermute | solution.py:26

commit v9 on v8

--- a/solution.py
+++ b/solution.py
@@ -132,12 +132,12 @@
     for index in range(CHUNKS):
         part = lax.slice_in_dim(filtered, index * chunk, (index + 1) * chunk, axis=2)
         seen = lax.slice_in_dim(observed, index * chunk, (index + 1) * chunk, axis=2)
-        z_first = index % 2 == 0
+        z_first = index % 2 == 1
         blurred = part
         for along_z in ((True, False) if z_first else (False, True)):
             if along_z:
                 blurred = along_planes(halo(blurred, "slab", 0, reach, reach), plane_fwd)
-            elif index == 0:
+            elif index == 1:
                 blurred, carried = halo(blurred, "tile", 1, reach, reach, riders)
                 blurred = along_rows(blurred, row_fwd)
             else:

time: 71.6 us -> 67.8 us (0.947)
  waiting for transfers between devices: 7.04 us -> 3.47 us
    ppermute x8, waiting for transfers between devices: 2.01 us -> 0.12 us  [halo(): got_up = lax.ppermute(send_up, axis, up)]
    ppermute x8, waiting for transfers between devices: 5.03 us -> 3.34 us  [halo(): got_down = lax.ppermute(send_down, axis, down)]
  transfers between devices with their start and end apart: 16 -> 16, of which waited for: 6 -> 2; matrix products, arithmetic and copies ran while one was open for 11% -> 13% of each run, Pallas kernels for 0% -> 0%
where the time goes in v9:
time: 67.8 us; the launch traced here: 67.1 us
  starting transfers between devices  47.9 us (71%)
  matrix products  8.41 us (12%)
  other arithmetic  4.44 us (7%)
  waiting for transfers between devices  3.47 us (5%)
  local copies, waits for them, and re-layouts  1.5 us (2%)
  between operations  1.29 us (2%)
    ppermute x8, starting transfers between devices, halo(): got_up = lax.ppermute(send_up, axis, up)  30.3 us
    ppermute x8, starting transfers between devices, halo(): got_down = lax.ppermute(send_down, axis, down)  17.6 us
    dot_general x5, matrix products, along_rows(): lax.dot_general(left, volume, (((2,), (1,)), ((0,), (0,))), precision=PRE...  3.4 us
    ppermute x8, waiting for transfers between devices, halo(): got_down = lax.ppermute(send_down, axis, down)  3.34 us
    dot_general x4, matrix products, along_planes(): lax.dot_general(matrix.T, volume, (((1,), (0,)), ((), ())), precision=PRE...  2.74 us
    dot_general x4, matrix products, along_columns(): lax.dot_general(volume, matrix, (((2,), (contract,)), ((), ())), precisio...  2.28 us
    reduce_sum x3, other arithmetic, band(): return jnp.sum(picked, axis=2)  1.67 us
    concatenate x7, other arithmetic, halo(): joined = jnp.concatenate(pieces_before + [shard] + pieces_after, axis=dim)  1.45 us
  transfers between devices with their start and end apart: 16, of which 2 were waited for; matrix products, arithmetic and copies ran while one was open for 13% of the time, Pallas kernels for 0%

profile of v9, /device:TPU:11, one launch (start us, length us, event | category | flops | bytes accessed | tf_op | source)
XLA Modules:
  0.0 67.1 jit_solution(11540196940370965427)
XLA Ops:
  0.7 1.4 %select_reduce_fusion.1 = (f32[128,128]{1,0:T(8,128)S(1)}, f32[128,128]{1,0:T(8,128)S(1)}, f32[128,128]{1,0:T(8,128)S(1)}) fusion(s32[128,128]{1,0:T(8,128)S(1)} %get-tuple-element.25, f32[31]{0:T(128)} %param.8, s32[128,128]{1,0:T(8,128)S(1)} %get-tuple-element.24, s32[128,128]{1,0:T(8,128)S(1)} %fusion.37), kind=kLoop, calls=%fused_computation.2 | loop fusion | flops 4521984 | bytes 393340 | tf_op jit(solution)/shard_map/reduce_sum | solution.py:51
  2.1 0.1 maximum_maximum_fusion
  2.2 0.6 convolution_bitcast_fusion
  2.8 0.0 copy-start.2
  2.8 0.0 copy-start.3
  2.9 2.6 %collective-permute-start.1 = (f32[16,15,256]{2,1,0:T(8,128)S(1)}, f32[16,15,256]{2,1,0:T(8,128)S(1)}, u32[]{:S(2)}, u32[]{:S(2)}) collective-permute-start(f32[16,15,256]{2,1,0:T(8,128)S(1)} %get-tuple-element.15), channel_id=1, source_target_pairs={{4,0},{8,4},{12,8},{16,12},{20,16},{24,20},{28,24},{5,1},{9,5},{13... | collective-permute-start | bytes 737288 | tf_op jit(solution)/shard_map/ppermute | solution.py:26
  5.5 3.9 %collective-permute-start = (f32[16,15,256]{2,1,0:T(8,128)S(1)}, f32[16,15,256]{2,1,0:T(8,128)S(1)}, u32[]{:S(2)}, u32[]{:S(2)}) collective-permute-start(f32[16,15,256]{2,1,0:T(8,128)S(1)} %get-tuple-element.14), channel_id=1, source_target_pairs={{0,4},{4,8},{8,12},{12,16},{16,20},{20,24},{24,28},{1,5},{5,9},{9,... | collective-permute-start | bytes 737288 | tf_op jit(solution)/shard_map/ppermute | solution.py:25
  9.4 2.1 %collective-permute-start.9 = (f32[15,16,256]{2,1,0:T(8,128)S(1)}, f32[15,16,256]{2,1,0:T(8,128)S(1)}, u32[]{:S(2)}, u32[]{:S(2)}) collective-permute-start(f32[15,16,256]{2,1,0:T(8,128)S(1)} %get-tuple-element.11), channel_id=1, source_target_pairs={{1,0},{2,1},{3,2},{5,4},{6,5},{7,6},{9,8},{10,9},{11,10},{13,12},{... | collective-permute-start | bytes 737288 | tf_op jit(solution)/shard_map/ppermute | solution.py:26
  11.5 3.2 %collective-permute-start.8 = (f32[15,16,256]{2,1,0:T(8,128)S(1)}, f32[15,16,256]{2,1,0:T(8,128)S(1)}, u32[]{:S(2)}, u32[]{:S(2)}) collective-permute-start(f32[15,16,256]{2,1,0:T(8,128)S(1)} %get-tuple-element.10), channel_id=1, source_target_pairs={{0,1},{1,2},{2,3},{4,5},{5,6},{6,7},{8,9},{9,10},{10,11},{12,13},{... | collective-permute-start | bytes 737288 | tf_op jit(solution)/shard_map/ppermute | solution.py:25
  14.7 0.2 slice_reduce_fusion.1
  14.9 0.2 select_select_fusion
  15.1 0.1 select_select_fusion.1
  15.2 0.2 select_reduce_fusion.5
  15.3 0.1 select_reduce_fusion.3
  15.5 0.0 collective-permute-done.1
  15.5 0.0 collective-permute-done
  15.5 0.4 fusion.3
  16.0 2.1 %collective-permute-start.3 = (f32[15,16,256]{2,1,0:T(8,128)S(1)}, f32[15,16,256]{2,1,0:T(8,128)S(1)}, u32[]{:S(2)}, u32[]{:S(2)}) collective-permute-start(f32[15,16,256]{2,1,0:T(8,128)S(1)} %get-tuple-element.23), channel_id=1, source_target_pairs={{1,0},{2,1},{3,2},{5,4},{6,5},{7,6},{9,8},{10,9},{11,10},{13,12},{... | collective-permute-start | bytes 737288 | tf_op jit(solution)/shard_map/ppermute | solution.py:26
  18.1 3.2 %collective-permute-start.2 = (f32[15,16,256]{2,1,0:T(8,128)S(1)}, f32[15,16,256]{2,1,0:T(8,128)S(1)}, u32[]{:S(2)}, u32[]{:S(2)}) collective-permute-start(f32[15,16,256]{2,1,0:T(8,128)S(1)} %get-tuple-element.22), channel_id=1, source_target_pairs={{0,1},{1,2},{2,3},{4,5},{5,6},{6,7},{8,9},{9,10},{10,11},{12,13},{... | collective-permute-start | bytes 737288 | tf_op jit(solution)/shard_map/ppermute | solution.py:25
  21.3 0.0 collective-permute-done.9
  21.3 0.0 collective-permute-done.8
  21.3 0.1 pad_maximum_fusion.4
  21.3 0.7 %fusion.19 = f32[16,16,256]{2,0,1:T(8,128)S(1)} fusion(f32[46,16,256]{2,1,0:T(8,128)S(1)} %pad_maximum_fusion.4, f32[46,16]{0,1:T(8,128)S(1)} %get-tuple-element.4), kind=kOutput, calls=%fused_computation.34 | convolution fusion | flops 18087936 | bytes 1018752 | tf_op jit(solution)/shard_map/dot_general | solution.py:100
  22.1 0.0 slice-start
  22.1 2.1 %collective-permute-start.11 = (f32[16,17,256]{2,0,1:T(8,128)S(1)}, f32[16,17,256]{2,0,1:T(8,128)S(1)}, u32[]{:S(2)}, u32[]{:S(2)}) collective-permute-start(f32[16,17,256]{2,0,1:T(8,128)S(1)} %pad_maximum_fusion.8), channel_id=1, source_target_pairs={{4,0},{8,4},{12,8},{16,12},{20,16},{24,20},{28,24},{5,1},{9,5},{13... | collective-permute-start | bytes 835592 | tf_op jit(solution)/shard_map/ppermute | solution.py:26
  24.2 4.5 %collective-permute-start.10 = (f32[16,17,256]{2,0,1:T(8,128)S(1)}, f32[16,17,256]{2,0,1:T(8,128)S(1)}, u32[]{:S(2)}, u32[]{:S(2)}) collective-permute-start(f32[16,17,256]{2,0,1:T(8,128)S(1)} %pad_maximum_fusion.7), channel_id=1, source_target_pairs={{0,4},{4,8},{8,12},{12,16},{16,20},{20,24},{24,28},{1,5},{5,9},{9,... | collective-permute-start | bytes 835592 | tf_op jit(solution)/shard_map/ppermute | solution.py:25
  28.8 0.0 collective-permute-done.3
  28.8 0.0 collective-permute-done.2
  28.8 0.1 pad_maximum_fusion.3
  28.9 0.8 %convolution_divide_fusion = f32[16,16,256]{2,0,1:T(8,128)S(1)} fusion(f32[46,16,256]{2,1,0:T(8,128)S(1)} %pad_maximum_fusion.3, f32[16,16,256]{2,1,0:T(8,128)S(1)} %slice-done, f32[46,16]{0,1:T(8,128)S(1)} %get-tuple-element.4), kind=kOutput, calls=%fused_computation.8 | convolution fusion | flops 18153472 | bytes 1280896 | tf_op jit(solution)/shard_map/dot_general | solution.py:100
  29.6 0.0 copy-start.1
  29.7 2.1 %collective-permute-start.5 = (f32[16,16,256]{2,0,1:T(8,128)S(1)}, f32[16,16,256]{2,0,1:T(8,128)S(1)}, u32[]{:S(2)}, u32[]{:S(2)}) collective-permute-start(f32[16,16,256]{2,0,1:T(8,128)S(1)} %convolution_divide_fusion), channel_id=1, source_target_pairs={{4,0},{8,4},{12,8},{16,12},{20,16},{24,20},{28,24},{5,1},{9,5},{13... | collective-permute-start | bytes 786440 | tf_op jit(solution)/shard_map/ppermute | solution.py:26
  31.7 4.5 %collective-permute-start.4 = (f32[16,16,256]{2,0,1:T(8,128)S(1)}, f32[16,16,256]{2,0,1:T(8,128)S(1)}, u32[]{:S(2)}, u32[]{:S(2)}) collective-permute-start(f32[16,16,256]{2,0,1:T(8,128)S(1)} %convolution_divide_fusion), channel_id=1, source_target_pairs={{0,4},{4,8},{8,12},{12,16},{16,20},{20,24},{24,28},{1,5},{5,9},{9,... | collective-permute-start | bytes 786440 | tf_op jit(solution)/shard_map/ppermute | solution.py:25
  36.3 0.0 collective-permute-done.11
  36.3 0.0 collective-permute-done.10
  36.3 0.1 pad_maximum_fusion.5
  36.4 0.7 %convolution_divide_fusion.1 = f32[16,16,256]{2,1,0:T(8,128)S(1)} fusion(f32[16,46,256]{2,0,1:T(8,128)S(1)} %pad_maximum_fusion.5, f32[16,16,512]{2,1,0:T(8,128)S(1)} %copy-done.1, f32[16,46]{1,0:T(8,128)S(1)} %bitcast.45), kind=kOutput, calls=%fused_computation.9 | convolution fusion | flops 18153472 | bytes 1280896 | tf_op jit(solution)/shard_map/dot_general | solution.py:94
  37.1 0.8 %fusion.58 = (f32[15,16,256]{2,1,0:T(8,128)}, f32[15,16,256]{2,1,0:T(8,128)}) fusion(f32[16,16,256]{2,1,0:T(8,128)S(1)} %convolution_divide_fusion.1), kind=kLoop, calls=%fused_computation.103 | loop fusion | bytes 983040 | tf_op jit(solution)/shard_map/slice | solution.py:20
  38.0 2.1 %collective-permute-start.13 = (f32[15,16,256]{2,1,0:T(8,128)}, f32[15,16,256]{2,1,0:T(8,128)}, u32[]{:S(2)}, u32[]{:S(2)}) collective-permute-start(f32[15,16,256]{2,1,0:T(8,128)} %get-tuple-element.19), channel_id=1, source_target_pairs={{1,0},{2,1},{3,2},{5,4},{6,5},{7,6},{9,8},{10,9},{11,10},{13,12},{... | collective-permute-start | bytes 737288 | tf_op jit(solution)/shard_map/ppermute | solution.py:26
  40.0 3.2 %collective-permute-start.12 = (f32[15,16,256]{2,1,0:T(8,128)}, f32[15,16,256]{2,1,0:T(8,128)}, u32[]{:S(2)}, u32[]{:S(2)}) collective-permute-start(f32[15,16,256]{2,1,0:T(8,128)} %get-tuple-element.18), channel_id=1, source_target_pairs={{0,1},{1,2},{2,3},{4,5},{5,6},{6,7},{8,9},{9,10},{10,11},{12,13},{... | collective-permute-start | bytes 737288 | tf_op jit(solution)/shard_map/ppermute | solution.py:25
  43.3 0.1 reshape.65
  43.4 0.1 reshape.64
  43.5 0.0 collective-permute-done.5
  43.5 0.1 pad_maximum_fusion.1
  43.5 0.7 %fusion.21 = f32[16,18,256]{2,1,0:T(8,128)S(1)} fusion(f32[16,48,256]{2,0,1:T(8,128)S(1)} %pad_maximum_fusion.1, f32[18,48]{1,0:T(8,128)S(1)} %bitcast.42), kind=kOutput, calls=%fused_computation.36 | convolution fusion | flops 21233664 | bytes 1084800 | tf_op jit(solution)/shard_map/dot_general | solution.py:94
  44.3 0.1 fusion.57
  44.3 2.8 %collective-permute-start.7 = (f32[15,18,256]{2,1,0:T(8,128)S(1)}, f32[15,18,256]{2,1,0:T(8,128)S(1)}, u32[]{:S(2)}, u32[]{:S(2)}) collective-permute-start(f32[15,18,256]{2,1,0:T(8,128)S(1)} %get-tuple-element.17), channel_id=1, source_target_pairs={{1,0},{2,1},{3,2},{5,4},{6,5},{7,6},{9,8},{10,9},{11,10},{13,12},{... | collective-permute-start | bytes 829448 | tf_op jit(solution)/shard_map/ppermute | solution.py:26
  47.1 3.0 %collective-permute-start.6 = (f32[15,18,256]{2,1,0:T(8,128)S(1)}, f32[15,18,256]{2,1,0:T(8,128)S(1)}, u32[]{:S(2)}, u32[]{:S(2)}) collective-permute-start(f32[15,18,256]{2,1,0:T(8,128)S(1)} %get-tuple-element.16), channel_id=1, source_target_pairs={{0,1},{1,2},{2,3},{4,5},{5,6},{6,7},{8,9},{9,10},{10,11},{12,13},{... | collective-permute-start | bytes 829448 | tf_op jit(solution)/shard_map/ppermute | solution.py:25
  50.2 0.0 collective-permute-done.12
  50.2 1.1 %pad_maximum_fusion.6 = f32[46,16,256]{2,1,0:T(8,128)S(1)} fusion(f32[15,16,256]{2,1,0:T(8,128)} %collective-permute-done.13, f32[16,16,256]{2,1,0:T(8,128)S(1)} %convolution_divide_fusion.1, f32[15,16,256]{2,1,0:T(8,128)} %collective-permute-done.12), kind=kLoop, calls=%fused_computation.42 | loop fusion | flops 376832 | bytes 1507328 | tf_op jit(solution)/shard_map/concatenate | solution.py:40
  51.3 0.7 %fusion.16 = f32[16,16,256]{2,0,1:T(8,128)S(1)} fusion(f32[46,16,256]{2,1,0:T(8,128)S(1)} %pad_maximum_fusion.6, f32[46,16]{0,1:T(8,128)S(1)} %get-tuple-element.6), kind=kOutput, calls=%fused_computation.31 | convolution fusion | flops 18087936 | bytes 1018752 | tf_op jit(solution)/shard_map/dot_general | solution.py:100
  52.0 1.9 %collective-permute-start.15 = (f32[16,16,256]{2,0,1:T(8,128)S(1)}, f32[16,16,256]{2,0,1:T(8,128)S(1)}, u32[]{:S(2)}, u32[]{:S(2)}) collective-permute-start(f32[16,16,256]{2,0,1:T(8,128)S(1)} %fusion.16), channel_id=1, source_target_pairs={{4,0},{8,4},{12,8},{16,12},{20,16},{24,20},{28,24},{5,1},{9,5},{13... | collective-permute-start | bytes 786440 | tf_op jit(solution)/shard_map/ppermute | solution.py:26
  53.9 4.7 %collective-permute-start.14 = (f32[16,16,256]{2,0,1:T(8,128)S(1)}, f32[16,16,256]{2,0,1:T(8,128)S(1)}, u32[]{:S(2)}, u32[]{:S(2)}) collective-permute-start(f32[16,16,256]{2,0,1:T(8,128)S(1)} %fusion.16), channel_id=1, source_target_pairs={{0,4},{4,8},{8,12},{12,16},{16,20},{20,24},{24,28},{1,5},{5,9},{9,... | collective-permute-start | bytes 786440 | tf_op jit(solution)/shard_map/ppermute | solution.py:25
  58.7 0.1 collective-permute-done.6
  58.8 0.1 pad_maximum_fusion
  58.9 0.6 fusion.1
  59.4 0.6 fusion.24
  60.0 3.3 %collective-permute-done.15 = f32[16,16,256]{2,0,1:T(8,128)S(1)} collective-permute-done((f32[16,16,256]{2,0,1:T(8,128)S(1)}, f32[16,16,256]{2,0,1:T(8,128)S(1)}, u32[]{:S(2)}, u32[]{:S(2)}) %collective-permute-start.15) | collective-permute-done | bytes 262176 | tf_op jit(solution)/shard_map/ppermute | solution.py:26
  63.4 0.1 pad_maximum_fusion.2
  63.4 0.7 %fusion.14 = f32[16,18,256]{2,1,0:T(8,128)S(1)} fusion(f32[16,48,256]{2,0,1:T(8,128)S(1)} %pad_maximum_fusion.2, f32[18,48]{1,0:T(8,128)S(1)} %bitcast.43), kind=kOutput, calls=%fused_computation.29 | convolution fusion | flops 21233664 | bytes 1084800 | tf_op jit(solution)/shard_map/dot_general | solution.py:94
  64.2 0.5 convolution_add_fusion
  64.7 0.9 %slice_multiply_fusion = f32[16,16,512]{2,1,0:T(8,128)} fusion(f32[16,16,512]{2,1,0:T(8,128)S(1)} %copy-done, f32[16,18,512]{2,1,0:T(8,128)S(1)} %convolution_add_fusion), kind=kLoop, calls=%fused_computation.43 | loop fusion | flops 131072 | bytes 1572864 | tf_op jit(solution)/shard_map/mul | solution.py:163
  65.6 0.6 fusion.9
  66.2 0.9 %fusion.40 = f32[16,8,256]{2,1,0:T(8,128)} fusion(f32[16,18,256]{2,1,0:T(8,128)S(1)} %fusion.9, f32[8,18]{1,0:T(8,128)S(1)} %bitcast.46), kind=kOutput, calls=%fused_computation.76 | convolution fusion | flops 3538944 | bytes 426560 | tf_op jit(solution)/shard_map/dot_general | solution.py:94
  (33 shorter events, 0.4 us)
Async XLA Ops:
  0.6 1.6 %copy-start = (f32[16,16,512]{2,1,0:T(8,128)S(1)}, f32[16,16,512]{2,1,0:T(8,128)}, u32[]{:S(2)}) copy-start(f32[16,16,512]{2,1,0:T(8,128)} %param.5) | copy-start | bytes 1572868
  2.8 12.3 %copy-start.2 = (f32[31]{0:T(128)S(1)}, f32[31]{0:T(128)}, u32[]{:S(2)}) copy-start(f32[31]{0:T(128)} %param.7) | copy-start | bytes 376
  2.8 12.3 %copy-start.3 = (f32[31]{0:T(128)S(1)}, f32[31]{0:T(128)}, u32[]{:S(2)}) copy-start(f32[31]{0:T(128)} %param.9) | copy-start | bytes 376
  2.9 12.6 %collective-permute-start.1 = (f32[16,15,256]{2,1,0:T(8,128)S(1)}, f32[16,15,256]{2,1,0:T(8,128)S(1)}, u32[]{:S(2)}, u32[]{:S(2)}) collective-permute-start(f32[16,15,256]{2,1,0:T(8,128)S(1)} %get-tuple-element.15), channel_id=1, source_target_pairs={{4,0},{8,4},{12,8},{16,12},{20,16},{24,20},{28,24},{5,1},{9,5},{13... | collective-permute-start | bytes 737288 | tf_op jit(solution)/shard_map/ppermute | solution.py:26
  5.5 10.1 %collective-permute-start = (f32[16,15,256]{2,1,0:T(8,128)S(1)}, f32[16,15,256]{2,1,0:T(8,128)S(1)}, u32[]{:S(2)}, u32[]{:S(2)}) collective-permute-start(f32[16,15,256]{2,1,0:T(8,128)S(1)} %get-tuple-element.14), channel_id=1, source_target_pairs={{0,4},{4,8},{8,12},{12,16},{16,20},{20,24},{24,28},{1,5},{5,9},{9,... | collective-permute-start | bytes 737288 | tf_op jit(solution)/shard_map/ppermute | solution.py:25
  9.4 11.9 %collective-permute-start.9 = (f32[15,16,256]{2,1,0:T(8,128)S(1)}, f32[15,16,256]{2,1,0:T(8,128)S(1)}, u32[]{:S(2)}, u32[]{:S(2)}) collective-permute-start(f32[15,16,256]{2,1,0:T(8,128)S(1)} %get-tuple-element.11), channel_id=1, source_target_pairs={{1,0},{2,1},{3,2},{5,4},{6,5},{7,6},{9,8},{10,9},{11,10},{13,12},{... | collective-permute-start | bytes 737288 | tf_op jit(solution)/shard_map/ppermute | solution.py:26
  11.5 9.8 %collective-permute-start.8 = (f32[15,16,256]{2,1,0:T(8,128)S(1)}, f32[15,16,256]{2,1,0:T(8,128)S(1)}, u32[]{:S(2)}, u32[]{:S(2)}) collective-permute-start(f32[15,16,256]{2,1,0:T(8,128)S(1)} %get-tuple-element.10), channel_id=1, source_target_pairs={{0,1},{1,2},{2,3},{4,5},{5,6},{6,7},{8,9},{9,10},{10,11},{12,13},{... | collective-permute-start | bytes 737288 | tf_op jit(solution)/shard_map/ppermute | solution.py:25
  16.0 12.8 %collective-permute-start.3 = (f32[15,16,256]{2,1,0:T(8,128)S(1)}, f32[15,16,256]{2,1,0:T(8,128)S(1)}, u32[]{:S(2)}, u32[]{:S(2)}) collective-permute-start(f32[15,16,256]{2,1,0:T(8,128)S(1)} %get-tuple-element.23), channel_id=1, source_target_pairs={{1,0},{2,1},{3,2},{5,4},{6,5},{7,6},{9,8},{10,9},{11,10},{13,12},{... | collective-permute-start | bytes 737288 | tf_op jit(solution)/shard_map/ppermute | solution.py:26
  18.1 10.7 %collective-permute-start.2 = (f32[15,16,256]{2,1,0:T(8,128)S(1)}, f32[15,16,256]{2,1,0:T(8,128)S(1)}, u32[]{:S(2)}, u32[]{:S(2)}) collective-permute-start(f32[15,16,256]{2,1,0:T(8,128)S(1)} %get-tuple-element.22), channel_id=1, source_target_pairs={{0,1},{1,2},{2,3},{4,5},{5,6},{6,7},{8,9},{9,10},{10,11},{12,13},{... | collective-permute-start | bytes 737288 | tf_op jit(solution)/shard_map/ppermute | solution.py:25
  22.1 6.7 %slice-start = ((f32[16,16,512]{2,1,0:T(8,128)}), f32[16,16,256]{2,1,0:T(8,128)S(1)}, s32[]{:S(2)}) async-start(f32[16,16,512]{2,1,0:T(8,128)} %param.6), calls=%async_computation | async-start | bytes 524288 | tf_op jit(solution)/shard_map/slice | solution.py:134
  22.1 14.1 %collective-permute-start.11 = (f32[16,17,256]{2,0,1:T(8,128)S(1)}, f32[16,17,256]{2,0,1:T(8,128)S(1)}, u32[]{:S(2)}, u32[]{:S(2)}) collective-permute-start(f32[16,17,256]{2,0,1:T(8,128)S(1)} %pad_maximum_fusion.8), channel_id=1, source_target_pairs={{4,0},{8,4},{12,8},{16,12},{20,16},{24,20},{28,24},{5,1},{9,5},{13... | collective-permute-start | bytes 835592 | tf_op jit(solution)/shard_map/ppermute | solution.py:26
  24.2 12.1 %collective-permute-start.10 = (f32[16,17,256]{2,0,1:T(8,128)S(1)}, f32[16,17,256]{2,0,1:T(8,128)S(1)}, u32[]{:S(2)}, u32[]{:S(2)}) collective-permute-start(f32[16,17,256]{2,0,1:T(8,128)S(1)} %pad_maximum_fusion.7), channel_id=1, source_target_pairs={{0,4},{4,8},{8,12},{12,16},{16,20},{20,24},{24,28},{1,5},{5,9},{9,... | collective-permute-start | bytes 835592 | tf_op jit(solution)/shard_map/ppermute | solution.py:25
  29.6 6.8 %copy-start.1 = (f32[16,16,512]{2,1,0:T(8,128)S(1)}, f32[16,16,512]{2,1,0:T(8,128)}, u32[]{:S(2)}) copy-start(f32[16,16,512]{2,1,0:T(8,128)} %param.6) | copy-start | bytes 1572868
  29.7 13.8 %collective-permute-start.5 = (f32[16,16,256]{2,0,1:T(8,128)S(1)}, f32[16,16,256]{2,0,1:T(8,128)S(1)}, u32[]{:S(2)}, u32[]{:S(2)}) collective-permute-start(f32[16,16,256]{2,0,1:T(8,128)S(1)} %convolution_divide_fusion), channel_id=1, source_target_pairs={{4,0},{8,4},{12,8},{16,12},{20,16},{24,20},{28,24},{5,1},{9,5},{13... | collective-permute-start | bytes 786440 | tf_op jit(solution)/shard_map/ppermute | solution.py:26
  31.7 11.8 %collective-permute-start.4 = (f32[16,16,256]{2,0,1:T(8,128)S(1)}, f32[16,16,256]{2,0,1:T(8,128)S(1)}, u32[]{:S(2)}, u32[]{:S(2)}) collective-permute-start(f32[16,16,256]{2,0,1:T(8,128)S(1)} %convolution_divide_fusion), channel_id=1, source_target_pairs={{0,4},{4,8},{8,12},{12,16},{16,20},{20,24},{24,28},{1,5},{5,9},{9,... | collective-permute-start | bytes 786440 | tf_op jit(solution)/shard_map/ppermute | solution.py:25
  38.0 12.2 %collective-permute-start.13 = (f32[15,16,256]{2,1,0:T(8,128)}, f32[15,16,256]{2,1,0:T(8,128)}, u32[]{:S(2)}, u32[]{:S(2)}) collective-permute-start(f32[15,16,256]{2,1,0:T(8,128)} %get-tuple-element.19), channel_id=1, source_target_pairs={{1,0},{2,1},{3,2},{5,4},{6,5},{7,6},{9,8},{10,9},{11,10},{13,12},{... | collective-permute-start | bytes 737288 | tf_op jit(solution)/shard_map/ppermute | solution.py:26
  40.0 10.1 %collective-permute-start.12 = (f32[15,16,256]{2,1,0:T(8,128)}, f32[15,16,256]{2,1,0:T(8,128)}, u32[]{:S(2)}, u32[]{:S(2)}) collective-permute-start(f32[15,16,256]{2,1,0:T(8,128)} %get-tuple-element.18), channel_id=1, source_target_pairs={{0,1},{1,2},{2,3},{4,5},{5,6},{6,7},{8,9},{9,10},{10,11},{12,13},{... | collective-permute-start | bytes 737288 | tf_op jit(solution)/shard_map/ppermute | solution.py:25
  44.3 14.3 %collective-permute-start.7 = (f32[15,18,256]{2,1,0:T(8,128)S(1)}, f32[15,18,256]{2,1,0:T(8,128)S(1)}, u32[]{:S(2)}, u32[]{:S(2)}) collective-permute-start(f32[15,18,256]{2,1,0:T(8,128)S(1)} %get-tuple-element.17), channel_id=1, source_target_pairs={{1,0},{2,1},{3,2},{5,4},{6,5},{7,6},{9,8},{10,9},{11,10},{13,12},{... | collective-permute-start | bytes 829448 | tf_op jit(solution)/shard_map/ppermute | solution.py:26
  47.1 11.7 %collective-permute-start.6 = (f32[15,18,256]{2,1,0:T(8,128)S(1)}, f32[15,18,256]{2,1,0:T(8,128)S(1)}, u32[]{:S(2)}, u32[]{:S(2)}) collective-permute-start(f32[15,18,256]{2,1,0:T(8,128)S(1)} %get-tuple-element.16), channel_id=1, source_target_pairs={{0,1},{1,2},{2,3},{4,5},{5,6},{6,7},{8,9},{9,10},{10,11},{12,13},{... | collective-permute-start | bytes 829448 | tf_op jit(solution)/shard_map/ppermute | solution.py:25
  52.0 11.4 %collective-permute-start.15 = (f32[16,16,256]{2,0,1:T(8,128)S(1)}, f32[16,16,256]{2,0,1:T(8,128)S(1)}, u32[]{:S(2)}, u32[]{:S(2)}) collective-permute-start(f32[16,16,256]{2,0,1:T(8,128)S(1)} %fusion.16), channel_id=1, source_target_pairs={{4,0},{8,4},{12,8},{16,12},{20,16},{24,20},{28,24},{5,1},{9,5},{13... | collective-permute-start | bytes 786440 | tf_op jit(solution)/shard_map/ppermute | solution.py:26
  53.9 9.4 %collective-permute-start.14 = (f32[16,16,256]{2,0,1:T(8,128)S(1)}, f32[16,16,256]{2,0,1:T(8,128)S(1)}, u32[]{:S(2)}, u32[]{:S(2)}) collective-permute-start(f32[16,16,256]{2,0,1:T(8,128)S(1)} %fusion.16), channel_id=1, source_target_pairs={{0,4},{4,8},{8,12},{12,16},{16,20},{20,24},{24,28},{1,5},{5,9},{9,... | collective-permute-start | bytes 786440 | tf_op jit(solution)/shard_map/ppermute | solution.py:25
